TPU v7x, 128 devices: a whole 4x4x4 slice. The times are simulated.
128 devices in a mesh: seq: 16 (over z, y), chan: 8 (over x, core).
Axes of the slice: x: 4, y: 4, z: 4, core: 2. Of those that a mesh axis runs over, the one named last changes fastest.
Arguments:
- query_projected: bfloat16 [4096, 4096], P('seq', 'chan'), may hold values from -6 to 6
- key_stream: bfloat16 [4096, 4096], P('seq', 'chan'), may hold values from -6 to 6
- value_stream: bfloat16 [4096, 4096], P('seq', 'chan'), may hold values from -6 to 6
- short_taps: float32 [3, 3, 4096], P(None, None, 'chan'), may hold values from -3 to 3
- skip_gain: float32 [4096], P('chan'), may hold values from -4 to 4
- long_filter: float32 [4096, 4096], P('seq', 'chan'), may hold values from -4 to 4
- out_weight: bfloat16 [4096, 4096], P('chan'), may hold values from -0.09375 to 0.09375
Outputs:
- mixed: bfloat16 [4096, 4096], P('seq')
All inputs are finite; a program needn't handle non-finite values.
Results may differ from a plain program's by a relative error of at most 0.005.
Values may be sent and summed in bfloat16 or wider, within the bound.
No kernel may reach another device: no remote copies, remote signals or barrier semaphores. Data moves between devices by JAX's collectives and lax.ppermute only.
A program may use at most 128 MiB of HBM per device.

v0:
```python
import math

import jax
import jax.numpy as jnp
from jax import lax
from jax.sharding import PartitionSpec as P

HIGH = lax.Precision.HIGHEST


def from_behind(array, axis, by):
    peers = lax.axis_size(axis)
    pairs = [(i, i + by) for i in range(peers) if 0 <= i + by < peers]
    return lax.ppermute(array, axis, pairs)


def from_partner(value, axis, stride):
    mask = 2**stride
    pairs = [(source, source ^ mask) for source in range(lax.axis_size(axis))]
    return lax.ppermute(value, axis, pairs)


def bit_reverse(place, seq_bits):
    result = jnp.zeros_like(place)
    for digit_count in range(seq_bits):
        result = result + ((place >> digit_count & 1) << seq_bits - 1 - digit_count)
    return result


def middle(real_part, imag_part, freq_low, seq_count, shard_len):
    padded_len = 2 * seq_count * shard_len
    steps_idx = jnp.arange(shard_len, dtype=jnp.int32)
    twist_turns = freq_low[:, None] * steps_idx[None, :] % padded_len
    twist_angle = twist_turns.astype(jnp.float32) * (2.0 * math.pi / padded_len)
    twist_cos = jnp.cos(twist_angle)[None, :, :, None]
    twist_sin = jnp.sin(twist_angle)[None, :, :, None]
    turned_real = real_part * twist_cos + imag_part * twist_sin
    turned_imag = imag_part * twist_cos - real_part * twist_sin
    shared_turns = steps_idx[:, None] * steps_idx[None, :] % shard_len
    shared_angle = shared_turns.astype(jnp.float32) * (2.0 * math.pi / shard_len)
    cosine = jnp.cos(shared_angle)
    sine = jnp.sin(shared_angle)
    spec_real = jnp.einsum("mn,fknc->fkmc", cosine, turned_real, precision=HIGH) + jnp.einsum(
        "mn,fknc->fkmc", sine, turned_imag, precision=HIGH
    )
    spec_imag = jnp.einsum("mn,fknc->fkmc", cosine, turned_imag, precision=HIGH) - jnp.einsum(
        "mn,fknc->fkmc", sine, turned_real, precision=HIGH
    )
    prod_real = spec_real[0] * spec_real[1] - spec_imag[0] * spec_imag[1]
    prod_imag = spec_real[0] * spec_imag[1] + spec_imag[0] * spec_real[1]
    summed_real = jnp.einsum("mn,kmc->knc", cosine, prod_real, precision=HIGH) - jnp.einsum(
        "mn,kmc->knc", sine, prod_imag, precision=HIGH
    )
    imaginary_summed = jnp.einsum("mn,kmc->knc", cosine, prod_imag, precision=HIGH) + jnp.einsum(
        "mn,kmc->knc", sine, prod_real, precision=HIGH
    )
    back_real = summed_real * twist_cos[0] - imaginary_summed * twist_sin[0]
    back_imag = imaginary_summed * twist_cos[0] + summed_real * twist_sin[0]
    return (back_real, back_imag)


def on_device(
    query_projected, key_stream, value_stream, short_taps, skip_gain, long_filter, out_weight
):
    shard_len = query_projected.shape[0]
    seq_count = lax.axis_size("seq")
    seq_bits = seq_count.bit_length() - 1
    padded_len = 2 * seq_count * shard_len
    place = lax.axis_index("seq")
    pair_idx = jnp.arange(2, dtype=jnp.int32)
    streams = jnp.stack([query_projected, key_stream, value_stream])
    rim_rows = from_behind(streams[:, -2:, :], "seq", 1)
    extended = jnp.concatenate([rim_rows, streams], axis=1).astype(jnp.float32)
    shaped = (
        short_taps[0][:, None, :] * extended[:, 2:]
        + short_taps[1][:, None, :] * extended[:, 1:-1]
        + short_taps[2][:, None, :] * extended[:, :-2]
    )
    source = shaped[1] * shaped[2]
    fields = jnp.stack([source, long_filter])
    base_angle = place.astype(jnp.float32) * (math.pi / seq_count)
    base_cos = jnp.cos(base_angle)
    base_sin = jnp.sin(base_angle)
    real_part = jnp.stack([fields, fields * base_cos], axis=1)
    imag_part = jnp.stack([jnp.zeros_like(fields), -fields * base_sin], axis=1)
    values = jnp.stack([real_part, imag_part])
    for section_bit in reversed(range(seq_bits)):
        half_span = 1 << section_bit
        partner = from_partner(values, "seq", section_bit)
        upper_side = place >> section_bit & 1 == 1
        angle = (place % half_span).astype(jnp.float32) * (math.pi / half_span)
        cosine = jnp.cos(angle)
        sine = jnp.sin(angle)
        gap_value = partner - values
        upper = jnp.stack(
            [
                gap_value[0] * cosine + gap_value[1] * sine,
                gap_value[1] * cosine - gap_value[0] * sine,
            ]
        )
        values = jnp.where(upper_side, upper, values + partner)
    freq_low = 2 * bit_reverse(place, seq_bits) + pair_idx
    back_real, back_imag = middle(values[0], values[1], freq_low, seq_count, shard_len)
    values = jnp.stack([back_real, back_imag])
    for section_bit in range(seq_bits):
        half_span = 1 << section_bit
        partner = from_partner(values, "seq", section_bit)
        upper_side = place >> section_bit & 1 == 1
        angle = (place % half_span).astype(jnp.float32) * (math.pi / half_span)
        cosine = jnp.cos(angle)
        sine = jnp.sin(angle)

        def rotate(field):
            return jnp.stack(
                [cosine * field[0] - sine * field[1], cosine * field[1] + sine * field[0]]
            )

        values = jnp.where(upper_side, partner - rotate(values), values + rotate(partner))
    convolved = (values[0, 0] + base_cos * values[0, 1] - base_sin * values[1, 1]) / padded_len
    gated = (shaped[0] * (convolved + skip_gain[None, :] * source)).astype(jnp.bfloat16)
    terms = jnp.dot(gated, out_weight, preferred_element_type=jnp.float32)
    mixed = lax.psum(terms, "chan").astype(jnp.bfloat16)
    return mixed


def solution(mesh):
    return jax.shard_map(
        on_device,
        mesh=mesh,
        in_specs=(
            P("seq", "chan"),
            P("seq", "chan"),
            P("seq", "chan"),
            P(None, None, "chan"),
            P("chan"),
            P("seq", "chan"),
            P("chan", None),
        ),
        out_specs=P("seq", None),
        check_vma=False,
    )
```

profile of v0, /device:TPU:0, one launch (start us, length us, event | category | flops | bytes accessed | tf_op | source)
XLA Modules:
  0.0 697.9 jit_solution(11717577540401559437)
XLA Ops:
  3.5 3.6 collective-permute-start
  7.5 7.9 %collective-permute-done = bf16[3,2,512]{1,2,0:T(8,128)(2,1)S(1)} collective-permute-done((bf16[3,2,512]{1,2,0:T(8,128)(2,1)S(1)}, bf16[3,2,512]{1,2,0:T(8,128)(2,1)S(1)}, u32[]{:S(2)}, u32[]{:S(2)}) %collective-permute-start) | collective-permute-done | bytes 6176 | tf_op jit(solution)/shard_map/ppermute | solution.py:14
  16.0 1.6 fusion.4
  19.3 2.7 pad_maximum_fusion
  22.0 6.9 collective-permute-start.1
  29.0 89.9 %collective-permute-done.1 = f32[2,2,2,256,512]{3,4,2,1,0:T(8,128)} collective-permute-done((f32[2,2,2,256,512]{3,4,2,1,0:T(8,128)}, f32[2,2,2,256,512]{3,4,2,1,0:T(8,128)}, u32[]{:S(2)}, u32[]{:S(2)}) %collective-permute-start.1) | collective-permute-done | bytes 4194336 | tf_op jit(solution)/shard_map/ppermute | solution.py:20
  118.9 3.6 fusion.93
  124.5 5.1 maximum_select_fusion
  131.0 89.7 %collective-permute-done.2 = f32[2,2,2,256,512]{3,4,2,1,0:T(8,128)} collective-permute-done((f32[2,2,2,256,512]{3,4,2,1,0:T(8,128)}, f32[2,2,2,256,512]{3,4,2,1,0:T(8,128)}, u32[]{:S(2)}, u32[]{:S(2)}) %collective-permute-start.2) | collective-permute-done | bytes 4194336 | tf_op jit(solution)/shard_map/ppermute | solution.py:20
  220.8 5.8 fusion.99
  229.4 5.8 maximum_select_fusion.1
  236.5 90.6 %collective-permute-done.3 = f32[2,2,2,256,512]{3,4,2,1,0:T(8,128)} collective-permute-done((f32[2,2,2,256,512]{3,4,2,1,0:T(8,128)}, f32[2,2,2,256,512]{3,4,2,1,0:T(8,128)}, u32[]{:S(2)}, u32[]{:S(2)}) %collective-permute-start.3) | collective-permute-done | bytes 4194336 | tf_op jit(solution)/shard_map/ppermute | solution.py:20
  327.1 4.2 sub.104
  331.7 6.3 maximum_select_fusion.2
  338.6 89.3 %collective-permute-done.4 = f32[2,2,2,256,512]{3,4,2,1,0:T(8,128)} collective-permute-done((f32[2,2,2,256,512]{3,4,2,1,0:T(8,128)}, f32[2,2,2,256,512]{3,4,2,1,0:T(8,128)}, u32[]{:S(2)}, u32[]{:S(2)}) %collective-permute-start.4) | collective-permute-done | bytes 4194336 | tf_op jit(solution)/shard_map/ppermute | solution.py:20
  427.9 4.2 sub.106
  432.4 4.3 maximum_select_fusion.3
  436.7 2.9 fusion.24
  439.6 2.8 fusion.23
  442.4 2.9 add_bitcast_fusion
  445.4 3.1 subtract_bitcast_fusion
  448.8 2.0 fusion.9
  450.8 2.0 fusion.13
  452.7 2.0 convolution_add_fusion
  454.7 2.2 fusion.8
  457.6 44.6 %collective-permute-done.5 = f32[2,2,256,512]{2,3,1,0:T(8,128)S(1)} collective-permute-done((f32[2,2,256,512]{2,3,1,0:T(8,128)S(1)}, f32[2,2,256,512]{2,3,1,0:T(8,128)S(1)}, u32[]{:S(2)}, u32[]{:S(2)}) %collective-permute-start.5) | collective-permute-done | bytes 2097184 | tf_op jit(solution)/shard_map/ppermute | solution.py:20
  503.4 42.4 %collective-permute-done.6 = f32[2,2,256,512]{2,3,1,0:T(8,128)S(1)} collective-permute-done((f32[2,2,256,512]{2,3,1,0:T(8,128)S(1)}, f32[2,2,256,512]{2,3,1,0:T(8,128)S(1)}, u32[]{:S(2)}, u32[]{:S(2)}) %collective-permute-start.6) | collective-permute-done | bytes 2097184 | tf_op jit(solution)/shard_map/ppermute | solution.py:20
  547.5 44.0 %collective-permute-done.7 = f32[2,2,256,512]{2,3,1,0:T(8,128)S(1)} collective-permute-done((f32[2,2,256,512]{2,3,1,0:T(8,128)S(1)}, f32[2,2,256,512]{2,3,1,0:T(8,128)S(1)}, u32[]{:S(2)}, u32[]{:S(2)}) %collective-permute-start.7) | collective-permute-done | bytes 2097184 | tf_op jit(solution)/shard_map/ppermute | solution.py:20
  592.3 1.8 collective-permute-start.8
  594.3 39.4 %collective-permute-done.8 = f32[2,2,256,512]{2,3,1,0:T(8,128)S(1)} collective-permute-done((f32[2,2,256,512]{2,3,1,0:T(8,128)S(1)}, f32[2,2,256,512]{2,3,1,0:T(8,128)S(1)}, u32[]{:S(2)}, u32[]{:S(2)}) %collective-permute-start.8) | collective-permute-done | bytes 2097184 | tf_op jit(solution)/shard_map/ppermute | solution.py:20
  636.7 3.4 fusion.28
  640.1 57.5 %all-reduce.2 = bf16[256,4096]{1,0:T(8,128)(2,1)} all-reduce(f32[256,4096]{1,0:T(8,128)} %fusion.28), channel_id=1, replica_groups=mesh['seq'=16,'chan'=8] {'chan'}, use_global_device_ids=true, to_apply=%region_0.1 | all-reduce | flops 1048576 | bytes 6291456 | tf_op jit(solution)/shard_map/psum | solution.py:122
  (64 shorter events, 22.1 us)
Async XLA Ops:
  0.0 7.1 %copy-start.12 = (f32[3,3,512]{2,1,0:T(4,128)S(1)}, f32[3,3,512]{2,1,0:T(4,128)}, u32[]{:S(2)}) copy-start(f32[3,3,512]{2,1,0:T(4,128)} %param.10) | copy-start | bytes 55300
  0.0 7.3 %copy-start.10 = (f32[256,512]{1,0:T(8,128)S(1)}, f32[256,512]{1,0:T(8,128)}, u32[]{:S(2)}) copy-start(f32[256,512]{1,0:T(8,128)} %param.12) | copy-start | bytes 1572868
  3.5 12.0 %collective-permute-start = (bf16[3,2,512]{1,2,0:T(8,128)(2,1)S(1)}, bf16[3,2,512]{1,2,0:T(8,128)(2,1)S(1)}, u32[]{:S(2)}, u32[]{:S(2)}) collective-permute-start(bf16[3,2,512]{1,2,0:T(8,128)(2,1)S(1)} %pad_maximum_fusion.3), channel_id=1, source_target_pairs={{0,8},{8,16},{16,24},{24,32},{32,40},{40,48},{48,56},{56,64},{64,7... | collective-permute-start | bytes 18440 | tf_op jit(solution)/shard_map/ppermute | solution.py:14
  17.6 1.2 copy-start.7
  19.3 2.7 copy-start
  22.0 96.9 %collective-permute-start.1 = (f32[2,2,2,256,512]{3,4,2,1,0:T(8,128)}, f32[2,2,2,256,512]{3,4,2,1,0:T(8,128)}, u32[]{:S(2)}, u32[]{:S(2)}) collective-permute-start(f32[2,2,2,256,512]{3,4,2,1,0:T(8,128)} %pad_maximum_fusion), channel_id=1, source_target_pairs={{0,64},{8,72},{16,80},{24,88},{32,96},{40,104},{48,112},{56,120},{... | collective-permute-start | bytes 12582920 | tf_op jit(solution)/shard_map/ppermute | solution.py:20
  122.5 1.9 copy-start.1
  123.0 6.6 copy-start.3
  123.0 6.6 copy-start.5
  129.6 91.2 %collective-permute-start.2 = (f32[2,2,2,256,512]{3,4,2,1,0:T(8,128)}, f32[2,2,2,256,512]{3,4,2,1,0:T(8,128)}, u32[]{:S(2)}, u32[]{:S(2)}) collective-permute-start(f32[2,2,2,256,512]{3,4,2,1,0:T(8,128)} %maximum_select_fusion), channel_id=1, source_target_pairs={{0,32},{8,40},{16,48},{24,56},{32,0},{40,8},{48,16},{56,24},{64,96... | collective-permute-start | bytes 12582920 | tf_op jit(solution)/shard_map/ppermute | solution.py:20
  226.5 1.6 copy-start.2
  226.5 2.2 copy-start.4
  226.6 2.8 copy-start.6
  235.2 91.8 %collective-permute-start.3 = (f32[2,2,2,256,512]{3,4,2,1,0:T(8,128)}, f32[2,2,2,256,512]{3,4,2,1,0:T(8,128)}, u32[]{:S(2)}, u32[]{:S(2)}) collective-permute-start(f32[2,2,2,256,512]{3,4,2,1,0:T(8,128)} %maximum_select_fusion.1), channel_id=1, source_target_pairs={{0,16},{8,24},{16,0},{24,8},{32,48},{40,56},{48,32},{56,40},{64,80... | collective-permute-start | bytes 12582920 | tf_op jit(solution)/shard_map/ppermute | solution.py:20
  338.0 89.9 %collective-permute-start.4 = (f32[2,2,2,256,512]{3,4,2,1,0:T(8,128)}, f32[2,2,2,256,512]{3,4,2,1,0:T(8,128)}, u32[]{:S(2)}, u32[]{:S(2)}) collective-permute-start(f32[2,2,2,256,512]{3,4,2,1,0:T(8,128)} %maximum_select_fusion.2), channel_id=1, source_target_pairs={{0,8},{8,0},{16,24},{24,16},{32,40},{40,32},{48,56},{56,48},{64,72... | collective-permute-start | bytes 12582920 | tf_op jit(solution)/shard_map/ppermute | solution.py:20
  457.1 45.1 %collective-permute-start.5 = (f32[2,2,256,512]{2,3,1,0:T(8,128)S(1)}, f32[2,2,256,512]{2,3,1,0:T(8,128)S(1)}, u32[]{:S(2)}, u32[]{:S(2)}) collective-permute-start(f32[2,2,256,512]{2,3,1,0:T(8,128)S(1)} %pad_maximum_fusion.1), channel_id=1, source_target_pairs={{0,8},{8,0},{16,24},{24,16},{32,40},{40,32},{48,56},{56,48},{64,72... | collective-permute-start | bytes 6291464 | tf_op jit(solution)/shard_map/ppermute | solution.py:20
  502.9 42.9 %collective-permute-start.6 = (f32[2,2,256,512]{2,3,1,0:T(8,128)S(1)}, f32[2,2,256,512]{2,3,1,0:T(8,128)S(1)}, u32[]{:S(2)}, u32[]{:S(2)}) collective-permute-start(f32[2,2,256,512]{2,3,1,0:T(8,128)S(1)} %fusion), channel_id=1, source_target_pairs={{0,16},{8,24},{16,0},{24,8},{32,48},{40,56},{48,32},{56,40},{64,80... | collective-permute-start | bytes 6291464 | tf_op jit(solution)/shard_map/ppermute | solution.py:20
  547.0 44.5 %collective-permute-start.7 = (f32[2,2,256,512]{2,3,1,0:T(8,128)S(1)}, f32[2,2,256,512]{2,3,1,0:T(8,128)S(1)}, u32[]{:S(2)}, u32[]{:S(2)}) collective-permute-start(f32[2,2,256,512]{2,3,1,0:T(8,128)S(1)} %fusion.1), channel_id=1, source_target_pairs={{0,32},{8,40},{16,48},{24,56},{32,0},{40,8},{48,16},{56,24},{64,96... | collective-permute-start | bytes 6291464 | tf_op jit(solution)/shard_map/ppermute | solution.py:20
  592.3 41.4 %collective-permute-start.8 = (f32[2,2,256,512]{2,3,1,0:T(8,128)S(1)}, f32[2,2,256,512]{2,3,1,0:T(8,128)S(1)}, u32[]{:S(2)}, u32[]{:S(2)}) collective-permute-start(f32[2,2,256,512]{2,3,1,0:T(8,128)S(1)} %fusion.2), channel_id=1, source_target_pairs={{0,64},{8,72},{16,80},{24,88},{32,96},{40,104},{48,112},{56,120},{... | collective-permute-start | bytes 6291464 | tf_op jit(solution)/shard_map/ppermute | solution.py:20
  634.0 1.4 copy-start.8
  634.0 2.7 copy-start.9
  634.0 2.7 copy-start.11
where the time goes:
time: 707 us; the launch traced here: 698 us
  waiting for transfers between devices  538 us (76%)
  blocking collectives  57.5 us (8%)
  other arithmetic  51.6 us (7%)
  matrix products  23.3 us (3%)
  starting transfers between devices  16 us (2%)
  local copies, waits for them, and re-layouts  10.3 us (1%)
    ppermute x8, waiting for transfers between devices, from_partner(): return lax.ppermute(value, axis, pairs)  530 us
    psum x1, blocking collectives, on_device(): mixed = lax.psum(terms, 'chan').astype(jnp.bfloat16)  57.5 us
    select_n x4, other arithmetic, on_device(): values = jnp.where(upper_side, upper, values + partner)  21.5 us
    sub x4, other arithmetic, on_device(): gap_value = partner - values  17.7 us
  transfers between devices with their start and end apart: 9, of which 9 were waited for; matrix products, arithmetic and copies ran while one was open for 0% of the time, Pallas kernels for 0%

commit v1 on v0

v1 whole, which is shorter than its diff:
```python
import numpy as np

import jax
import jax.numpy as jnp
from jax import lax
from jax.sharding import PartitionSpec as P

HIGH = lax.Precision.HIGHEST


def dft_tables(seq_len):
    padded_len = 2 * seq_len
    rows = 64
    cols = padded_len // rows
    half_rows = rows // 2
    k1 = np.arange(rows)[:, None]
    n1 = np.arange(half_rows)[None, :]
    angle1 = 2.0 * np.pi * k1 * n1 / rows
    first = np.concatenate([np.cos(angle1), -np.sin(angle1)], axis=0)
    n2 = np.arange(cols)[None, :]
    angle_t = 2.0 * np.pi * k1 * n2 / padded_len
    twist = (np.cos(angle_t), np.sin(angle_t))
    k2 = np.arange(cols)[:, None]
    angle2 = 2.0 * np.pi * k2 * n2 / cols
    c2, s2 = np.cos(angle2), np.sin(angle2)
    forward = np.block([[c2, -s2], [s2, c2]])
    backward = np.block([[c2, s2], [-s2, c2]])
    last = np.concatenate([np.cos(angle1.T), -np.sin(angle1.T)], axis=1) / padded_len
    as32 = lambda a: jnp.asarray(a.astype(np.float32))
    return rows, cols, as32(first), tuple(as32(t) for t in twist), as32(forward), as32(backward), as32(last)


def spectrum(field, tables):
    rows, cols, first, twist, forward, _, _ = tables
    chans = field.shape[1]
    grid = field.reshape(rows // 2, cols, chans).transpose(0, 2, 1).reshape(rows // 2, chans * cols)
    stage = jnp.dot(first, grid, precision=HIGH).reshape(2, rows, chans, cols)
    tw_cos = twist[0][:, None, :]
    tw_sin = twist[1][:, None, :]
    turned_real = stage[0] * tw_cos + stage[1] * tw_sin
    turned_imag = stage[1] * tw_cos - stage[0] * tw_sin
    joined = jnp.concatenate([turned_real, turned_imag], axis=2).reshape(rows * chans, 2 * cols)
    return jnp.dot(joined, forward, precision=HIGH).reshape(rows, chans, 2 * cols)


def causal_conv(source, long_filter, tables):
    rows, cols, _, twist, _, backward, last = tables
    chans = source.shape[1]
    spec_s = spectrum(source, tables)
    spec_f = spectrum(long_filter, tables)
    sr, si = spec_s[..., :cols], spec_s[..., cols:]
    fr, fi = spec_f[..., :cols], spec_f[..., cols:]
    prod = jnp.concatenate([sr * fr - si * fi, sr * fi + si * fr], axis=2).reshape(rows * chans, 2 * cols)
    back = jnp.dot(prod, backward, precision=HIGH).reshape(rows, chans, 2 * cols)
    br, bi = back[..., :cols], back[..., cols:]
    tw_cos = twist[0][:, None, :]
    tw_sin = twist[1][:, None, :]
    turned_real = br * tw_cos - bi * tw_sin
    turned_imag = bi * tw_cos + br * tw_sin
    stacked = jnp.concatenate([turned_real, turned_imag], axis=0).reshape(2 * rows, chans * cols)
    out = jnp.dot(last, stacked, precision=HIGH).reshape(rows // 2, chans, cols)
    return out.transpose(0, 2, 1).reshape(rows // 2 * cols, chans)


def on_device(
    query_projected, key_stream, value_stream, short_taps, skip_gain, long_filter, out_weight
):
    seq_count = lax.axis_size("seq")
    place = lax.axis_index("seq")
    streams = jnp.stack([query_projected, key_stream, value_stream])
    full = lax.all_to_all(streams, "seq", 2, 1, tiled=True)
    filt = lax.all_to_all(long_filter, "seq", 1, 0, tiled=True)
    chans = full.shape[2]
    seq_len = full.shape[1]
    taps = lax.dynamic_slice_in_dim(short_taps, place * chans, chans, axis=2)
    gain = lax.dynamic_slice_in_dim(skip_gain, place * chans, chans, axis=0)
    x = full.astype(jnp.float32)
    zeros = jnp.zeros_like(x[:, :2])
    extended = jnp.concatenate([zeros, x], axis=1)
    shaped = (
        taps[0][:, None, :] * extended[:, 2:]
        + taps[1][:, None, :] * extended[:, 1:-1]
        + taps[2][:, None, :] * extended[:, :-2]
    )
    source = shaped[1] * shaped[2]
    tables = dft_tables(seq_len)
    convolved = causal_conv(source, filt, tables)
    gated = (shaped[0] * (convolved + gain[None, :] * source)).astype(jnp.bfloat16)
    gated = lax.all_to_all(gated, "seq", 0, 1, tiled=True)
    terms = jnp.dot(gated, out_weight, preferred_element_type=jnp.float32)
    summed = lax.psum_scatter(terms, "chan", scatter_dimension=1, tiled=True)
    return lax.all_gather(summed.astype(jnp.bfloat16), "chan", axis=1, tiled=True)


def solution(mesh):
    return jax.shard_map(
        on_device,
        mesh=mesh,
        in_specs=(
            P("seq", "chan"),
            P("seq", "chan"),
            P("seq", "chan"),
            P(None, None, "chan"),
            P("chan"),
            P("seq", "chan"),
            P("chan", None),
        ),
        out_specs=P("seq", None),
        check_vma=False,
    )
```

time: 707 us -> 155 us (0.22); the launches traced: 698 us -> 154 us
  waiting for transfers between devices: 538 us -> 81.8 us
  other arithmetic: 51.6 us -> 4.85 us
  blocking collectives: 57.5 us -> 11.7 us
  between operations: 1.35 us -> 13.7 us
    ppermute x9 -> x0, waiting for transfers between devices: 538 us -> none  [the longest x8 530 us: from_partner(): return lax.ppermute(value, axis, pairs)]
    psum x1 -> x0, blocking collectives: 57.5 us -> none  [on_device(): mixed = lax.psum(terms, 'chan').astype(jnp.bfloat16)]
    reduce_scatter x0 -> x1, waiting for transfers between devices: none -> 35.5 us  [on_device(): summed = lax.psum_scatter(terms, 'chan', scatter_dimension=1, tiled=True)]
    all_gather x0 -> x1, waiting for transfers between devices: none -> 24.3 us  [on_device(): lax.all_gather(summed.astype(jnp.bfloat16), 'chan', axis=1, tiled=True)]
    select_n x8 -> x0, other arithmetic: 24.1 us -> none  [the longest x4 21.5 us: on_device(): values = jnp.where(upper_side, upper, values + partner)]
    all_to_all x0 -> x2, waiting for transfers between devices: none -> 22 us  [the longest x1 12 us: on_device(): full = lax.all_to_all(streams, 'seq', 2, 1, tiled=True)]
    sub x12 -> x2, other arithmetic: 19.6 us -> 0.66 us  [the longest x1 0.34 us: causal_conv(): turned_real = br * tw_cos - bi * tw_sin]
    ppermute x9 -> x0, starting transfers between devices: 16 us -> none  [the longest x8 12.4 us: from_partner(): return lax.ppermute(value, axis, pairs)]
  transfers between devices with their start and end apart: 9 -> 4, of which waited for: 9 -> 4; matrix products, arithmetic and copies ran while one was open for 0% -> 4% of each run, Pallas kernels for 0% -> 0%
where the time goes in v1:
time: 155 us; the launch traced here: 154 us
  waiting for transfers between devices  81.8 us (53%)
  matrix products  17.1 us (11%)
  between operations  13.7 us (9%)
  local copies, waits for them, and re-layouts  12.6 us (8%)
  starting transfers between devices  11.9 us (8%)
  blocking collectives  11.7 us (8%)
  other arithmetic  4.85 us (3%)
    reduce_scatter x1, waiting for transfers between devices, on_device(): summed = lax.psum_scatter(terms, 'chan', scatter_dimension=1, tiled=True)  35.5 us
    all_gather x1, waiting for transfers between devices, on_device(): lax.all_gather(summed.astype(jnp.bfloat16), 'chan', axis=1, tiled=True)  24.3 us
    all_to_all x1, waiting for transfers between devices, on_device(): full = lax.all_to_all(streams, 'seq', 2, 1, tiled=True)  12 us
    all_to_all x1, blocking collectives, on_device(): gated = lax.all_to_all(gated, 'seq', 0, 1, tiled=True)  11.7 us
    all_to_all x1, waiting for transfers between devices, on_device(): filt = lax.all_to_all(long_filter, 'seq', 1, 0, tiled=True)  10 us
    unnamed x29, local copies, waits for them, and re-layouts  8.44 us
    all_to_all x1, starting transfers between devices, on_device(): filt = lax.all_to_all(long_filter, 'seq', 1, 0, tiled=True)  8.16 us
    dot_general x1, matrix products, on_device(): terms = jnp.dot(gated, out_weight, preferred_element_type=jnp.float32)  5.4 us
  transfers between devices with their start and end apart: 4, of which 4 were waited for; matrix products, arithmetic and copies ran while one was open for 4% of the time, Pallas kernels for 0%

profile of v1, /device:TPU:0, one launch (start us, length us, event | category | flops | bytes accessed | tf_op | source)
XLA Modules:
  0.0 153.6 jit_solution(11696978924810241537)
XLA Ops:
  6.5 2.1 %copy.39 = f32[256,512]{0,1:T(8,128)} copy(f32[256,512]{1,0:T(8,128)} %param.18) | data formatting | bytes 1048576 | tf_op args[5]
  8.7 8.2 %all-to-all-start.1 = ((f32[256,16,32]{0,2,1:T(8,128)}), f32[256,16,32]{0,2,1:T(8,128)S(1)}, u32[]{:S(2)}, u32[]{:S(2)}) async-start(f32[256,16,32]{0,2,1:T(8,128)} %bitcast.10), calls=%async_computation.1 | async-start | bytes 1048576 | tf_op jit(solution)/shard_map/all_to_all | solution.py:72
  17.0 1.4 copy.35
  18.4 10.0 %all-to-all-done.1 = f32[256,16,32]{0,2,1:T(8,128)S(1)} async-done(((f32[256,16,32]{0,2,1:T(8,128)}), f32[256,16,32]{0,2,1:T(8,128)S(1)}, u32[]{:S(2)}, u32[]{:S(2)}) %all-to-all-start.1) | async-done | bytes 524320 | tf_op jit(solution)/shard_map/all_to_all | solution.py:72
  28.4 3.7 %all-to-all-start = ((bf16[3,256,512]{1,0,2:T(4,128)(2,1)}), bf16[3,256,512]{1,0,2:T(4,128)(2,1)S(1)}, u32[]{:S(2)}, u32[]{:S(2)}) async-start(bf16[3,256,512]{1,0,2:T(4,128)(2,1)} %copy.35), calls=%async_computation | async-start | bytes 2097152 | tf_op jit(solution)/shard_map/all_to_all | solution.py:71
  32.1 0.8 dynamic_slice.7
  32.8 0.8 dynamic-slice_bitcast_fusion.2
  33.6 0.3 copy.40
  34.0 1.8 %fusion.28 = f32[128,4096]{1,0:T(8,128)S(1)} fusion(f32[128,32]{1,0:T(8,128)S(1)} %copy-done.5, f32[32,128,32]{1,0,2:T(8,128)S(1)} %reshape.102), kind=kOutput, calls=%fused_computation.47 | convolution fusion | flops 201326592 | bytes 2637824 | tf_op jit(solution)/shard_map/dot_general | solution.py:37
  36.0 0.2 copy.52
  36.2 0.2 copy.53
  36.4 12.0 %all-to-all-done = bf16[3,256,512]{1,0,2:T(4,128)(2,1)S(1)} async-done(((bf16[3,256,512]{1,0,2:T(4,128)(2,1)}), bf16[3,256,512]{1,0,2:T(4,128)(2,1)S(1)}, u32[]{:S(2)}, u32[]{:S(2)}) %all-to-all-start) | async-done | bytes 786464 | tf_op jit(solution)/shard_map/all_to_all | solution.py:71
  48.7 0.9 multiply_add_fusion
  50.0 0.3 copy.38
  50.5 1.9 %fusion.25 = f32[128,4096]{1,0:T(8,128)S(1)} fusion(f32[128,32]{1,0:T(8,128)S(1)} %copy-done.5, f32[4,8,32,128]{3,2,1,0:T(8,128)S(1)} %bitcast.129), kind=kOutput, calls=%fused_computation.44 | convolution fusion | flops 201326592 | bytes 2637824 | tf_op jit(solution)/shard_map/dot_general | solution.py:37
  52.6 0.2 copy.50
  53.0 0.3 copy-done.6
  53.4 0.8 fusion.20
  54.3 1.9 %fusion.3 = f32[64,32,256]{2,1,0:T(8,128)S(1)} fusion(f32[256,256,1]{1,0,2:T(8,128)S(1)} %copy-done, f32[64,32,128]{2,1,0:T(8,128)S(1)} %get-tuple-element.10, f32[64,32,128]{2,1,0:T(8,128)S(1)} %get-tuple-element.9), kind=kOutput, calls=%fused_computation.3 | convolution fusion | flops 1611137024 | bytes 4456448 | tf_op jit(solution)/shard_map/dot_general | solution.py:43
  56.2 1.8 %fusion.7 = f32[64,32,256]{2,1,0:T(8,128)S(1)} fusion(f32[256,256,1]{1,0,2:T(8,128)S(1)} %copy-done, f32[64,32,128]{2,1,0:T(8,128)S(1)} %get-tuple-element.19, f32[64,32,128]{2,1,0:T(8,128)S(1)} %get-tuple-element.20), kind=kOutput, calls=%fused_computation.7 | convolution fusion | flops 1611137024 | bytes 4456448 | tf_op jit(solution)/shard_map/dot_general | solution.py:43
  58.0 0.3 multiply_subtract_fusion.1
  58.4 0.6 copy-done.1
  59.0 2.1 %fusion.11 = f32[64,32,256]{2,1,0:T(8,128)S(1)} fusion(f32[256,256,1]{1,0,2:T(8,128)S(1)} %copy-done.1, f32[64,32,128]{2,1,0:T(8,128)S(1)} %get-tuple-element.6, f32[64,32,128]{2,1,0:T(8,128)S(1)} %get-tuple-element.5), kind=kOutput, calls=%fused_computation.11 | convolution fusion | flops 1611137024 | bytes 4456448 | tf_op jit(solution)/shard_map/dot_general | solution.py:54
  61.1 0.3 multiply_subtract_fusion
  61.6 0.5 copy-done.8
  62.1 2.3 %fusion.15 = f32[4,32,8,128]{3,2,1,0:T(8,128)S(1)} fusion(f32[32,128]{1,0:T(8,128)S(1)} %copy-done.8, f32[16,8,32,128]{3,2,1,0:T(8,128)S(1)} %bitcast.120), kind=kOutput, calls=%fused_computation.18 | convolution fusion | flops 201326592 | bytes 2637824 | tf_op jit(solution)/shard_map/dot_general | solution.py:61
  64.9 11.7 %all_to_all.41 = bf16[16,256,32]{1,2,0:T(8,128)(2,1)S(1)} all-to-all(bf16[16,256,32]{1,2,0:T(8,128)(2,1)S(1)} %copy.43), channel_id=1, replica_groups=mesh['seq'=16,'chan'=8] {'seq'}, dimensions={0} | all-to-all | bytes 524288 | tf_op jit(solution)/shard_map/all_to_all | solution.py:89
  76.6 5.4 %fusion.35 = f32[256,4096]{1,0:T(8,128)} fusion(bf16[256,512]{0,1:T(8,128)(2,1)S(1)} %bitcast.130, bf16[512,4096]{1,0:T(8,128)(2,1)} %param.19), kind=kOutput, calls=%fused_computation.59 | convolution fusion | flops 1073741824 | bytes 8650752 | tf_op jit(solution)/shard_map/dot_general | solution.py:90
  82.1 35.5 %reduce-scatter.2.cloned.1.call-done = f32[256,512]{1,0:T(8,128)} async-done(((f32[256,4096]{1,0:T(8,128)}), f32[256,512]{1,0:T(8,128)}) %reduce-scatter.2.cloned.1.call-update) | async-done | bytes 524304 | tf_op jit(solution)/shard_map/reduce_scatter | solution.py:91
  117.5 1.8 %convert_element_type.24 = bf16[256,512]{1,0:T(8,128)(2,1)} convert(f32[256,512]{1,0:T(8,128)} %reduce-scatter.2.cloned.1.call-done) | non-fusion elementwise | flops 131072 | bytes 786432 | tf_op jit(solution)/shard_map/convert_element_type | solution.py:92
  119.3 24.3 %all-gather.2.cloned.1.call-done = bf16[256,4096]{1,0:T(8,128)(2,1)} async-done(((bf16[256,512]{1,0:T(8,128)(2,1)}), bf16[256,4096]{1,0:T(8,128)(2,1)}) %all-gather.2.cloned.1.call-update) | async-done | bytes 2097168 | tf_op jit(solution)/shard_map/all_gather | solution.py:92
  143.7 3.1 %copy.73 = bf16[256,4096]{1,0:T(8,128)(2,1)} copy(bf16[256,4096]{1,0:T(8,128)(2,1)} %all-gather.2.cloned.1.call-done) | data formatting | bytes 4194304
  (36 shorter events, 2.5 us)
Async XLA Ops:
  6.5 10.3 %copy-start.2 = (bf16[256,512]{1,0:T(8,128)(2,1)S(1)}, bf16[256,512]{1,0:T(8,128)(2,1)}, u32[]{:S(2)}) copy-start(bf16[256,512]{1,0:T(8,128)(2,1)} %param.15) | copy-start | bytes 786436
  6.5 10.3 %copy-start.3 = (bf16[256,512]{1,0:T(8,128)(2,1)S(1)}, bf16[256,512]{1,0:T(8,128)(2,1)}, u32[]{:S(2)}) copy-start(bf16[256,512]{1,0:T(8,128)(2,1)} %param.14) | copy-start | bytes 786436
  6.5 10.3 %copy-start.4 = (bf16[256,512]{1,0:T(8,128)(2,1)S(1)}, bf16[256,512]{1,0:T(8,128)(2,1)}, u32[]{:S(2)}) copy-start(bf16[256,512]{1,0:T(8,128)(2,1)} %param.13) | copy-start | bytes 786436
  8.7 19.7 %all-to-all-start.1 = ((f32[256,16,32]{0,2,1:T(8,128)}), f32[256,16,32]{0,2,1:T(8,128)S(1)}, u32[]{:S(2)}, u32[]{:S(2)}) async-start(f32[256,16,32]{0,2,1:T(8,128)} %bitcast.10), calls=%async_computation.1 | async-start | bytes 1048576 | tf_op jit(solution)/shard_map/all_to_all | solution.py:72
  18.4 15.6 %copy-start.5 = (f32[128,32]{1,0:T(8,128)S(1)}, f32[128,32]{1,0:T(8,128)}, u32[]{:S(2)}) copy-start(f32[128,32]{1,0:T(8,128)} %constant.26.clone) | copy-start | bytes 49156
  28.4 19.9 %all-to-all-start = ((bf16[3,256,512]{1,0,2:T(4,128)(2,1)}), bf16[3,256,512]{1,0,2:T(4,128)(2,1)S(1)}, u32[]{:S(2)}, u32[]{:S(2)}) async-start(bf16[3,256,512]{1,0,2:T(4,128)(2,1)} %copy.35), calls=%async_computation | async-start | bytes 2097152 | tf_op jit(solution)/shard_map/all_to_all | solution.py:71
  32.0 85.5 %reduce-scatter.2.cloned.1.call-start = ((), (), s32[]{:S(2)}) async-start(), calls=%async_computation.4 | async-start | bytes 4718592 | tf_op jit(solution)/shard_map/reduce_scatter | solution.py:91
  52.6 0.8 copy-start.6
  52.6 0.8 copy-start.7
  53.4 0.9 copy-start
  58.0 1.0 copy-start.1
  61.4 0.7 copy-start.8
  82.0 61.6 %all-gather.2.cloned.1.call-start = ((), (), s32[]{:S(2)}) async-start(), calls=%async_computation.5 | async-start | bytes 2359296 | tf_op jit(solution)/shard_map/all_gather | solution.py:92
Sparse Core Ops, SparseCore 0:
  82.1 35.3 reduce-scatter.1
  119.5 24.1 all-gather.1

commit v2 on v1

--- a/solution.py
+++ b/solution.py
@@ -88,22 +88,27 @@
     gated = (shaped[0] * (convolved + gain[None, :] * source)).astype(jnp.bfloat16)
     gated = lax.all_to_all(gated, "seq", 0, 1, tiled=True)
     terms = jnp.dot(gated, out_weight, preferred_element_type=jnp.float32)
-    summed = lax.psum_scatter(terms, "chan", scatter_dimension=1, tiled=True)
-    return lax.all_gather(summed.astype(jnp.bfloat16), "chan", axis=1, tiled=True)
+    summed = lax.psum_scatter(terms, "cc", scatter_dimension=1, tiled=True)
+    summed = lax.psum_scatter(summed, "cx", scatter_dimension=1, tiled=True)
+    rounded = lax.all_gather(summed.astype(jnp.bfloat16), "cx", axis=1, tiled=True)
+    return lax.all_gather(rounded, "cc", axis=1, tiled=True)
 
 
 def solution(mesh):
+    seq_size, chan_size = mesh.devices.shape
+    split = jax.sharding.Mesh(mesh.devices.reshape(seq_size, chan_size // 2, 2), ("seq", "cx", "cc"))
+    chan = ("cx", "cc")
     return jax.shard_map(
         on_device,
-        mesh=mesh,
+        mesh=split,
         in_specs=(
-            P("seq", "chan"),
-            P("seq", "chan"),
-            P("seq", "chan"),
-            P(None, None, "chan"),
-            P("chan"),
-            P("seq", "chan"),
-            P("chan", None),
+            P("seq", chan),
+            P("seq", chan),
+            P("seq", chan),
+            P(None, None, chan),
+            P(chan),
+            P("seq", chan),
+            P(chan, None),
         ),
         out_specs=P("seq", None),
         check_vma=False,

time: 155 us -> 180 us (1.16)
  waiting for transfers between devices: 81.8 us -> 107 us
    all_gather x1 -> x2, waiting for transfers between devices: 24.3 us -> 39.1 us  [the longest x1 23.9 us: on_device(): lax.all_gather(summed.astype(jnp.bfloat16), 'cx', axis=1, tiled=True)]
    reduce_scatter x1 -> x2, waiting for transfers between devices: 35.5 us -> 45.6 us  [the longest x1 33.4 us: on_device(): summed = lax.psum_scatter(summed, 'cx', scatter_dimension=1, tiled=True)]
  transfers between devices with their start and end apart: 4 -> 6, of which waited for: 4 -> 6; matrix products, arithmetic and copies ran while one was open for 4% -> 3% of each run, Pallas kernels for 0% -> 0%
where the time goes in v2:
time: 180 us; the launch traced here: 178 us
  waiting for transfers between devices  107 us (59%)
  matrix products  17.1 us (10%)
  between operations  13.5 us (8%)
  local copies, waits for them, and re-layouts  12.6 us (7%)
  starting transfers between devices  12 us (7%)
  blocking collectives  11.7 us (6%)
  other arithmetic  4.85 us (3%)
    reduce_scatter x1, waiting for transfers between devices, on_device(): summed = lax.psum_scatter(summed, 'cx', scatter_dimension=1, tiled=True)  33.4 us
    all_gather x1, waiting for transfers between devices, on_device(): lax.all_gather(summed.astype(jnp.bfloat16), 'cx', axis=1, tiled=True)  23.9 us
    all_gather x1, waiting for transfers between devices, on_device(): return lax.all_gather(rounded, 'cc', axis=1, tiled=True)  15.1 us
    reduce_scatter x1, waiting for transfers between devices, on_device(): summed = lax.psum_scatter(terms, 'cc', scatter_dimension=1, tiled=True)  12.2 us
    all_to_all x1, waiting for transfers between devices, on_device(): full = lax.all_to_all(streams, 'seq', 2, 1, tiled=True)  12 us
    all_to_all x1, blocking collectives, on_device(): gated = lax.all_to_all(gated, 'seq', 0, 1, tiled=True)  11.7 us
    all_to_all x1, waiting for transfers between devices, on_device(): filt = lax.all_to_all(long_filter, 'seq', 1, 0, tiled=True)  10 us
    unnamed x29, local copies, waits for them, and re-layouts  8.43 us
  transfers between devices with their start and end apart: 6, of which 6 were waited for; matrix products, arithmetic and copies ran while one was open for 3% of the time, Pallas kernels for 0%

profile of v2, /device:TPU:0, one launch (start us, length us, event | category | flops | bytes accessed | tf_op | source)
XLA Modules:
  0.0 178.4 jit_solution(8405225857322728920)
XLA Ops:
  6.5 2.1 %copy.39 = f32[256,512]{0,1:T(8,128)} copy(f32[256,512]{1,0:T(8,128)} %param.18) | data formatting | bytes 1048576 | tf_op args[5]
  8.7 8.2 %all-to-all-start.1 = ((f32[256,16,32]{0,2,1:T(8,128)}), f32[256,16,32]{0,2,1:T(8,128)S(1)}, u32[]{:S(2)}, u32[]{:S(2)}) async-start(f32[256,16,32]{0,2,1:T(8,128)} %bitcast.10), calls=%async_computation.1 | async-start | bytes 1048576 | tf_op jit(solution)/shard_map/all_to_all | solution.py:72
  16.9 1.4 copy.35
  18.4 10.0 %all-to-all-done.1 = f32[256,16,32]{0,2,1:T(8,128)S(1)} async-done(((f32[256,16,32]{0,2,1:T(8,128)}), f32[256,16,32]{0,2,1:T(8,128)S(1)}, u32[]{:S(2)}, u32[]{:S(2)}) %all-to-all-start.1) | async-done | bytes 524320 | tf_op jit(solution)/shard_map/all_to_all | solution.py:72
  28.4 3.7 %all-to-all-start = ((bf16[3,256,512]{1,0,2:T(4,128)(2,1)}), bf16[3,256,512]{1,0,2:T(4,128)(2,1)S(1)}, u32[]{:S(2)}, u32[]{:S(2)}) async-start(bf16[3,256,512]{1,0,2:T(4,128)(2,1)} %copy.35), calls=%async_computation | async-start | bytes 2097152 | tf_op jit(solution)/shard_map/all_to_all | solution.py:71
  32.1 0.8 dynamic_slice.7
  32.8 0.8 dynamic-slice_bitcast_fusion.2
  33.6 0.3 copy.40
  34.0 1.8 fusion.28
  36.0 0.2 copy.52
  36.3 12.0 %all-to-all-done = bf16[3,256,512]{1,0,2:T(4,128)(2,1)S(1)} async-done(((bf16[3,256,512]{1,0,2:T(4,128)(2,1)}), bf16[3,256,512]{1,0,2:T(4,128)(2,1)S(1)}, u32[]{:S(2)}, u32[]{:S(2)}) %all-to-all-start) | async-done | bytes 786464 | tf_op jit(solution)/shard_map/all_to_all | solution.py:71
  48.7 0.9 multiply_add_fusion
  50.0 0.3 copy.38
  50.5 1.9 %fusion.25 = f32[128,4096]{1,0:T(8,128)S(1)} fusion(f32[128,32]{1,0:T(8,128)S(1)} %copy-done.5, f32[4,8,32,128]{3,2,1,0:T(8,128)S(1)} %bitcast.129), kind=kOutput, calls=%fused_computation.44 | convolution fusion | flops 201326592 | bytes 2637824 | tf_op jit(solution)/shard_map/dot_general | solution.py:37
  53.0 0.3 copy-done.6
  53.4 0.8 fusion.20
  54.3 1.9 %fusion.3 = f32[64,32,256]{2,1,0:T(8,128)S(1)} fusion(f32[256,256,1]{1,0,2:T(8,128)S(1)} %copy-done, f32[64,32,128]{2,1,0:T(8,128)S(1)} %get-tuple-element.10, f32[64,32,128]{2,1,0:T(8,128)S(1)} %get-tuple-element.9), kind=kOutput, calls=%fused_computation.3 | convolution fusion | flops 1611137024 | bytes 4456448 | tf_op jit(solution)/shard_map/dot_general | solution.py:43
  56.2 1.8 %fusion.7 = f32[64,32,256]{2,1,0:T(8,128)S(1)} fusion(f32[256,256,1]{1,0,2:T(8,128)S(1)} %copy-done, f32[64,32,128]{2,1,0:T(8,128)S(1)} %get-tuple-element.19, f32[64,32,128]{2,1,0:T(8,128)S(1)} %get-tuple-element.20), kind=kOutput, calls=%fused_computation.7 | convolution fusion | flops 1611137024 | bytes 4456448 | tf_op jit(solution)/shard_map/dot_general | solution.py:43
  58.0 0.3 multiply_subtract_fusion.1
  58.4 0.6 copy-done.1
  59.0 2.1 %fusion.11 = f32[64,32,256]{2,1,0:T(8,128)S(1)} fusion(f32[256,256,1]{1,0,2:T(8,128)S(1)} %copy-done.1, f32[64,32,128]{2,1,0:T(8,128)S(1)} %get-tuple-element.6, f32[64,32,128]{2,1,0:T(8,128)S(1)} %get-tuple-element.5), kind=kOutput, calls=%fused_computation.11 | convolution fusion | flops 1611137024 | bytes 4456448 | tf_op jit(solution)/shard_map/dot_general | solution.py:54
  61.1 0.3 multiply_subtract_fusion
  61.6 0.5 copy-done.8
  62.1 2.3 %fusion.15 = f32[4,32,8,128]{3,2,1,0:T(8,128)S(1)} fusion(f32[32,128]{1,0:T(8,128)S(1)} %copy-done.8, f32[16,8,32,128]{3,2,1,0:T(8,128)S(1)} %bitcast.120), kind=kOutput, calls=%fused_computation.18 | convolution fusion | flops 201326592 | bytes 2637824 | tf_op jit(solution)/shard_map/dot_general | solution.py:61
  64.9 11.7 %all_to_all.41 = bf16[16,256,32]{1,2,0:T(8,128)(2,1)S(1)} all-to-all(bf16[16,256,32]{1,2,0:T(8,128)(2,1)S(1)} %copy.43), channel_id=1, replica_groups=mesh['seq'=16,'cx'=4,'cc'=2] {'seq'}, dimensions={0} | all-to-all | bytes 524288 | tf_op jit(solution)/shard_map/all_to_all | solution.py:89
  76.6 5.4 %fusion.35 = f32[256,4096]{1,0:T(8,128)} fusion(bf16[256,512]{0,1:T(8,128)(2,1)S(1)} %bitcast.130, bf16[512,4096]{1,0:T(8,128)(2,1)} %param.19), kind=kOutput, calls=%fused_computation.59 | convolution fusion | flops 1073741824 | bytes 8650752 | tf_op jit(solution)/shard_map/dot_general | solution.py:90
  82.1 12.2 %reduce-scatter.3.cloned.1.call-done = f32[256,2048]{1,0:T(8,128)} async-done(((f32[256,4096]{1,0:T(8,128)}), f32[256,2048]{1,0:T(8,128)}) %reduce-scatter.3.cloned.1.call-update) | async-done | bytes 2097168 | tf_op jit(solution)/shard_map/reduce_scatter | solution.py:91
  94.4 33.4 %reduce-scatter.5.cloned.1.call-done = f32[256,512]{1,0:T(8,128)} async-done(((f32[256,2048]{1,0:T(8,128)}), f32[256,512]{1,0:T(8,128)}) %reduce-scatter.5.cloned.1.call-update) | async-done | bytes 524304 | tf_op jit(solution)/shard_map/reduce_scatter | solution.py:92
  127.8 1.8 convert_element_type.24
  129.6 23.9 %all-gather.3.cloned.1.call-done = bf16[256,2048]{1,0:T(8,128)(2,1)} async-done(((bf16[256,512]{1,0:T(8,128)(2,1)}), bf16[256,2048]{1,0:T(8,128)(2,1)}) %all-gather.3.cloned.1.call-update) | async-done | bytes 1048592 | tf_op jit(solution)/shard_map/all_gather | solution.py:93
  153.6 15.1 %all-gather.5.cloned.1.call-done = bf16[256,4096]{1,0:T(8,128)(2,1)} async-done(((bf16[256,2048]{1,0:T(8,128)(2,1)}), bf16[256,4096]{1,0:T(8,128)(2,1)}) %all-gather.5.cloned.1.call-update) | async-done | bytes 2097168 | tf_op jit(solution)/shard_map/all_gather | solution.py:94
  168.7 3.1 %copy.73 = bf16[256,4096]{1,0:T(8,128)(2,1)} copy(bf16[256,4096]{1,0:T(8,128)(2,1)} %all-gather.5.cloned.1.call-done) | data formatting | bytes 4194304
  (42 shorter events, 3.0 us)
Async XLA Ops:
  6.5 10.3 %copy-start.2 = (bf16[256,512]{1,0:T(8,128)(2,1)S(1)}, bf16[256,512]{1,0:T(8,128)(2,1)}, u32[]{:S(2)}) copy-start(bf16[256,512]{1,0:T(8,128)(2,1)} %param.15) | copy-start | bytes 786436
  6.5 10.3 %copy-start.3 = (bf16[256,512]{1,0:T(8,128)(2,1)S(1)}, bf16[256,512]{1,0:T(8,128)(2,1)}, u32[]{:S(2)}) copy-start(bf16[256,512]{1,0:T(8,128)(2,1)} %param.14) | copy-start | bytes 786436
  6.5 10.3 %copy-start.4 = (bf16[256,512]{1,0:T(8,128)(2,1)S(1)}, bf16[256,512]{1,0:T(8,128)(2,1)}, u32[]{:S(2)}) copy-start(bf16[256,512]{1,0:T(8,128)(2,1)} %param.13) | copy-start | bytes 786436
  8.7 19.7 %all-to-all-start.1 = ((f32[256,16,32]{0,2,1:T(8,128)}), f32[256,16,32]{0,2,1:T(8,128)S(1)}, u32[]{:S(2)}, u32[]{:S(2)}) async-start(f32[256,16,32]{0,2,1:T(8,128)} %bitcast.10), calls=%async_computation.1 | async-start | bytes 1048576 | tf_op jit(solution)/shard_map/all_to_all | solution.py:72
  18.3 15.6 %copy-start.5 = (f32[128,32]{1,0:T(8,128)S(1)}, f32[128,32]{1,0:T(8,128)}, u32[]{:S(2)}) copy-start(f32[128,32]{1,0:T(8,128)} %constant.26.clone) | copy-start | bytes 49156
  28.4 19.9 %all-to-all-start = ((bf16[3,256,512]{1,0,2:T(4,128)(2,1)}), bf16[3,256,512]{1,0,2:T(4,128)(2,1)S(1)}, u32[]{:S(2)}, u32[]{:S(2)}) async-start(bf16[3,256,512]{1,0,2:T(4,128)(2,1)} %copy.35), calls=%async_computation | async-start | bytes 2097152 | tf_op jit(solution)/shard_map/all_to_all | solution.py:71
  32.0 62.3 %reduce-scatter.3.cloned.1.call-start = ((), (), s32[]{:S(2)}) async-start(), calls=%async_computation.5 | async-start | bytes 6291456 | tf_op jit(solution)/shard_map/reduce_scatter | solution.py:91
  52.6 0.8 copy-start.6
  52.6 0.8 copy-start.7
  53.4 0.9 copy-start
  58.0 1.0 copy-start.1
  61.4 0.7 copy-start.8
  82.0 45.7 %reduce-scatter.5.cloned.1.call-start = ((), (), s32[]{:S(2)}) async-start(), calls=%async_computation.6 | async-start | bytes 2621440 | tf_op jit(solution)/shard_map/reduce_scatter | solution.py:92
  94.3 59.2 %all-gather.3.cloned.1.call-start = ((), (), s32[]{:S(2)}) async-start(), calls=%async_computation.7 | async-start | bytes 1310720 | tf_op jit(solution)/shard_map/all_gather | solution.py:93
  129.6 39.1 %all-gather.5.cloned.1.call-start = ((), (), s32[]{:S(2)}) async-start(), calls=%async_computation.8 | async-start | bytes 3145728 | tf_op jit(solution)/shard_map/all_gather | solution.py:94
Sparse Core Ops, SparseCore 0:
  82.1 12.1 reduce-scatter.2
  96.7 31.0 reduce-scatter.4
  129.7 23.8 all-gather.2
  155.1 13.6 all-gather.4

commit v3 on v1

--- a/solution.py
+++ b/solution.py
@@ -5,7 +5,7 @@
 from jax import lax
 from jax.sharding import PartitionSpec as P
 
-HIGH = lax.Precision.HIGHEST
+HIGH = lax.Precision.HIGH
 
 
 def dft_tables(seq_len):
@@ -88,8 +88,7 @@
     gated = (shaped[0] * (convolved + gain[None, :] * source)).astype(jnp.bfloat16)
     gated = lax.all_to_all(gated, "seq", 0, 1, tiled=True)
     terms = jnp.dot(gated, out_weight, preferred_element_type=jnp.float32)
-    summed = lax.psum_scatter(terms, "chan", scatter_dimension=1, tiled=True)
-    return lax.all_gather(summed.astype(jnp.bfloat16), "chan", axis=1, tiled=True)
+    return lax.psum(terms, "chan").astype(jnp.bfloat16)
 
 
 def solution(mesh):

time: 155 us -> 130 us (0.84)
  waiting for transfers between devices: 81.8 us -> 22.8 us
  blocking collectives: 11.7 us -> 69.2 us
  between operations: 13.7 us -> 0.33 us
  matrix products: 17.1 us -> 12.2 us
  local copies, waits for them, and re-layouts: 12.6 us -> 10.2 us
  other arithmetic: 4.85 us -> 3.08 us
    psum x0 -> x1, blocking collectives: none -> 57.5 us  [on_device(): return lax.psum(terms, 'chan').astype(jnp.bfloat16)]
    reduce_scatter x1 -> x0, waiting for transfers between devices: 35.5 us -> none  [on_device(): summed = lax.psum_scatter(terms, 'chan', scatter_dimension=1, tiled=True)]
    all_gather x1 -> x0, waiting for transfers between devices: 24.3 us -> none  [on_device(): lax.all_gather(summed.astype(jnp.bfloat16), 'chan', axis=1, tiled=True)]
    unnamed x29 -> x30, local copies, waits for them, and re-layouts: 8.44 us -> 6.11 us
    convert_element_type x1 -> x0, other arithmetic: 1.77 us -> none  [on_device(): summed.astype(jnp.bfloat16)]
    dot_general x2, matrix products: 3.68 us -> 2.03 us  [spectrum(): jnp.dot(joined, forward, precision=HIGH).reshape(rows, chans, 2 * cols)]
    dot_general x2, matrix products: 3.64 us -> 2 us  [spectrum(): stage = jnp.dot(first, grid, precision=HIGH).reshape(2, rows, chans, cols)]
  transfers between devices with their start and end apart: 4 -> 2, of which waited for: 4 -> 2; matrix products, arithmetic and copies ran while one was open for 4% -> 4% of each run, Pallas kernels for 0% -> 0%
where the time goes in v3:
time: 130 us
  blocking collectives  69.2 us (53%)
  waiting for transfers between devices  22.8 us (18%)
  matrix products  12.2 us (9%)
  starting transfers between devices  11.8 us (9%)
  local copies, waits for them, and re-layouts  10.2 us (8%)
  other arithmetic  3.08 us (2%)
    psum x1, blocking collectives, on_device(): return lax.psum(terms, 'chan').astype(jnp.bfloat16)  57.5 us
    all_to_all x1, waiting for transfers between devices, on_device(): full = lax.all_to_all(streams, 'seq', 2, 1, tiled=True)  12.8 us
    all_to_all x1, blocking collectives, on_device(): gated = lax.all_to_all(gated, 'seq', 0, 1, tiled=True)  11.7 us
    all_to_all x1, waiting for transfers between devices, on_device(): filt = lax.all_to_all(long_filter, 'seq', 1, 0, tiled=True)  10 us
    all_to_all x1, starting transfers between devices, on_device(): filt = lax.all_to_all(long_filter, 'seq', 1, 0, tiled=True)  8.16 us
    unnamed x30, local copies, waits for them, and re-layouts  6.11 us
    dot_general x1, matrix products, on_device(): terms = jnp.dot(gated, out_weight, preferred_element_type=jnp.float32)  5.43 us
    all_to_all x1, starting transfers between devices, on_device(): full = lax.all_to_all(streams, 'seq', 2, 1, tiled=True)  3.66 us
  transfers between devices with their start and end apart: 2, of which 2 were waited for; matrix products, arithmetic and copies ran while one was open for 4% of the time, Pallas kernels for 0%

profile of v3, /device:TPU:0, one launch (start us, length us, event | category | flops | bytes accessed | tf_op | source)
XLA Modules:
  0.0 129.7 jit_solution(15449576378823709886)
XLA Ops:
  0.0 2.1 %copy.39 = f32[256,512]{0,1:T(8,128)} copy(f32[256,512]{1,0:T(8,128)} %param.18) | data formatting | bytes 1048576 | tf_op args[5]
  2.1 8.2 %all-to-all-start.1 = ((f32[256,16,32]{0,2,1:T(8,128)}), f32[256,16,32]{0,2,1:T(8,128)S(1)}, u32[]{:S(2)}, u32[]{:S(2)}) async-start(f32[256,16,32]{0,2,1:T(8,128)} %bitcast.10), calls=%async_computation.1 | async-start | bytes 1048576 | tf_op jit(solution)/shard_map/all_to_all | solution.py:72
  10.4 1.4 %copy.35 = bf16[3,256,512]{1,0,2:T(4,128)(2,1)} copy(bf16[3,256,512]{2,1,0:T(8,128)(2,1)S(1)} %pad_maximum_fusion.1) | data formatting | bytes 1572864 | tf_op jit(solution)/shard_map/stack | solution.py:70
  11.8 10.0 %all-to-all-done.1 = f32[256,16,32]{0,2,1:T(8,128)S(1)} async-done(((f32[256,16,32]{0,2,1:T(8,128)}), f32[256,16,32]{0,2,1:T(8,128)S(1)}, u32[]{:S(2)}, u32[]{:S(2)}) %all-to-all-start.1) | async-done | bytes 524320 | tf_op jit(solution)/shard_map/all_to_all | solution.py:72
  21.8 3.7 %all-to-all-start = ((bf16[3,256,512]{1,0,2:T(4,128)(2,1)}), bf16[3,256,512]{1,0,2:T(4,128)(2,1)S(1)}, u32[]{:S(2)}, u32[]{:S(2)}) async-start(bf16[3,256,512]{1,0,2:T(4,128)(2,1)} %copy.35), calls=%async_computation | async-start | bytes 2097152 | tf_op jit(solution)/shard_map/all_to_all | solution.py:71
  25.5 0.8 dynamic_slice.7
  26.3 0.8 dynamic-slice_bitcast_fusion.2
  27.0 0.3 copy.40
  27.4 1.0 fusion.28
  28.6 0.2 copy.52
  28.8 0.2 copy.53
  29.0 12.8 %all-to-all-done = bf16[3,256,512]{1,0,2:T(4,128)(2,1)S(1)} async-done(((bf16[3,256,512]{1,0,2:T(4,128)(2,1)}), bf16[3,256,512]{1,0,2:T(4,128)(2,1)S(1)}, u32[]{:S(2)}, u32[]{:S(2)}) %all-to-all-start) | async-done | bytes 786464 | tf_op jit(solution)/shard_map/all_to_all | solution.py:71
  42.2 0.9 multiply_add_fusion
  43.5 0.3 copy.38
  43.8 1.0 copy.55
  44.8 1.0 fusion.25
  45.8 0.2 slice_bitcast_fusion.3
  46.1 0.2 copy.50
  46.3 0.2 copy.51
  46.5 0.3 copy-done.7
  46.8 0.8 fusion.20
  47.8 1.0 fusion.3
  48.8 1.0 fusion.7
  49.8 0.3 multiply_subtract_fusion.1
  50.2 0.6 copy-done.2
  50.8 1.0 fusion.11
  51.8 0.3 multiply_subtract_fusion
  52.3 0.5 copy-done.9
  52.9 1.7 %fusion.15 = f32[4,32,8,128]{3,2,1,0:T(8,128)S(1)} fusion(f32[32,128]{1,0:T(8,128)S(1)} %copy-done.9, f32[16,8,32,128]{3,2,1,0:T(8,128)S(1)} %bitcast.120), kind=kOutput, calls=%fused_computation.18 | convolution fusion | flops 100663296 | bytes 2637824 | tf_op jit(solution)/shard_map/dot_general | solution.py:61
  55.0 11.7 %all_to_all.41 = bf16[16,256,32]{1,2,0:T(8,128)(2,1)S(1)} all-to-all(bf16[16,256,32]{1,2,0:T(8,128)(2,1)S(1)} %copy.43), channel_id=1, replica_groups=mesh['seq'=16,'chan'=8] {'seq'}, dimensions={0} | all-to-all | bytes 524288 | tf_op jit(solution)/shard_map/all_to_all | solution.py:89
  66.7 5.4 %fusion.35 = f32[256,4096]{1,0:T(8,128)} fusion(bf16[256,512]{0,1:T(8,128)(2,1)S(1)} %bitcast.130, bf16[512,4096]{1,0:T(8,128)(2,1)} %param.19), kind=kOutput, calls=%fused_computation.59 | convolution fusion | flops 1073741824 | bytes 8650752 | tf_op jit(solution)/shard_map/dot_general | solution.py:90
  72.2 57.5 %all-reduce.2 = bf16[256,4096]{1,0:T(8,128)(2,1)} all-reduce(f32[256,4096]{1,0:T(8,128)} %fusion.35), channel_id=1, replica_groups=mesh['seq'=16,'chan'=8] {'chan'}, use_global_device_ids=true, to_apply=%region_0.0 | all-reduce | flops 1048576 | bytes 6291456 | tf_op jit(solution)/shard_map/psum | solution.py:91
  (31 shorter events, 1.8 us)
Async XLA Ops:
  0.0 10.3 %copy-start.3 = (bf16[256,512]{1,0:T(8,128)(2,1)S(1)}, bf16[256,512]{1,0:T(8,128)(2,1)}, u32[]{:S(2)}) copy-start(bf16[256,512]{1,0:T(8,128)(2,1)} %param.15) | copy-start | bytes 786436
  0.0 10.3 %copy-start.4 = (bf16[256,512]{1,0:T(8,128)(2,1)S(1)}, bf16[256,512]{1,0:T(8,128)(2,1)}, u32[]{:S(2)}) copy-start(bf16[256,512]{1,0:T(8,128)(2,1)} %param.14) | copy-start | bytes 786436
  0.0 10.3 %copy-start.5 = (bf16[256,512]{1,0:T(8,128)(2,1)S(1)}, bf16[256,512]{1,0:T(8,128)(2,1)}, u32[]{:S(2)}) copy-start(bf16[256,512]{1,0:T(8,128)(2,1)} %param.13) | copy-start | bytes 786436
  2.1 19.7 %all-to-all-start.1 = ((f32[256,16,32]{0,2,1:T(8,128)}), f32[256,16,32]{0,2,1:T(8,128)S(1)}, u32[]{:S(2)}, u32[]{:S(2)}) async-start(f32[256,16,32]{0,2,1:T(8,128)} %bitcast.10), calls=%async_computation.1 | async-start | bytes 1048576 | tf_op jit(solution)/shard_map/all_to_all | solution.py:72
  11.8 15.6 %copy-start.6 = (f32[128,32]{1,0:T(8,128)S(1)}, f32[128,32]{1,0:T(8,128)}, u32[]{:S(2)}) copy-start(f32[128,32]{1,0:T(8,128)} %constant.26.clone) | copy-start | bytes 49156
  21.8 19.9 %all-to-all-start = ((bf16[3,256,512]{1,0,2:T(4,128)(2,1)}), bf16[3,256,512]{1,0,2:T(4,128)(2,1)S(1)}, u32[]{:S(2)}, u32[]{:S(2)}) async-start(bf16[3,256,512]{1,0,2:T(4,128)(2,1)} %copy.35), calls=%async_computation | async-start | bytes 2097152 | tf_op jit(solution)/shard_map/all_to_all | solution.py:71
  46.0 0.8 copy-start.7
  46.1 0.8 copy-start.8
  46.8 0.9 copy-start.1
  49.8 1.0 copy-start.2
  52.1 0.7 copy-start.9
  52.9 2.0 %copy-start = (f32[4,8,16,256]{3,2,1,0:T(8,128)S(1)}, f32[4,8,16,256]{3,2,1,0:T(8,128)}, u32[]{:S(2)}) copy-start(f32[4,8,16,256]{3,2,1,0:T(8,128)} %copy.55) | copy-start | bytes 1572868

commit v4 on v3

--- a/solution.py
+++ b/solution.py
@@ -67,10 +67,14 @@
 ):
     seq_count = lax.axis_size("seq")
     place = lax.axis_index("seq")
+    shard_len, local_chans = query_projected.shape
+    chans = local_chans // seq_count
     streams = jnp.stack([query_projected, key_stream, value_stream])
-    full = lax.all_to_all(streams, "seq", 2, 1, tiled=True)
-    filt = lax.all_to_all(long_filter, "seq", 1, 0, tiled=True)
-    chans = full.shape[2]
+    streams = streams.reshape(3, shard_len, seq_count, chans).transpose(2, 0, 1, 3)
+    full = lax.all_to_all(streams, "seq", 0, 0, tiled=True)
+    full = full.transpose(1, 0, 2, 3).reshape(3, seq_count * shard_len, chans)
+    filt = long_filter.reshape(shard_len, seq_count, chans).transpose(1, 0, 2)
+    filt = lax.all_to_all(filt, "seq", 0, 0, tiled=True).reshape(seq_count * shard_len, chans)
     seq_len = full.shape[1]
     taps = lax.dynamic_slice_in_dim(short_taps, place * chans, chans, axis=2)
     gain = lax.dynamic_slice_in_dim(skip_gain, place * chans, chans, axis=0)
@@ -86,9 +90,16 @@
     tables = dft_tables(seq_len)
     convolved = causal_conv(source, filt, tables)
     gated = (shaped[0] * (convolved + gain[None, :] * source)).astype(jnp.bfloat16)
-    gated = lax.all_to_all(gated, "seq", 0, 1, tiled=True)
-    terms = jnp.dot(gated, out_weight, preferred_element_type=jnp.float32)
-    return lax.psum(terms, "chan").astype(jnp.bfloat16)
+    gated = gated.reshape(seq_count, 2, shard_len // 2, chans)
+    halves = []
+    for half in range(2):
+        back = lax.all_to_all(gated[:, half], "seq", 0, 0, tiled=True)
+        back = back.transpose(1, 0, 2).reshape(shard_len // 2, local_chans)
+        terms = jnp.dot(back, out_weight, preferred_element_type=jnp.float32)
+        if halves:
+            halves[-1], terms = lax.optimization_barrier((halves[-1], terms))
+        halves.append(lax.psum(terms, "chan"))
+    return jnp.concatenate(halves, axis=0).astype(jnp.bfloat16)
 
 
 def solution(mesh):

time: 130 us -> 186 us (1.43)
  blocking collectives: 69.2 us -> 107 us
  starting transfers between devices: 11.8 us -> 18.8 us
  waiting for transfers between devices: 22.8 us -> 27 us
  other arithmetic: 3.08 us -> 6.17 us
  local copies, waits for them, and re-layouts: 10.2 us -> 12.8 us
    psum x1 -> x2, blocking collectives: 57.5 us -> 107 us  [on_device(): halves.append(lax.psum(terms, 'chan'))]
    all_to_all x1 -> x0, blocking collectives: 11.7 us -> none  [on_device(): gated = lax.all_to_all(gated, 'seq', 0, 1, tiled=True)]
    all_to_all x2 -> x4, starting transfers between devices: 11.8 us -> 18.8 us  [the longest x1 8.16 us: on_device(): lax.all_to_all(filt, 'seq', 0, 0, tiled=True)]
    all_to_all x2 -> x4, waiting for transfers between devices: 22.8 us -> 27 us  [the longest x1 10.1 us: on_device(): lax.all_to_all(filt, 'seq', 0, 0, tiled=True)]
    concatenate x0 -> x1, other arithmetic: none -> 2.73 us  [on_device(): return jnp.concatenate(halves, axis=0).astype(jnp.bfloat16)]
    unnamed x30 -> x32, local copies, waits for them, and re-layouts: 6.11 us -> 5.68 us
    dot_general x1 -> x2, matrix products: 5.43 us -> 5.86 us  [on_device(): terms = jnp.dot(back, out_weight, preferred_element_type=jnp.float32)]
  transfers between devices with their start and end apart: 2 -> 4, of which waited for: 2 -> 3; matrix products, arithmetic and copies ran while one was open for 4% -> 5% of each run, Pallas kernels for 0% -> 0%
where the time goes in v4:
time: 186 us; the launch traced here: 185 us
  blocking collectives  107 us (58%)
  waiting for transfers between devices  27 us (15%)
  starting transfers between devices  18.8 us (10%)
  local copies, waits for them, and re-layouts  12.8 us (7%)
  matrix products  12.8 us (7%)
  other arithmetic  6.17 us (3%)
    psum x2, blocking collectives, on_device(): halves.append(lax.psum(terms, 'chan'))  107 us
    all_to_all x1, waiting for transfers between devices, on_device(): lax.all_to_all(filt, 'seq', 0, 0, tiled=True)  10.1 us
    all_to_all x1, waiting for transfers between devices, on_device(): full = lax.all_to_all(streams, 'seq', 0, 0, tiled=True)  9.77 us
    all_to_all x1, starting transfers between devices, on_device(): lax.all_to_all(filt, 'seq', 0, 0, tiled=True)  8.16 us
    all_to_all x2, waiting for transfers between devices, on_device(): back = lax.all_to_all(gated[:, half], 'seq', 0, 0, tiled=True)  7.21 us
    all_to_all x2, starting transfers between devices, on_device(): back = lax.all_to_all(gated[:, half], 'seq', 0, 0, tiled=True)  7.02 us
    dot_general x2, matrix products, on_device(): terms = jnp.dot(back, out_weight, preferred_element_type=jnp.float32)  5.86 us
    unnamed x32, local copies, waits for them, and re-layouts  5.68 us
  transfers between devices with their start and end apart: 4, of which 3 were waited for; matrix products, arithmetic and copies ran while one was open for 5% of the time, Pallas kernels for 0%

profile of v4, /device:TPU:0, one launch (start us, length us, event | category | flops | bytes accessed | tf_op | source)
XLA Modules:
  0.0 185.4 jit_solution(14469542539871681092)
XLA Ops:
  0.0 2.1 %copy.40 = f32[256,512]{0,1:T(8,128)} copy(f32[256,512]{1,0:T(8,128)} %param.18) | data formatting | bytes 1048576 | tf_op args[5]
  2.1 8.2 %all-to-all-start.1 = ((f32[16,256,32]{1,2,0:T(8,128)}), f32[16,256,32]{1,2,0:T(8,128)S(1)}, u32[]{:S(2)}, u32[]{:S(2)}) async-start(f32[16,256,32]{1,2,0:T(8,128)} %bitcast.11), calls=%async_computation.1 | async-start | bytes 1048576 | tf_op jit(solution)/shard_map/all_to_all | solution.py:77
  10.8 0.9 copy.37
  11.8 10.1 %all-to-all-done.1 = f32[16,256,32]{1,2,0:T(8,128)S(1)} async-done(((f32[16,256,32]{1,2,0:T(8,128)}), f32[16,256,32]{1,2,0:T(8,128)S(1)}, u32[]{:S(2)}, u32[]{:S(2)}) %all-to-all-start.1) | async-done | bytes 524320 | tf_op jit(solution)/shard_map/all_to_all | solution.py:77
  21.8 3.6 %all-to-all-start = ((bf16[16,3,256,32]{2,3,1,0:T(8,128)(2,1)}), bf16[16,3,256,32]{2,3,1,0:T(8,128)(2,1)S(1)}, u32[]{:S(2)}, u32[]{:S(2)}) async-start(bf16[16,3,256,32]{2,3,1,0:T(8,128)(2,1)} %copy.37), calls=%async_computation | async-start | bytes 1572864 | tf_op jit(solution)/shard_map/all_to_all | solution.py:74
  25.4 0.8 dynamic_slice.7
  26.2 0.8 dynamic-slice_bitcast_fusion.2
  27.4 1.0 fusion.25
  28.9 9.8 %all-to-all-done = bf16[16,3,256,32]{2,3,1,0:T(8,128)(2,1)S(1)} async-done(((bf16[16,3,256,32]{2,3,1,0:T(8,128)(2,1)}), bf16[16,3,256,32]{2,3,1,0:T(8,128)(2,1)S(1)}, u32[]{:S(2)}, u32[]{:S(2)}) %all-to-all-start) | async-done | bytes 786464 | tf_op jit(solution)/shard_map/all_to_all | solution.py:74
  39.0 0.9 multiply_add_fusion
  40.0 1.2 squeeze.27
  41.3 0.4 mul.193
  42.1 1.0 fusion.22
  44.2 0.6 fusion.20
  45.1 1.0 fusion.3
  46.1 1.0 fusion.7
  47.5 0.6 copy-done.2
  48.1 1.0 fusion.11
  49.7 0.5 copy-done.9
  50.2 1.9 %fusion.15 = f32[4,8,32,128]{3,1,2,0:T(8,128)S(1)} fusion(f32[32,128]{1,0:T(8,128)S(1)} %copy-done.9, f32[16,8,32,128]{3,2,1,0:T(8,128)S(1)} %bitcast.114), kind=kOutput, calls=%fused_computation.19 | convolution fusion | flops 100663296 | bytes 2637824 | tf_op jit(solution)/shard_map/dot_general | solution.py:61
  52.5 0.7 multiply_convert_fusion
  53.2 0.4 fusion.31
  53.6 0.7 copy.73
  54.3 3.5 %all-to-all-start.2 = ((bf16[16,128,32]{1,2,0:T(8,128)(2,1)}), bf16[16,128,32]{1,2,0:T(8,128)(2,1)S(1)}, u32[]{:S(2)}, u32[]{:S(2)}) async-start(bf16[16,128,32]{1,2,0:T(8,128)(2,1)} %bitcast.113), calls=%async_computation.2 | async-start | bytes 262144 | tf_op jit(solution)/shard_map/all_to_all | solution.py:96
  57.9 0.7 copy.72
  58.6 7.2 %all-to-all-done.2 = bf16[16,128,32]{1,2,0:T(8,128)(2,1)S(1)} async-done(((bf16[16,128,32]{1,2,0:T(8,128)(2,1)}), bf16[16,128,32]{1,2,0:T(8,128)(2,1)S(1)}, u32[]{:S(2)}, u32[]{:S(2)}) %all-to-all-start.2) | async-done | bytes 131104 | tf_op jit(solution)/shard_map/all_to_all | solution.py:96
  65.8 3.5 %all-to-all-start.3 = ((bf16[16,128,32]{1,2,0:T(8,128)(2,1)}), bf16[16,128,32]{1,2,0:T(8,128)(2,1)S(1)}, u32[]{:S(2)}, u32[]{:S(2)}) async-start(bf16[16,128,32]{1,2,0:T(8,128)(2,1)} %bitcast.112), calls=%async_computation.3 | async-start | bytes 262144 | tf_op jit(solution)/shard_map/all_to_all | solution.py:96
  69.3 2.9 %fusion.32 = f32[128,4096]{1,0:T(8,128)S(1)} fusion(bf16[128,512]{0,1:T(8,128)(2,1)S(1)} %bitcast.124, bf16[512,4096]{1,0:T(8,128)(2,1)} %param.19), kind=kOutput, calls=%fused_computation.58 | convolution fusion | flops 536870912 | bytes 6422528 | tf_op jit(solution)/shard_map/dot_general | solution.py:98
  72.3 52.4 %all-reduce.3 = bf16[128,4096]{1,0:T(8,128)(2,1)S(1)} all-reduce(f32[128,4096]{1,0:T(8,128)S(1)} %fusion.32), channel_id=1, replica_groups=mesh['seq'=16,'chan'=8] {'chan'}, use_global_device_ids=true, to_apply=%region_0.0 | all-reduce | flops 524288 | bytes 3145728 | tf_op jit(solution)/shard_map/psum | solution.py:101
  124.6 2.9 %fusion.33 = f32[128,4096]{1,0:T(8,128)S(1)} fusion(bf16[128,512]{0,1:T(8,128)(2,1)S(1)} %bitcast.125, bf16[512,4096]{1,0:T(8,128)(2,1)} %param.19), kind=kOutput, calls=%fused_computation.59 | convolution fusion | flops 536870912 | bytes 6422528 | tf_op jit(solution)/shard_map/dot_general | solution.py:98
  127.6 55.1 %all-reduce.4 = bf16[128,4096]{1,0:T(8,128)(2,1)} all-reduce(f32[128,4096]{1,0:T(8,128)S(1)} %fusion.33), channel_id=1, replica_groups=mesh['seq'=16,'chan'=8] {'chan'}, use_global_device_ids=true, to_apply=%region_1.0 | all-reduce | flops 524288 | bytes 3145728 | tf_op jit(solution)/shard_map/psum | solution.py:101
  182.7 2.7 %pad_maximum_fusion.1 = bf16[256,4096]{1,0:T(8,128)(2,1)} fusion(bf16[128,4096]{1,0:T(8,128)(2,1)} %all-reduce.4, bf16[128,4096]{1,0:T(8,128)(2,1)S(1)} %all-reduce.3), kind=kLoop, calls=%fused_computation.16 | loop fusion | flops 4194304 | bytes 4194304 | tf_op jit(solution)/shard_map/concatenate | solution.py:102
  (41 shorter events, 4.7 us)
Async XLA Ops:
  0.0 10.3 %copy-start.3 = (bf16[256,512]{1,0:T(8,128)(2,1)S(1)}, bf16[256,512]{1,0:T(8,128)(2,1)}, u32[]{:S(2)}) copy-start(bf16[256,512]{1,0:T(8,128)(2,1)} %param.13) | copy-start | bytes 786436
  0.0 10.4 %copy-start.4 = (bf16[256,512]{1,0:T(8,128)(2,1)S(1)}, bf16[256,512]{1,0:T(8,128)(2,1)}, u32[]{:S(2)}) copy-start(bf16[256,512]{1,0:T(8,128)(2,1)} %param.14) | copy-start | bytes 786436
  0.0 10.6 %copy-start.5 = (bf16[256,512]{1,0:T(8,128)(2,1)S(1)}, bf16[256,512]{1,0:T(8,128)(2,1)}, u32[]{:S(2)}) copy-start(bf16[256,512]{1,0:T(8,128)(2,1)} %param.15) | copy-start | bytes 786436
  2.1 19.7 %all-to-all-start.1 = ((f32[16,256,32]{1,2,0:T(8,128)}), f32[16,256,32]{1,2,0:T(8,128)S(1)}, u32[]{:S(2)}, u32[]{:S(2)}) async-start(f32[16,256,32]{1,2,0:T(8,128)} %bitcast.11), calls=%async_computation.1 | async-start | bytes 1048576 | tf_op jit(solution)/shard_map/all_to_all | solution.py:77
  11.8 15.6 %copy-start.6 = (f32[128,32]{1,0:T(8,128)S(1)}, f32[128,32]{1,0:T(8,128)}, u32[]{:S(2)}) copy-start(f32[128,32]{1,0:T(8,128)} %constant.26.clone) | copy-start | bytes 49156
  21.8 16.9 %all-to-all-start = ((bf16[16,3,256,32]{2,3,1,0:T(8,128)(2,1)}), bf16[16,3,256,32]{2,3,1,0:T(8,128)(2,1)S(1)}, u32[]{:S(2)}, u32[]{:S(2)}) async-start(bf16[16,3,256,32]{2,3,1,0:T(8,128)(2,1)} %copy.37), calls=%async_computation | async-start | bytes 1572864 | tf_op jit(solution)/shard_map/all_to_all | solution.py:74
  43.4 0.8 copy-start.7
  43.4 0.8 copy-start.8
  44.2 0.9 copy-start.1
  47.1 1.0 copy-start.2
  49.5 0.7 copy-start.9
  50.2 2.3 %copy-start = (f32[16,2,128,32]{2,1,0,3:T(2,128)S(1)}, f32[16,2,128,32]{2,1,0,3:T(2,128)}, u32[]{:S(2)}) copy-start(f32[16,2,128,32]{2,1,0,3:T(2,128)} %squeeze.27) | copy-start | bytes 1572868
  54.3 11.5 %all-to-all-start.2 = ((bf16[16,128,32]{1,2,0:T(8,128)(2,1)}), bf16[16,128,32]{1,2,0:T(8,128)(2,1)S(1)}, u32[]{:S(2)}, u32[]{:S(2)}) async-start(bf16[16,128,32]{1,2,0:T(8,128)(2,1)} %bitcast.113), calls=%async_computation.2 | async-start | bytes 262144 | tf_op jit(solution)/shard_map/all_to_all | solution.py:96
  65.8 58.8 %all-to-all-start.3 = ((bf16[16,128,32]{1,2,0:T(8,128)(2,1)}), bf16[16,128,32]{1,2,0:T(8,128)(2,1)S(1)}, u32[]{:S(2)}, u32[]{:S(2)}) async-start(bf16[16,128,32]{1,2,0:T(8,128)(2,1)} %bitcast.112), calls=%async_computation.3 | async-start | bytes 262144 | tf_op jit(solution)/shard_map/all_to_all | solution.py:96

commit v5 on v3

--- a/solution.py
+++ b/solution.py
@@ -30,11 +30,10 @@
     return rows, cols, as32(first), tuple(as32(t) for t in twist), as32(forward), as32(backward), as32(last)
 
 
-def spectrum(field, tables):
+def spectrum(grid, tables):
     rows, cols, first, twist, forward, _, _ = tables
-    chans = field.shape[1]
-    grid = field.reshape(rows // 2, cols, chans).transpose(0, 2, 1).reshape(rows // 2, chans * cols)
-    stage = jnp.dot(first, grid, precision=HIGH).reshape(2, rows, chans, cols)
+    chans = grid.shape[1]
+    stage = jnp.dot(first, grid.reshape(rows // 2, chans * cols), precision=HIGH).reshape(2, rows, chans, cols)
     tw_cos = twist[0][:, None, :]
     tw_sin = twist[1][:, None, :]
     turned_real = stage[0] * tw_cos + stage[1] * tw_sin
@@ -58,8 +57,13 @@
     turned_real = br * tw_cos - bi * tw_sin
     turned_imag = bi * tw_cos + br * tw_sin
     stacked = jnp.concatenate([turned_real, turned_imag], axis=0).reshape(2 * rows, chans * cols)
-    out = jnp.dot(last, stacked, precision=HIGH).reshape(rows // 2, chans, cols)
-    return out.transpose(0, 2, 1).reshape(rows // 2 * cols, chans)
+    return jnp.dot(last, stacked, precision=HIGH).reshape(rows // 2, chans, cols)
+
+
+def shift_back(grid, steps):
+    prev = jnp.concatenate([jnp.zeros_like(grid[:, :1]), grid[:, :-1]], axis=1)
+    cols = grid.shape[3]
+    return jnp.concatenate([prev[..., cols - steps :], grid[..., : cols - steps]], axis=3)
 
 
 def on_device(
@@ -67,26 +71,30 @@
 ):
     seq_count = lax.axis_size("seq")
     place = lax.axis_index("seq")
+    shard_len, local_chans = query_projected.shape
+    chans = local_chans // seq_count
+    tables = dft_tables(seq_count * shard_len)
+    cols = tables[1]
+    blocks = shard_len // cols
     streams = jnp.stack([query_projected, key_stream, value_stream])
-    full = lax.all_to_all(streams, "seq", 2, 1, tiled=True)
-    filt = lax.all_to_all(long_filter, "seq", 1, 0, tiled=True)
-    chans = full.shape[2]
-    seq_len = full.shape[1]
+    streams = streams.reshape(3, blocks, cols, seq_count, chans).transpose(3, 0, 1, 4, 2)
+    full = lax.all_to_all(streams, "seq", 0, 0, tiled=True)
+    full = full.transpose(1, 0, 2, 3, 4).reshape(3, seq_count * blocks, chans, cols)
+    filt = long_filter.reshape(blocks, cols, seq_count, chans).transpose(2, 0, 3, 1)
+    filt = lax.all_to_all(filt, "seq", 0, 0, tiled=True).reshape(seq_count * blocks, chans, cols)
     taps = lax.dynamic_slice_in_dim(short_taps, place * chans, chans, axis=2)
     gain = lax.dynamic_slice_in_dim(skip_gain, place * chans, chans, axis=0)
     x = full.astype(jnp.float32)
-    zeros = jnp.zeros_like(x[:, :2])
-    extended = jnp.concatenate([zeros, x], axis=1)
     shaped = (
-        taps[0][:, None, :] * extended[:, 2:]
-        + taps[1][:, None, :] * extended[:, 1:-1]
-        + taps[2][:, None, :] * extended[:, :-2]
+        taps[0][:, None, :, None] * x
+        + taps[1][:, None, :, None] * shift_back(x, 1)
+        + taps[2][:, None, :, None] * shift_back(x, 2)
     )
     source = shaped[1] * shaped[2]
-    tables = dft_tables(seq_len)
     convolved = causal_conv(source, filt, tables)
-    gated = (shaped[0] * (convolved + gain[None, :] * source)).astype(jnp.bfloat16)
-    gated = lax.all_to_all(gated, "seq", 0, 1, tiled=True)
+    gated = (shaped[0] * (convolved + gain[None, :, None] * source)).astype(jnp.bfloat16)
+    gated = lax.all_to_all(gated.reshape(seq_count, blocks, chans, cols), "seq", 0, 0, tiled=True)
+    gated = gated.transpose(1, 3, 0, 2).reshape(shard_len, local_chans)
     terms = jnp.dot(gated, out_weight, preferred_element_type=jnp.float32)
     return lax.psum(terms, "chan").astype(jnp.bfloat16)
 

time: 130 us -> 125 us (0.962)
  waiting for transfers between devices: 22.8 us -> 17.8 us
  matrix products: 12.2 us -> 10.1 us
  other arithmetic: 3.08 us -> 4.59 us
    all_to_all x2, waiting for transfers between devices: 22.8 us -> 17.8 us  [the longest x1 9.8 us: on_device(): full = lax.all_to_all(streams, 'seq', 0, 0, tiled=True)]
    dot_general x1, matrix products: 5.43 us -> 3.28 us  [on_device(): terms = jnp.dot(gated, out_weight, preferred_element_type=jnp.float32)]
    transpose x0 -> x2, local copies, waits for them, and re-layouts: none -> 1.8 us  [the longest x1 1.56 us: on_device(): streams.reshape(3, blocks, cols, seq_count, chans).transpose(3, 0, 1, 4, 2)]
    unnamed x30 -> x31, local copies, waits for them, and re-layouts: 6.11 us -> 4.57 us
    transpose x0 -> x1, other arithmetic: none -> 1.31 us  [on_device(): streams.reshape(3, blocks, cols, seq_count, chans).transpose(3, 0, 1, 4, 2)]
  transfers between devices with their start and end apart: 2 -> 2, of which waited for: 2 -> 2; matrix products, arithmetic and copies ran while one was open for 4% -> 5% of each run, Pallas kernels for 0% -> 0%
where the time goes in v5:
time: 125 us; the launch traced here: 124 us
  blocking collectives  69.3 us (55%)
  waiting for transfers between devices  17.8 us (14%)
  starting transfers between devices  12 us (10%)
  local copies, waits for them, and re-layouts  10.3 us (8%)
  matrix products  10.1 us (8%)
  other arithmetic  4.59 us (4%)
    psum x1, blocking collectives, on_device(): return lax.psum(terms, 'chan').astype(jnp.bfloat16)  57.5 us
    all_to_all x1, blocking collectives, on_device(): lax.all_to_all(gated.reshape(seq_count, blocks, chans, cols), 'seq', 0, 0...  11.8 us
    all_to_all x1, waiting for transfers between devices, on_device(): full = lax.all_to_all(streams, 'seq', 0, 0, tiled=True)  9.8 us
    all_to_all x1, starting transfers between devices, on_device(): lax.all_to_all(filt, 'seq', 0, 0, tiled=True)  8.16 us
    all_to_all x1, waiting for transfers between devices, on_device(): lax.all_to_all(filt, 'seq', 0, 0, tiled=True)  7.98 us
    unnamed x31, local copies, waits for them, and re-layouts  4.57 us
    all_to_all x1, starting transfers between devices, on_device(): full = lax.all_to_all(streams, 'seq', 0, 0, tiled=True)  3.8 us
    dot_general x1, matrix products, on_device(): terms = jnp.dot(gated, out_weight, preferred_element_type=jnp.float32)  3.28 us
  transfers between devices with their start and end apart: 2, of which 2 were waited for; matrix products, arithmetic and copies ran while one was open for 5% of the time, Pallas kernels for 0%

profile of v5, /device:TPU:0, one launch (start us, length us, event | category | flops | bytes accessed | tf_op | source)
XLA Modules:
  0.0 124.4 jit_solution(15605803076657802490)
XLA Ops:
  0.0 1.3 %copy.38 = f32[256,512]{0,1:T(8,128)S(1)} copy(f32[256,512]{1,0:T(8,128)} %param.18) | data formatting | bytes 1048576 | tf_op args[5]
  1.3 1.1 reshape.90
  2.4 8.2 %all-to-all-start.1 = ((f32[16,2,32,128]{3,1,2,0:T(2,128)}), f32[16,2,32,128]{3,1,2,0:T(2,128)S(1)}, u32[]{:S(2)}, u32[]{:S(2)}) async-start(f32[16,2,32,128]{3,1,2,0:T(2,128)} %bitcast.9), calls=%async_computation.1 | async-start | bytes 1048576 | tf_op jit(solution)/shard_map/all_to_all | solution.py:84
  11.2 1.3 %maximum_bitcast_fusion = bf16[16,3,2,32,128]{4,2,3,0,1:T(2,128)(2,1)S(1)} fusion(bf16[1,2,128,16,32]{2,1,4,3,0:T(2,128)(2,1)S(1)} %stack.14, bf16[1,2,128,16,32]{2,1,4,3,0:T(2,128)(2,1)S(1)} %stack.13, bf16[1,2,128,16,32]{2,1,4,3,0:T(2,128)(2,1)S(1)} %stack.12), kind=kLoop, calls=%fused_computation.43 | loop fusion | flops 786432 | bytes 1572864 | tf_op jit(solution)/shard_map/transpose | solution.py:80
  12.6 1.6 %copy.36 = bf16[16,3,2,32,128]{4,2,3,1,0:T(2,128)(2,1)} copy(bf16[16,3,2,32,128]{4,2,3,0,1:T(2,128)(2,1)S(1)} %maximum_bitcast_fusion) | data formatting | bytes 1572864 | tf_op jit(solution)/shard_map/transpose | solution.py:80
  14.1 8.0 %all-to-all-done.1 = f32[16,2,32,128]{3,1,2,0:T(2,128)S(1)} async-done(((f32[16,2,32,128]{3,1,2,0:T(2,128)}), f32[16,2,32,128]{3,1,2,0:T(2,128)S(1)}, u32[]{:S(2)}, u32[]{:S(2)}) %all-to-all-start.1) | async-done | bytes 524320 | tf_op jit(solution)/shard_map/all_to_all | solution.py:84
  22.1 3.8 %all-to-all-start = ((bf16[16,3,2,32,128]{4,2,3,1,0:T(2,128)(2,1)}), bf16[16,3,2,32,128]{4,2,3,1,0:T(2,128)(2,1)S(1)}, u32[]{:S(2)}, u32[]{:S(2)}) async-start(bf16[16,3,2,32,128]{4,2,3,1,0:T(2,128)(2,1)} %copy.36), calls=%async_computation | async-start | bytes 1572864 | tf_op jit(solution)/shard_map/all_to_all | solution.py:81
  25.9 0.8 dynamic_slice.7
  26.7 0.8 dynamic-slice_bitcast_fusion.2
  27.5 1.0 fusion.24
  28.8 0.2 copy.45
  29.1 9.8 %all-to-all-done = bf16[16,3,2,32,128]{4,2,3,1,0:T(2,128)(2,1)S(1)} async-done(((bf16[16,3,2,32,128]{4,2,3,1,0:T(2,128)(2,1)}), bf16[16,3,2,32,128]{4,2,3,1,0:T(2,128)(2,1)S(1)}, u32[]{:S(2)}, u32[]{:S(2)}) %all-to-all-start) | async-done | bytes 786464 | tf_op jit(solution)/shard_map/all_to_all | solution.py:81
  38.9 0.2 copy_convert_fusion
  39.3 0.5 pad_slice_fusion
  39.8 0.5 pad_slice_fusion.1
  40.2 1.1 fusion.16
  41.5 1.0 fusion.27
  43.1 0.3 copy-done.7
  43.5 0.8 fusion.22
  44.4 1.0 fusion.3
  45.5 1.0 fusion.7
  46.5 0.3 multiply_subtract_fusion.1
  46.8 0.6 copy-done.2
  47.4 1.0 fusion.11
  48.5 0.3 multiply_subtract_fusion
  49.0 0.5 copy-done.9
  49.5 1.7 %fusion.17 = f32[4,8,32,128]{3,1,2,0:T(8,128)S(1)} fusion(f32[32,128]{1,0:T(8,128)S(1)} %copy-done.9, f32[16,8,32,128]{3,2,1,0:T(8,128)S(1)} %bitcast.101), kind=kOutput, calls=%fused_computation.22 | convolution fusion | flops 100663296 | bytes 2637824 | tf_op jit(solution)/shard_map/dot_general | solution.py:60
  51.4 0.2 multiply_convert_fusion
  51.6 11.8 %all_to_all.15 = bf16[16,2,32,128]{3,2,1,0:T(8,128)(2,1)S(1)} all-to-all(bf16[16,2,32,128]{3,2,1,0:T(8,128)(2,1)S(1)} %multiply_convert_fusion), channel_id=1, replica_groups=mesh['seq'=16,'chan'=8] {'seq'}, dimensions={0} | all-to-all | bytes 524288 | tf_op jit(solution)/shard_map/all_to_all | solution.py:96
  63.3 0.2 copy.40
  63.6 3.3 %fusion.30 = f32[256,4096]{1,0:T(8,128)} fusion(bf16[512,4096]{1,0:T(8,128)(2,1)S(1)} %copy-done, bf16[64,8,2,128]{3,2,1,0:T(2,128)(2,1)S(1)} %bitcast.107), kind=kOutput, calls=%fused_computation.53 | convolution fusion | flops 1073741824 | bytes 8650752 | tf_op jit(solution)/shard_map/dot_general | solution.py:98
  66.9 57.5 %all-reduce.2 = bf16[256,4096]{1,0:T(8,128)(2,1)} all-reduce(f32[256,4096]{1,0:T(8,128)} %fusion.30), channel_id=1, replica_groups=mesh['seq'=16,'chan'=8] {'chan'}, use_global_device_ids=true, to_apply=%region_0.0 | all-reduce | flops 1048576 | bytes 6291456 | tf_op jit(solution)/shard_map/psum | solution.py:99
  (33 shorter events, 2.3 us)
Async XLA Ops:
  0.0 10.6 %copy-start.3 = (bf16[256,512]{1,0:T(8,128)(2,1)S(1)}, bf16[256,512]{1,0:T(8,128)(2,1)}, u32[]{:S(2)}) copy-start(bf16[256,512]{1,0:T(8,128)(2,1)} %param.13) | copy-start | bytes 786436
  0.0 10.8 %copy-start.4 = (bf16[256,512]{1,0:T(8,128)(2,1)S(1)}, bf16[256,512]{1,0:T(8,128)(2,1)}, u32[]{:S(2)}) copy-start(bf16[256,512]{1,0:T(8,128)(2,1)} %param.14) | copy-start | bytes 786436
  1.3 9.7 %copy-start.5 = (bf16[256,512]{1,0:T(8,128)(2,1)S(1)}, bf16[256,512]{1,0:T(8,128)(2,1)}, u32[]{:S(2)}) copy-start(bf16[256,512]{1,0:T(8,128)(2,1)} %param.15) | copy-start | bytes 786436
  2.4 19.7 %all-to-all-start.1 = ((f32[16,2,32,128]{3,1,2,0:T(2,128)}), f32[16,2,32,128]{3,1,2,0:T(2,128)S(1)}, u32[]{:S(2)}, u32[]{:S(2)}) async-start(f32[16,2,32,128]{3,1,2,0:T(2,128)} %bitcast.9), calls=%async_computation.1 | async-start | bytes 1048576 | tf_op jit(solution)/shard_map/all_to_all | solution.py:84
  12.5 15.0 %copy-start.6 = (f32[128,32]{1,0:T(8,128)S(1)}, f32[128,32]{1,0:T(8,128)}, u32[]{:S(2)}) copy-start(f32[128,32]{1,0:T(8,128)} %constant.26.clone) | copy-start | bytes 49156
  22.1 16.9 %all-to-all-start = ((bf16[16,3,2,32,128]{4,2,3,1,0:T(2,128)(2,1)}), bf16[16,3,2,32,128]{4,2,3,1,0:T(2,128)(2,1)S(1)}, u32[]{:S(2)}, u32[]{:S(2)}) async-start(bf16[16,3,2,32,128]{4,2,3,1,0:T(2,128)(2,1)} %copy.36), calls=%async_computation | async-start | bytes 1572864 | tf_op jit(solution)/shard_map/all_to_all | solution.py:81
  42.7 0.8 copy-start.7
  42.7 0.8 copy-start.8
  43.5 0.9 copy-start.1
  46.5 1.0 copy-start.2
  48.8 0.7 copy-start.9
  49.5 14.1 %copy-start = (bf16[512,4096]{1,0:T(8,128)(2,1)S(1)}, bf16[512,4096]{1,0:T(8,128)(2,1)}, u32[]{:S(2)}) copy-start(bf16[512,4096]{1,0:T(8,128)(2,1)} %param.19) | copy-start | bytes 12582916

commit v6 on v5

--- a/solution.py
+++ b/solution.py
@@ -78,10 +78,16 @@
     blocks = shard_len // cols
     streams = jnp.stack([query_projected, key_stream, value_stream])
     streams = streams.reshape(3, blocks, cols, seq_count, chans).transpose(3, 0, 1, 4, 2)
-    full = lax.all_to_all(streams, "seq", 0, 0, tiled=True)
-    full = full.transpose(1, 0, 2, 3, 4).reshape(3, seq_count * blocks, chans, cols)
     filt = long_filter.reshape(blocks, cols, seq_count, chans).transpose(2, 0, 3, 1)
-    filt = lax.all_to_all(filt, "seq", 0, 0, tiled=True).reshape(seq_count * blocks, chans, cols)
+    high = filt.astype(jnp.bfloat16)
+    rest = filt - high.astype(jnp.float32)
+    mid = rest.astype(jnp.bfloat16)
+    low = (rest - mid.astype(jnp.float32)).astype(jnp.bfloat16)
+    planes = jnp.concatenate([streams, jnp.stack([high, mid, low], axis=1)], axis=1)
+    planes = lax.all_to_all(planes, "seq", 0, 0, tiled=True)
+    full = planes[:, :3].transpose(1, 0, 2, 3, 4).reshape(3, seq_count * blocks, chans, cols)
+    parts = planes[:, 3:].astype(jnp.float32)
+    filt = ((parts[:, 0] + parts[:, 1]) + parts[:, 2]).reshape(seq_count * blocks, chans, cols)
     taps = lax.dynamic_slice_in_dim(short_taps, place * chans, chans, axis=2)
     gain = lax.dynamic_slice_in_dim(skip_gain, place * chans, chans, axis=0)
     x = full.astype(jnp.float32)

time: 125 us -> 138 us (1.10)
  other arithmetic: 4.59 us -> 14.5 us
  waiting for transfers between devices: 17.8 us -> 22.8 us
  starting transfers between devices: 12 us -> 8.34 us
    concatenate x0 -> x1, other arithmetic: none -> 7.58 us  [on_device(): jnp.concatenate([streams, jnp.stack([high, mid, low], axis=1)], axis=1)]
    all_to_all x2 -> x1, waiting for transfers between devices: 17.8 us -> 22.8 us  [on_device(): planes = lax.all_to_all(planes, 'seq', 0, 0, tiled=True)]
    all_to_all x2 -> x1, starting transfers between devices: 12 us -> 8.34 us  [on_device(): planes = lax.all_to_all(planes, 'seq', 0, 0, tiled=True)]
    concatenate x0 -> x1, local copies, waits for them, and re-layouts: none -> 3.09 us  [on_device(): jnp.concatenate([streams, jnp.stack([high, mid, low], axis=1)], axis=1)]
    transpose x1 -> x0, local copies, waits for them, and re-layouts: 1.56 us -> none  [on_device(): streams.reshape(3, blocks, cols, seq_count, chans).transpose(3, 0, 1, 4, 2)]
  transfers between devices with their start and end apart: 2 -> 1, of which waited for: 2 -> 1; matrix products, arithmetic and copies ran while one was open for 5% -> 1% of each run, Pallas kernels for 0% -> 0%
where the time goes in v6:
time: 138 us; the launch traced here: 137 us
  blocking collectives  69.4 us (50%)
  waiting for transfers between devices  22.8 us (17%)
  other arithmetic  14.5 us (11%)
  local copies, waits for them, and re-layouts  11.6 us (8%)
  matrix products  10.4 us (8%)
  starting transfers between devices  8.34 us (6%)
    psum x1, blocking collectives, on_device(): return lax.psum(terms, 'chan').astype(jnp.bfloat16)  57.9 us
    all_to_all x1, waiting for transfers between devices, on_device(): planes = lax.all_to_all(planes, 'seq', 0, 0, tiled=True)  22.8 us
    all_to_all x1, blocking collectives, on_device(): lax.all_to_all(gated.reshape(seq_count, blocks, chans, cols), 'seq', 0, 0...  11.5 us
    all_to_all x1, starting transfers between devices, on_device(): planes = lax.all_to_all(planes, 'seq', 0, 0, tiled=True)  8.34 us
    concatenate x1, other arithmetic, on_device(): jnp.concatenate([streams, jnp.stack([high, mid, low], axis=1)], axis=1)  7.58 us
    unnamed x31, local copies, waits for them, and re-layouts  5.14 us
    dot_general x1, matrix products, on_device(): terms = jnp.dot(gated, out_weight, preferred_element_type=jnp.float32)  3.28 us
    concatenate x1, local copies, waits for them, and re-layouts, on_device(): jnp.concatenate([streams, jnp.stack([high, mid, low], axis=1)], axis=1)  3.09 us
  transfers between devices with their start and end apart: 1, of which 1 were waited for; matrix products, arithmetic and copies ran while one was open for 1% of the time, Pallas kernels for 0%

profile of v6, /device:TPU:0, one launch (start us, length us, event | category | flops | bytes accessed | tf_op | source)
XLA Modules:
  0.0 137.4 jit_solution(1431655882935162259)
XLA Ops:
  0.0 1.2 copy.36
  1.3 0.3 reshape.95
  1.8 0.5 fusion.32
  3.0 1.3 maximum_bitcast_fusion
  4.3 7.6 %pad_maximum_fusion.1 = bf16[16,6,2,32,128]{4,2,3,0,1:T(2,128)(2,1)S(1)} fusion(bf16[16,1,2,32,128]{4,2,3,0,1:T(2,128)(2,1)S(1)} %get-tuple-element.22, bf16[16,1,2,32,128]{4,2,3,0,1:T(2,128)(2,1)S(1)} %get-tuple-element.21, bf16[16,1,2,32,128]{4,2,3,0,1:T(2,128)(2,1)S(1)} %fusion.31, bf16[16,3,2,32,128]{4,2,3,0,1:T(2,128)(2,1)S(1)} %maximum_bitcast_fusion), kind=kLoop, calls=%fused_computation.16 | loop fusion | flops 2359296 | bytes 3145728 | tf_op jit(solution)/shard_map/concatenate | solution.py:86
  11.9 3.1 %copy.37 = bf16[16,6,2,32,128]{4,2,3,1,0:T(2,128)(2,1)} copy(bf16[16,6,2,32,128]{4,2,3,0,1:T(2,128)(2,1)S(1)} %pad_maximum_fusion.1) | data formatting | bytes 3145728 | tf_op jit(solution)/shard_map/concatenate | solution.py:86
  15.0 8.3 %all-to-all-start = ((bf16[16,6,2,32,128]{4,2,3,1,0:T(2,128)(2,1)}), bf16[16,6,2,32,128]{4,2,3,1,0:T(2,128)(2,1)S(1)}, u32[]{:S(2)}, u32[]{:S(2)}) async-start(bf16[16,6,2,32,128]{4,2,3,1,0:T(2,128)(2,1)} %copy.37), calls=%async_computation | async-start | bytes 3145728 | tf_op jit(solution)/shard_map/all_to_all | solution.py:87
  23.3 0.8 dynamic_slice.7
  24.1 0.8 dynamic-slice_bitcast_fusion.2
  24.9 22.8 %all-to-all-done = bf16[16,6,2,32,128]{4,2,3,1,0:T(2,128)(2,1)S(1)} async-done(((bf16[16,6,2,32,128]{4,2,3,1,0:T(2,128)(2,1)}), bf16[16,6,2,32,128]{4,2,3,1,0:T(2,128)(2,1)S(1)}, u32[]{:S(2)}, u32[]{:S(2)}) %all-to-all-start) | async-done | bytes 1572896 | tf_op jit(solution)/shard_map/all_to_all | solution.py:87
  47.7 1.3 slice_convert_fusion
  49.3 0.5 pad_slice_fusion
  49.8 0.5 pad_slice_fusion.1
  50.2 0.4 slice_add_fusion
  50.7 0.3 copy-done.6
  51.1 1.0 fusion.24
  52.7 1.1 fusion.16
  53.9 1.0 fusion.27
  55.6 0.5 copy-done.7
  56.1 0.8 fusion.22
  57.1 1.0 fusion.3
  58.1 1.0 fusion.7
  59.1 0.3 multiply_subtract_fusion.1
  59.5 0.6 copy-done.2
  60.1 1.0 fusion.11
  61.1 0.3 multiply_subtract_fusion
  61.6 0.5 copy-done.9
  62.2 1.9 %fusion.17 = f32[4,8,32,128]{3,1,2,0:T(8,128)S(1)} fusion(f32[32,128]{1,0:T(8,128)S(1)} %copy-done.9, f32[16,8,32,128]{3,2,1,0:T(8,128)S(1)} %bitcast.126), kind=kOutput, calls=%fused_computation.23 | convolution fusion | flops 100663296 | bytes 2637824 | tf_op jit(solution)/shard_map/dot_general | solution.py:60
  64.4 11.5 %all_to_all.10 = bf16[16,2,32,128]{3,2,1,0:T(8,128)(2,1)S(1)} all-to-all(bf16[16,2,32,128]{3,2,1,0:T(8,128)(2,1)S(1)} %multiply_convert_fusion), channel_id=1, replica_groups=mesh['seq'=16,'chan'=8] {'seq'}, dimensions={0} | all-to-all | bytes 524288 | tf_op jit(solution)/shard_map/all_to_all | solution.py:102
  75.9 0.2 copy.40
  76.2 3.3 %fusion.33 = f32[256,4096]{1,0:T(8,128)} fusion(bf16[512,4096]{1,0:T(8,128)(2,1)S(1)} %copy-done, bf16[64,8,2,128]{3,2,1,0:T(2,128)(2,1)S(1)} %bitcast.132), kind=kOutput, calls=%fused_computation.63 | convolution fusion | flops 1073741824 | bytes 8650752 | tf_op jit(solution)/shard_map/dot_general | solution.py:104
  79.5 57.9 %all-reduce.2 = bf16[256,4096]{1,0:T(8,128)(2,1)} all-reduce(f32[256,4096]{1,0:T(8,128)} %fusion.33), channel_id=1, replica_groups=mesh['seq'=16,'chan'=8] {'chan'}, use_global_device_ids=true, to_apply=%region_0.0 | all-reduce | flops 1048576 | bytes 6291456 | tf_op jit(solution)/shard_map/psum | solution.py:105
  (36 shorter events, 3.2 us)
Async XLA Ops:
  1.2 1.1 copy-start.3
  1.5 1.0 copy-start.4
  1.8 1.0 copy-start.5
  15.0 32.7 %all-to-all-start = ((bf16[16,6,2,32,128]{4,2,3,1,0:T(2,128)(2,1)}), bf16[16,6,2,32,128]{4,2,3,1,0:T(2,128)(2,1)S(1)}, u32[]{:S(2)}, u32[]{:S(2)}) async-start(bf16[16,6,2,32,128]{4,2,3,1,0:T(2,128)(2,1)} %copy.37), calls=%async_computation | async-start | bytes 3145728 | tf_op jit(solution)/shard_map/all_to_all | solution.py:87
  50.2 0.8 copy-start.6
  55.4 0.8 copy-start.7
  55.4 0.8 copy-start.8
  56.1 0.9 copy-start.1
  59.1 1.0 copy-start.2
  61.4 0.7 copy-start.9
  62.2 14.0 %copy-start = (bf16[512,4096]{1,0:T(8,128)(2,1)S(1)}, bf16[512,4096]{1,0:T(8,128)(2,1)}, u32[]{:S(2)}) copy-start(bf16[512,4096]{1,0:T(8,128)(2,1)} %param.19) | copy-start | bytes 12582916

commit v7 on v5

--- a/solution.py
+++ b/solution.py
@@ -93,10 +93,16 @@
     source = shaped[1] * shaped[2]
     convolved = causal_conv(source, filt, tables)
     gated = (shaped[0] * (convolved + gain[None, :, None] * source)).astype(jnp.bfloat16)
-    gated = lax.all_to_all(gated.reshape(seq_count, blocks, chans, cols), "seq", 0, 0, tiled=True)
-    gated = gated.transpose(1, 3, 0, 2).reshape(shard_len, local_chans)
-    terms = jnp.dot(gated, out_weight, preferred_element_type=jnp.float32)
-    return lax.psum(terms, "chan").astype(jnp.bfloat16)
+    gated = gated.reshape(seq_count, blocks, chans, cols)
+    halves = []
+    for half in range(blocks):
+        back = lax.all_to_all(gated[:, half], "seq", 0, 0, tiled=True)
+        back = back.transpose(2, 0, 1).reshape(cols, local_chans)
+        terms = jnp.dot(back, out_weight, preferred_element_type=jnp.float32)
+        if halves:
+            halves[-1], terms = lax.optimization_barrier((halves[-1], terms))
+        halves.append(lax.psum(terms, "chan").astype(jnp.bfloat16))
+    return jnp.concatenate(halves, axis=0)
 
 
 def solution(mesh):

time: 125 us -> 184 us (1.47)
  blocking collectives: 69.3 us -> 118 us
  starting transfers between devices: 12 us -> 15.5 us
  other arithmetic: 4.59 us -> 7.53 us
  matrix products: 10.1 us -> 12.7 us
    psum x1 -> x2, blocking collectives: 57.5 us -> 107 us  [on_device(): halves.append(lax.psum(terms, 'chan').astype(jnp.bfloat16))]
    all_to_all x0 -> x1, starting transfers between devices: none -> 3.51 us  [on_device(): back = lax.all_to_all(gated[:, half], 'seq', 0, 0, tiled=True)]
    concatenate x0 -> x1, other arithmetic: none -> 2.73 us  [on_device(): return jnp.concatenate(halves, axis=0)]
    dot_general x1 -> x2, matrix products: 3.28 us -> 5.87 us  [on_device(): terms = jnp.dot(back, out_weight, preferred_element_type=jnp.float32)]
    unnamed x31 -> x29, local copies, waits for them, and re-layouts: 4.57 us -> 4.57 us
  transfers between devices with their start and end apart: 2 -> 3, of which waited for: 2 -> 2; matrix products, arithmetic and copies ran while one was open for 5% -> 5% of each run, Pallas kernels for 0% -> 0%
where the time goes in v7:
time: 184 us; the launch traced here: 183 us
  blocking collectives  118 us (64%)
  waiting for transfers between devices  17.8 us (10%)
  starting transfers between devices  15.5 us (8%)
  matrix products  12.7 us (7%)
  local copies, waits for them, and re-layouts  10.7 us (6%)
  other arithmetic  7.53 us (4%)
    psum x2, blocking collectives, on_device(): halves.append(lax.psum(terms, 'chan').astype(jnp.bfloat16))  107 us
    all_to_all x1, blocking collectives, on_device(): back = lax.all_to_all(gated[:, half], 'seq', 0, 0, tiled=True)  11 us
    all_to_all x1, waiting for transfers between devices, on_device(): full = lax.all_to_all(streams, 'seq', 0, 0, tiled=True)  9.8 us
    all_to_all x1, starting transfers between devices, on_device(): lax.all_to_all(filt, 'seq', 0, 0, tiled=True)  8.16 us
    all_to_all x1, waiting for transfers between devices, on_device(): lax.all_to_all(filt, 'seq', 0, 0, tiled=True)  7.98 us
    dot_general x2, matrix products, on_device(): terms = jnp.dot(back, out_weight, preferred_element_type=jnp.float32)  5.87 us
    unnamed x29, local copies, waits for them, and re-layouts  4.57 us
    all_to_all x1, starting transfers between devices, on_device(): full = lax.all_to_all(streams, 'seq', 0, 0, tiled=True)  3.8 us
  transfers between devices with their start and end apart: 3, of which 2 were waited for; matrix products, arithmetic and copies ran while one was open for 5% of the time, Pallas kernels for 0%

profile of v7, /device:TPU:0, one launch (start us, length us, event | category | flops | bytes accessed | tf_op | source)
XLA Modules:
  0.0 183.0 jit_solution(16853990575302265507)
XLA Ops:
  0.0 1.3 copy.25
  1.3 1.0 reshape.93
  2.4 8.2 %all-to-all-start.1 = ((f32[16,2,32,128]{3,1,2,0:T(2,128)}), f32[16,2,32,128]{3,1,2,0:T(2,128)S(1)}, u32[]{:S(2)}, u32[]{:S(2)}) async-start(f32[16,2,32,128]{3,1,2,0:T(2,128)} %bitcast.9), calls=%async_computation.1 | async-start | bytes 1048576 | tf_op jit(solution)/shard_map/all_to_all | solution.py:84
  11.2 1.3 maximum_bitcast_fusion
  12.5 1.6 copy.23
  14.1 8.0 %all-to-all-done.1 = f32[16,2,32,128]{3,1,2,0:T(2,128)S(1)} async-done(((f32[16,2,32,128]{3,1,2,0:T(2,128)}), f32[16,2,32,128]{3,1,2,0:T(2,128)S(1)}, u32[]{:S(2)}, u32[]{:S(2)}) %all-to-all-start.1) | async-done | bytes 524320 | tf_op jit(solution)/shard_map/all_to_all | solution.py:84
  22.1 3.8 %all-to-all-start = ((bf16[16,3,2,32,128]{4,2,3,1,0:T(2,128)(2,1)}), bf16[16,3,2,32,128]{4,2,3,1,0:T(2,128)(2,1)S(1)}, u32[]{:S(2)}, u32[]{:S(2)}) async-start(bf16[16,3,2,32,128]{4,2,3,1,0:T(2,128)(2,1)} %copy.23), calls=%async_computation | async-start | bytes 1572864 | tf_op jit(solution)/shard_map/all_to_all | solution.py:81
  25.9 0.8 dynamic_slice.7
  26.6 0.8 dynamic-slice_bitcast_fusion.2
  27.5 1.0 fusion.24
  29.1 9.8 %all-to-all-done = bf16[16,3,2,32,128]{4,2,3,1,0:T(2,128)(2,1)S(1)} async-done(((bf16[16,3,2,32,128]{4,2,3,1,0:T(2,128)(2,1)}), bf16[16,3,2,32,128]{4,2,3,1,0:T(2,128)(2,1)S(1)}, u32[]{:S(2)}, u32[]{:S(2)}) %all-to-all-start) | async-done | bytes 786464 | tf_op jit(solution)/shard_map/all_to_all | solution.py:81
  39.3 0.5 pad_slice_fusion
  39.8 0.5 pad_slice_fusion.1
  40.2 1.1 fusion.16
  41.4 1.0 fusion.27
  43.1 0.3 copy-done.6
  43.5 0.8 fusion.22
  44.4 1.0 fusion.3
  45.4 1.0 fusion.7
  46.8 0.6 copy-done.1
  47.4 1.0 fusion.11
  49.0 0.5 copy-done.8
  49.5 1.7 fusion.17
  51.3 0.4 multiply_convert_fusion
  51.8 0.7 slice_bitcast_fusion.4
  52.4 11.0 %all_to_all.20 = bf16[16,32,128]{2,1,0:T(8,128)(2,1)S(1)} all-to-all(bf16[16,32,128]{2,1,0:T(8,128)(2,1)S(1)} %get-tuple-element.24), channel_id=1, replica_groups=mesh['seq'=16,'chan'=8] {'seq'}, dimensions={0} | all-to-all | bytes 262144 | tf_op jit(solution)/shard_map/all_to_all | solution.py:99
  63.5 3.5 %all-to-all-start.3 = ((bf16[16,32,128]{2,1,0:T(8,128)(2,1)}), bf16[16,32,128]{2,1,0:T(8,128)(2,1)S(1)}, u32[]{:S(2)}, u32[]{:S(2)}) async-start(bf16[16,32,128]{2,1,0:T(8,128)(2,1)} %get-tuple-element.23), calls=%async_computation.3 | async-start | bytes 262144 | tf_op jit(solution)/shard_map/all_to_all | solution.py:99
  67.0 2.9 %fusion.33 = f32[128,4096]{1,0:T(8,128)S(1)} fusion(bf16[128,512]{0,1:T(8,128)(2,1)S(1)} %bitcast.113, bf16[512,4096]{1,0:T(8,128)(2,1)} %param.19), kind=kOutput, calls=%fused_computation.62 | convolution fusion | flops 536870912 | bytes 6422528 | tf_op jit(solution)/shard_map/dot_general | solution.py:101
  69.9 52.4 %all-reduce.3 = bf16[128,4096]{1,0:T(8,128)(2,1)S(1)} all-reduce(f32[128,4096]{1,0:T(8,128)S(1)} %fusion.33), channel_id=1, replica_groups=mesh['seq'=16,'chan'=8] {'chan'}, use_global_device_ids=true, to_apply=%region_0.0 | all-reduce | flops 524288 | bytes 3145728 | tf_op jit(solution)/shard_map/psum | solution.py:104
  122.3 2.9 %fusion.34 = f32[128,4096]{1,0:T(8,128)S(1)} fusion(bf16[128,512]{0,1:T(8,128)(2,1)S(1)} %bitcast.112, bf16[512,4096]{1,0:T(8,128)(2,1)} %param.19), kind=kOutput, calls=%fused_computation.63 | convolution fusion | flops 536870912 | bytes 6422528 | tf_op jit(solution)/shard_map/dot_general | solution.py:101
  125.3 55.1 %all-reduce.4 = bf16[128,4096]{1,0:T(8,128)(2,1)} all-reduce(f32[128,4096]{1,0:T(8,128)S(1)} %fusion.34), channel_id=1, replica_groups=mesh['seq'=16,'chan'=8] {'chan'}, use_global_device_ids=true, to_apply=%region_1.0 | all-reduce | flops 524288 | bytes 3145728 | tf_op jit(solution)/shard_map/psum | solution.py:104
  180.3 2.7 %pad_maximum_fusion.1 = bf16[256,4096]{1,0:T(8,128)(2,1)} fusion(bf16[128,4096]{1,0:T(8,128)(2,1)} %all-reduce.4, bf16[128,4096]{1,0:T(8,128)(2,1)S(1)} %all-reduce.3), kind=kLoop, calls=%fused_computation.16 | loop fusion | flops 4194304 | bytes 4194304 | tf_op jit(solution)/shard_map/concatenate | solution.py:105
  (36 shorter events, 3.4 us)
Async XLA Ops:
  0.0 10.5 %copy-start.2 = (bf16[256,512]{1,0:T(8,128)(2,1)S(1)}, bf16[256,512]{1,0:T(8,128)(2,1)}, u32[]{:S(2)}) copy-start(bf16[256,512]{1,0:T(8,128)(2,1)} %param.13) | copy-start | bytes 786436
  0.0 10.8 %copy-start.3 = (bf16[256,512]{1,0:T(8,128)(2,1)S(1)}, bf16[256,512]{1,0:T(8,128)(2,1)}, u32[]{:S(2)}) copy-start(bf16[256,512]{1,0:T(8,128)(2,1)} %param.14) | copy-start | bytes 786436
  1.3 9.7 %copy-start.4 = (bf16[256,512]{1,0:T(8,128)(2,1)S(1)}, bf16[256,512]{1,0:T(8,128)(2,1)}, u32[]{:S(2)}) copy-start(bf16[256,512]{1,0:T(8,128)(2,1)} %param.15) | copy-start | bytes 786436
  2.4 19.7 %all-to-all-start.1 = ((f32[16,2,32,128]{3,1,2,0:T(2,128)}), f32[16,2,32,128]{3,1,2,0:T(2,128)S(1)}, u32[]{:S(2)}, u32[]{:S(2)}) async-start(f32[16,2,32,128]{3,1,2,0:T(2,128)} %bitcast.9), calls=%async_computation.1 | async-start | bytes 1048576 | tf_op jit(solution)/shard_map/all_to_all | solution.py:84
  12.5 15.0 %copy-start.5 = (f32[128,32]{1,0:T(8,128)S(1)}, f32[128,32]{1,0:T(8,128)}, u32[]{:S(2)}) copy-start(f32[128,32]{1,0:T(8,128)} %constant.26.clone) | copy-start | bytes 49156
  22.1 16.9 %all-to-all-start = ((bf16[16,3,2,32,128]{4,2,3,1,0:T(2,128)(2,1)}), bf16[16,3,2,32,128]{4,2,3,1,0:T(2,128)(2,1)S(1)}, u32[]{:S(2)}, u32[]{:S(2)}) async-start(bf16[16,3,2,32,128]{4,2,3,1,0:T(2,128)(2,1)} %copy.23), calls=%async_computation | async-start | bytes 1572864 | tf_op jit(solution)/shard_map/all_to_all | solution.py:81
  42.7 0.8 copy-start.6
  42.7 0.8 copy-start.7
  43.5 0.9 copy-start
  46.4 1.0 copy-start.1
  48.8 0.7 copy-start.8
  63.5 58.8 %all-to-all-start.3 = ((bf16[16,32,128]{2,1,0:T(8,128)(2,1)}), bf16[16,32,128]{2,1,0:T(8,128)(2,1)S(1)}, u32[]{:S(2)}, u32[]{:S(2)}) async-start(bf16[16,32,128]{2,1,0:T(8,128)(2,1)} %get-tuple-element.23), calls=%async_computation.3 | async-start | bytes 262144 | tf_op jit(solution)/shard_map/all_to_all | solution.py:99

commit v8 on v5

--- a/solution.py
+++ b/solution.py
@@ -42,11 +42,10 @@
     return jnp.dot(joined, forward, precision=HIGH).reshape(rows, chans, 2 * cols)
 
 
-def causal_conv(source, long_filter, tables):
+def causal_conv(source, spec_f, tables):
     rows, cols, _, twist, _, backward, last = tables
     chans = source.shape[1]
     spec_s = spectrum(source, tables)
-    spec_f = spectrum(long_filter, tables)
     sr, si = spec_s[..., :cols], spec_s[..., cols:]
     fr, fi = spec_f[..., :cols], spec_f[..., cols:]
     prod = jnp.concatenate([sr * fr - si * fi, sr * fi + si * fr], axis=2).reshape(rows * chans, 2 * cols)
@@ -76,12 +75,15 @@
     tables = dft_tables(seq_count * shard_len)
     cols = tables[1]
     blocks = shard_len // cols
+    filt = long_filter.reshape(blocks, cols, seq_count, chans).transpose(2, 0, 3, 1)
+    filt = lax.all_to_all(filt, "seq", 0, 0, tiled=True).reshape(seq_count * blocks, chans, cols)
     streams = jnp.stack([query_projected, key_stream, value_stream])
     streams = streams.reshape(3, blocks, cols, seq_count, chans).transpose(3, 0, 1, 4, 2)
+    filt, streams = lax.optimization_barrier((filt, streams))
+    spec_f = spectrum(filt, tables)
     full = lax.all_to_all(streams, "seq", 0, 0, tiled=True)
+    spec_f, full = lax.optimization_barrier((spec_f, full))
     full = full.transpose(1, 0, 2, 3, 4).reshape(3, seq_count * blocks, chans, cols)
-    filt = long_filter.reshape(blocks, cols, seq_count, chans).transpose(2, 0, 3, 1)
-    filt = lax.all_to_all(filt, "seq", 0, 0, tiled=True).reshape(seq_count * blocks, chans, cols)
     taps = lax.dynamic_slice_in_dim(short_taps, place * chans, chans, axis=2)
     gain = lax.dynamic_slice_in_dim(skip_gain, place * chans, chans, axis=0)
     x = full.astype(jnp.float32)
@@ -91,7 +93,7 @@
         + taps[2][:, None, :, None] * shift_back(x, 2)
     )
     source = shaped[1] * shaped[2]
-    convolved = causal_conv(source, filt, tables)
+    convolved = causal_conv(source, spec_f, tables)
     gated = (shaped[0] * (convolved + gain[None, :, None] * source)).astype(jnp.bfloat16)
     gated = lax.all_to_all(gated.reshape(seq_count, blocks, chans, cols), "seq", 0, 0, tiled=True)
     gated = gated.transpose(1, 3, 0, 2).reshape(shard_len, local_chans)

time: 125 us -> 125 us (level)
    optimization_barrier x0 -> x1, local copies, waits for them, and re-layouts: none -> 1.64 us  [on_device(): filt, streams = lax.optimization_barrier((filt, streams))]
    transpose x1 -> x0, local copies, waits for them, and re-layouts: 1.56 us -> none  [on_device(): streams.reshape(3, blocks, cols, seq_count, chans).transpose(3, 0, 1, 4, 2)]
where the time goes in v8:
time: 125 us; the launch traced here: 124 us
  blocking collectives  69.3 us (55%)
  waiting for transfers between devices  17.1 us (14%)
  starting transfers between devices  12 us (10%)
  local copies, waits for them, and re-layouts  10.8 us (9%)
  matrix products  10.1 us (8%)
  other arithmetic  4.51 us (4%)
    psum x1, blocking collectives, on_device(): return lax.psum(terms, 'chan').astype(jnp.bfloat16)  57.5 us
    all_to_all x1, blocking collectives, on_device(): lax.all_to_all(gated.reshape(seq_count, blocks, chans, cols), 'seq', 0, 0...  11.8 us
    all_to_all x1, waiting for transfers between devices, on_device(): full = lax.all_to_all(streams, 'seq', 0, 0, tiled=True)  9.06 us
    all_to_all x1, starting transfers between devices, on_device(): lax.all_to_all(filt, 'seq', 0, 0, tiled=True)  8.16 us
    all_to_all x1, waiting for transfers between devices, on_device(): lax.all_to_all(filt, 'seq', 0, 0, tiled=True)  7.99 us
    unnamed x31, local copies, waits for them, and re-layouts  5.01 us
    all_to_all x1, starting transfers between devices, on_device(): full = lax.all_to_all(streams, 'seq', 0, 0, tiled=True)  3.79 us
    dot_general x1, matrix products, on_device(): terms = jnp.dot(gated, out_weight, preferred_element_type=jnp.float32)  3.27 us
  transfers between devices with their start and end apart: 2, of which 2 were waited for; matrix products, arithmetic and copies ran while one was open for 5% of the time, Pallas kernels for 0%

profile of v8, /device:TPU:0, one launch (start us, length us, event | category | flops | bytes accessed | tf_op | source)
XLA Modules:
  0.0 124.1 jit_solution(956714496291219181)
XLA Ops:
  0.0 1.3 %copy.33 = f32[256,512]{0,1:T(8,128)S(1)} copy(f32[256,512]{1,0:T(8,128)} %param.18) | data formatting | bytes 1048576 | tf_op args[5]
  1.3 1.1 reshape.96
  2.4 8.2 %all-to-all-start = ((f32[16,2,32,128]{3,1,2,0:T(2,128)}), f32[16,2,32,128]{3,1,2,0:T(2,128)S(1)}, u32[]{:S(2)}, u32[]{:S(2)}) async-start(f32[16,2,32,128]{3,1,2,0:T(2,128)} %bitcast.1), calls=%async_computation | async-start | bytes 1048576 | tf_op jit(solution)/shard_map/all_to_all | solution.py:79
  11.2 0.8 dynamic_slice.7
  12.0 0.8 dynamic-slice_bitcast_fusion.2
  12.8 1.3 %maximum_bitcast_fusion = bf16[16,3,2,32,128]{4,2,3,0,1:T(2,128)(2,1)S(1)} fusion(bf16[1,2,128,16,32]{2,1,4,3,0:T(2,128)(2,1)S(1)} %stack.14, bf16[1,2,128,16,32]{2,1,4,3,0:T(2,128)(2,1)S(1)} %stack.13, bf16[1,2,128,16,32]{2,1,4,3,0:T(2,128)(2,1)S(1)} %stack.12), kind=kLoop, calls=%fused_computation.43 | loop fusion | flops 786432 | bytes 1572864 | tf_op jit(solution)/shard_map/transpose | solution.py:81
  14.1 8.0 %all-to-all-done = f32[16,2,32,128]{3,1,2,0:T(2,128)S(1)} async-done(((f32[16,2,32,128]{3,1,2,0:T(2,128)}), f32[16,2,32,128]{3,1,2,0:T(2,128)S(1)}, u32[]{:S(2)}, u32[]{:S(2)}) %all-to-all-start) | async-done | bytes 524320 | tf_op jit(solution)/shard_map/all_to_all | solution.py:79
  22.1 1.6 %copy.38 = bf16[16,3,2,32,128]{4,2,3,1,0:T(2,128)(2,1)} copy(bf16[16,3,2,32,128]{4,2,3,0,1:T(2,128)(2,1)S(1)} %maximum_bitcast_fusion) | data formatting | bytes 1572864 | tf_op jit(solution)/shard_map/optimization_barrier | solution.py:82
  23.8 3.8 %all-to-all-start.1 = ((bf16[16,3,2,32,128]{4,2,3,1,0:T(2,128)(2,1)}), bf16[16,3,2,32,128]{4,2,3,1,0:T(2,128)(2,1)S(1)}, u32[]{:S(2)}, u32[]{:S(2)}) async-start(bf16[16,3,2,32,128]{4,2,3,1,0:T(2,128)(2,1)} %copy.38), calls=%async_computation.1 | async-start | bytes 1572864 | tf_op jit(solution)/shard_map/all_to_all | solution.py:84
  27.6 1.0 fusion.27
  29.3 0.3 copy-done.2
  29.6 0.4 fusion.22
  30.0 0.6 copy-done.1
  30.6 1.0 fusion.3
  31.6 9.1 %all-to-all-done.1 = bf16[16,3,2,32,128]{4,2,3,1,0:T(2,128)(2,1)S(1)} async-done(((bf16[16,3,2,32,128]{4,2,3,1,0:T(2,128)(2,1)}), bf16[16,3,2,32,128]{4,2,3,1,0:T(2,128)(2,1)S(1)}, u32[]{:S(2)}, u32[]{:S(2)}) %all-to-all-start.1) | async-done | bytes 786464 | tf_op jit(solution)/shard_map/all_to_all | solution.py:84
  41.0 0.5 pad_slice_fusion
  41.5 0.5 pad_slice_fusion.1
  41.9 1.1 fusion.16
  43.1 1.0 fusion.24
  44.8 0.4 fusion.20
  45.2 1.0 fusion.7
  46.2 0.3 multiply_subtract_fusion.1
  46.5 0.6 copy-done.4
  47.1 1.0 fusion.11
  48.2 0.3 multiply_subtract_fusion
  48.7 0.5 copy-done.9
  49.2 1.7 %fusion.17 = f32[4,8,32,128]{3,1,2,0:T(8,128)S(1)} fusion(f32[32,128]{1,0:T(8,128)S(1)} %copy-done.9, f32[16,8,32,128]{3,2,1,0:T(8,128)S(1)} %bitcast.101), kind=kOutput, calls=%fused_computation.22 | convolution fusion | flops 100663296 | bytes 2637824 | tf_op jit(solution)/shard_map/dot_general | solution.py:59
  51.1 0.2 multiply_convert_fusion
  51.3 11.8 %all_to_all.15 = bf16[16,2,32,128]{3,2,1,0:T(8,128)(2,1)S(1)} all-to-all(bf16[16,2,32,128]{3,2,1,0:T(8,128)(2,1)S(1)} %multiply_convert_fusion), channel_id=1, replica_groups=mesh['seq'=16,'chan'=8] {'seq'}, dimensions={0} | all-to-all | bytes 524288 | tf_op jit(solution)/shard_map/all_to_all | solution.py:98
  63.1 0.2 copy.40
  63.3 3.3 %fusion.30 = f32[256,4096]{1,0:T(8,128)} fusion(bf16[512,4096]{1,0:T(8,128)(2,1)S(1)} %copy-done, bf16[64,8,2,128]{3,2,1,0:T(2,128)(2,1)S(1)} %bitcast.107), kind=kOutput, calls=%fused_computation.53 | convolution fusion | flops 1073741824 | bytes 8650752 | tf_op jit(solution)/shard_map/dot_general | solution.py:100
  66.6 57.5 %all-reduce.2 = bf16[256,4096]{1,0:T(8,128)(2,1)} all-reduce(f32[256,4096]{1,0:T(8,128)} %fusion.30), channel_id=1, replica_groups=mesh['seq'=16,'chan'=8] {'chan'}, use_global_device_ids=true, to_apply=%region_0.0 | all-reduce | flops 1048576 | bytes 6291456 | tf_op jit(solution)/shard_map/psum | solution.py:101
  (34 shorter events, 2.6 us)
Async XLA Ops:
  0.0 10.5 %copy-start.5 = (bf16[256,512]{1,0:T(8,128)(2,1)S(1)}, bf16[256,512]{1,0:T(8,128)(2,1)}, u32[]{:S(2)}) copy-start(bf16[256,512]{1,0:T(8,128)(2,1)} %param.13) | copy-start | bytes 786436
  0.0 10.8 %copy-start.6 = (bf16[256,512]{1,0:T(8,128)(2,1)S(1)}, bf16[256,512]{1,0:T(8,128)(2,1)}, u32[]{:S(2)}) copy-start(bf16[256,512]{1,0:T(8,128)(2,1)} %param.14) | copy-start | bytes 786436
  1.3 9.7 %copy-start.7 = (bf16[256,512]{1,0:T(8,128)(2,1)S(1)}, bf16[256,512]{1,0:T(8,128)(2,1)}, u32[]{:S(2)}) copy-start(bf16[256,512]{1,0:T(8,128)(2,1)} %param.15) | copy-start | bytes 786436
  2.4 19.7 %all-to-all-start = ((f32[16,2,32,128]{3,1,2,0:T(2,128)}), f32[16,2,32,128]{3,1,2,0:T(2,128)S(1)}, u32[]{:S(2)}, u32[]{:S(2)}) async-start(f32[16,2,32,128]{3,1,2,0:T(2,128)} %bitcast.1), calls=%async_computation | async-start | bytes 1048576 | tf_op jit(solution)/shard_map/all_to_all | solution.py:79
  14.1 13.5 %copy-start.8 = (f32[128,32]{1,0:T(8,128)S(1)}, f32[128,32]{1,0:T(8,128)}, u32[]{:S(2)}) copy-start(f32[128,32]{1,0:T(8,128)} %constant.26.clone) | copy-start | bytes 49156
  23.8 16.9 %all-to-all-start.1 = ((bf16[16,3,2,32,128]{4,2,3,1,0:T(2,128)(2,1)}), bf16[16,3,2,32,128]{4,2,3,1,0:T(2,128)(2,1)S(1)}, u32[]{:S(2)}, u32[]{:S(2)}) async-start(bf16[16,3,2,32,128]{4,2,3,1,0:T(2,128)(2,1)} %copy.38), calls=%async_computation.1 | async-start | bytes 1572864 | tf_op jit(solution)/shard_map/all_to_all | solution.py:84
  28.8 0.8 copy-start.2
  28.9 0.8 copy-start.3
  29.6 0.9 copy-start.1
  46.2 1.0 copy-start.4
  48.5 0.7 copy-start.9
  49.2 14.1 %copy-start = (bf16[512,4096]{1,0:T(8,128)(2,1)S(1)}, bf16[512,4096]{1,0:T(8,128)(2,1)}, u32[]{:S(2)}) copy-start(bf16[512,4096]{1,0:T(8,128)(2,1)} %param.19) | copy-start | bytes 12582916

commit v9 on v8

--- a/solution.py
+++ b/solution.py
@@ -13,7 +13,8 @@
     rows = 64
     cols = padded_len // rows
     half_rows = rows // 2
-    k1 = np.arange(rows)[:, None]
+    freqs = half_rows + 1
+    k1 = np.arange(freqs)[:, None]
     n1 = np.arange(half_rows)[None, :]
     angle1 = 2.0 * np.pi * k1 * n1 / rows
     first = np.concatenate([np.cos(angle1), -np.sin(angle1)], axis=0)
@@ -25,15 +26,17 @@
     c2, s2 = np.cos(angle2), np.sin(angle2)
     forward = np.block([[c2, -s2], [s2, c2]])
     backward = np.block([[c2, s2], [-s2, c2]])
-    last = np.concatenate([np.cos(angle1.T), -np.sin(angle1.T)], axis=1) / padded_len
+    weight = np.full(freqs, 2.0)
+    weight[0] = weight[-1] = 1.0
+    last = np.concatenate([np.cos(angle1.T) * weight, -np.sin(angle1.T) * weight], axis=1) / padded_len
     as32 = lambda a: jnp.asarray(a.astype(np.float32))
-    return rows, cols, as32(first), tuple(as32(t) for t in twist), as32(forward), as32(backward), as32(last)
+    return freqs, cols, as32(first), tuple(as32(t) for t in twist), as32(forward), as32(backward), as32(last)
 
 
 def spectrum(grid, tables):
     rows, cols, first, twist, forward, _, _ = tables
     chans = grid.shape[1]
-    stage = jnp.dot(first, grid.reshape(rows // 2, chans * cols), precision=HIGH).reshape(2, rows, chans, cols)
+    stage = jnp.dot(first, grid.reshape(grid.shape[0], chans * cols), precision=HIGH).reshape(2, rows, chans, cols)
     tw_cos = twist[0][:, None, :]
     tw_sin = twist[1][:, None, :]
     turned_real = stage[0] * tw_cos + stage[1] * tw_sin
@@ -56,7 +59,7 @@
     turned_real = br * tw_cos - bi * tw_sin
     turned_imag = bi * tw_cos + br * tw_sin
     stacked = jnp.concatenate([turned_real, turned_imag], axis=0).reshape(2 * rows, chans * cols)
-    return jnp.dot(last, stacked, precision=HIGH).reshape(rows // 2, chans, cols)
+    return jnp.dot(last, stacked, precision=HIGH).reshape(last.shape[0], chans, cols)
 
 
 def shift_back(grid, steps):

time: 125 us -> 122 us (0.976)
  matrix products: 10.1 us -> 7.19 us
  waiting for transfers between devices: 17.1 us -> 18.4 us
    dot_general x3, matrix products: 3.81 us -> 2.14 us  [the longest x2 1.72 us: spectrum(): jnp.dot(first, grid.reshape(grid.shape[0], chans * cols), precision=HIGH)]
    all_to_all x1, waiting for transfers between devices: 9.06 us -> 10.4 us  [on_device(): full = lax.all_to_all(streams, 'seq', 0, 0, tiled=True)]
  transfers between devices with their start and end apart: 2 -> 2, of which waited for: 2 -> 2; matrix products, arithmetic and copies ran while one was open for 5% -> 4% of each run, Pallas kernels for 0% -> 0%
where the time goes in v9:
time: 122 us
  blocking collectives  69.4 us (57%)
  waiting for transfers between devices  18.4 us (15%)
  starting transfers between devices  12.1 us (10%)
  local copies, waits for them, and re-layouts  10.5 us (9%)
  matrix products  7.19 us (6%)
  other arithmetic  3.68 us (3%)
    psum x1, blocking collectives, on_device(): return lax.psum(terms, 'chan').astype(jnp.bfloat16)  57.5 us
    all_to_all x1, blocking collectives, on_device(): lax.all_to_all(gated.reshape(seq_count, blocks, chans, cols), 'seq', 0, 0...  11.9 us
    all_to_all x1, waiting for transfers between devices, on_device(): full = lax.all_to_all(streams, 'seq', 0, 0, tiled=True)  10.4 us
    all_to_all x1, starting transfers between devices, on_device(): lax.all_to_all(filt, 'seq', 0, 0, tiled=True)  8.29 us
    all_to_all x1, waiting for transfers between devices, on_device(): lax.all_to_all(filt, 'seq', 0, 0, tiled=True)  8 us
    unnamed x31, local copies, waits for them, and re-layouts  4.52 us
    all_to_all x1, starting transfers between devices, on_device(): full = lax.all_to_all(streams, 'seq', 0, 0, tiled=True)  3.79 us
    dot_general x1, matrix products, on_device(): terms = jnp.dot(gated, out_weight, preferred_element_type=jnp.float32)  3.28 us
  transfers between devices with their start and end apart: 2, of which 2 were waited for; matrix products, arithmetic and copies ran while one was open for 4% of the time, Pallas kernels for 0%

profile of v9, /device:TPU:0, one launch (start us, length us, event | category | flops | bytes accessed | tf_op | source)
XLA Modules:
  0.0 121.7 jit_solution(18162765272065241982)
XLA Ops:
  0.0 1.3 %copy.33 = f32[256,512]{0,1:T(8,128)S(1)} copy(f32[256,512]{1,0:T(8,128)} %param.18) | data formatting | bytes 1048576 | tf_op args[5]
  1.3 1.1 reshape.96
  2.4 8.3 %all-to-all-start = ((f32[16,2,32,128]{3,1,2,0:T(2,128)}), f32[16,2,32,128]{3,1,2,0:T(2,128)S(1)}, u32[]{:S(2)}, u32[]{:S(2)}) async-start(f32[16,2,32,128]{3,1,2,0:T(2,128)} %bitcast.1), calls=%async_computation | async-start | bytes 1048576 | tf_op jit(solution)/shard_map/all_to_all | solution.py:82
  11.3 0.8 dynamic_slice.7
  12.1 0.8 dynamic-slice_bitcast_fusion.2
  12.9 1.3 %maximum_bitcast_fusion = bf16[16,3,2,32,128]{4,2,3,0,1:T(2,128)(2,1)S(1)} fusion(bf16[1,2,128,16,32]{2,1,4,3,0:T(2,128)(2,1)S(1)} %stack.14, bf16[1,2,128,16,32]{2,1,4,3,0:T(2,128)(2,1)S(1)} %stack.13, bf16[1,2,128,16,32]{2,1,4,3,0:T(2,128)(2,1)S(1)} %stack.12), kind=kLoop, calls=%fused_computation.20 | loop fusion | flops 786432 | bytes 1572864 | tf_op jit(solution)/shard_map/transpose | solution.py:84
  14.2 8.0 %all-to-all-done = f32[16,2,32,128]{3,1,2,0:T(2,128)S(1)} async-done(((f32[16,2,32,128]{3,1,2,0:T(2,128)}), f32[16,2,32,128]{3,1,2,0:T(2,128)S(1)}, u32[]{:S(2)}, u32[]{:S(2)}) %all-to-all-start) | async-done | bytes 524320 | tf_op jit(solution)/shard_map/all_to_all | solution.py:82
  22.3 1.6 %copy.38 = bf16[16,3,2,32,128]{4,2,3,1,0:T(2,128)(2,1)} copy(bf16[16,3,2,32,128]{4,2,3,0,1:T(2,128)(2,1)S(1)} %maximum_bitcast_fusion) | data formatting | bytes 1572864 | tf_op jit(solution)/shard_map/optimization_barrier | solution.py:85
  23.9 3.8 %all-to-all-start.1 = ((bf16[16,3,2,32,128]{4,2,3,1,0:T(2,128)(2,1)}), bf16[16,3,2,32,128]{4,2,3,1,0:T(2,128)(2,1)S(1)}, u32[]{:S(2)}, u32[]{:S(2)}) async-start(bf16[16,3,2,32,128]{4,2,3,1,0:T(2,128)(2,1)} %copy.38), calls=%async_computation.1 | async-start | bytes 1572864 | tf_op jit(solution)/shard_map/all_to_all | solution.py:87
  27.7 0.9 fusion.17
  29.0 0.4 copy-done.6
  29.4 0.2 multiply_add_fusion.3
  29.6 0.2 copy-done.1
  29.8 0.6 fusion.2
  30.4 10.4 %all-to-all-done.1 = bf16[16,3,2,32,128]{4,2,3,1,0:T(2,128)(2,1)S(1)} async-done(((bf16[16,3,2,32,128]{4,2,3,1,0:T(2,128)(2,1)}), bf16[16,3,2,32,128]{4,2,3,1,0:T(2,128)(2,1)S(1)}, u32[]{:S(2)}, u32[]{:S(2)}) %all-to-all-start.1) | async-done | bytes 786464 | tf_op jit(solution)/shard_map/all_to_all | solution.py:87
  40.8 0.2 copy_convert_fusion
  41.1 0.5 pad_slice_fusion
  41.6 0.5 pad_slice_fusion.1
  42.1 1.1 fusion.1
  43.3 0.9 fusion.14
  44.5 0.2 multiply_add_fusion.2
  44.7 0.6 fusion.6
  45.5 0.8 copy-done.2
  46.2 0.6 fusion.10
  46.8 0.2 multiply_subtract_fusion
  47.2 0.7 copy.47
  47.9 0.4 convolution_bitcast_fusion
  48.5 0.2 multiply_convert_fusion
  48.7 11.9 %all_to_all.15 = bf16[16,2,32,128]{3,2,1,0:T(8,128)(2,1)S(1)} all-to-all(bf16[16,2,32,128]{3,2,1,0:T(8,128)(2,1)S(1)} %multiply_convert_fusion), channel_id=1, replica_groups=mesh['seq'=16,'chan'=8] {'seq'}, dimensions={0} | all-to-all | bytes 524288 | tf_op jit(solution)/shard_map/all_to_all | solution.py:101
  60.6 0.2 copy.40
  60.9 3.3 %fusion.20 = f32[256,4096]{1,0:T(8,128)} fusion(bf16[512,4096]{1,0:T(8,128)(2,1)S(1)} %copy-done, bf16[64,8,2,128]{3,2,1,0:T(2,128)(2,1)S(1)} %bitcast.90), kind=kOutput, calls=%fused_computation.38 | convolution fusion | flops 1073741824 | bytes 8650752 | tf_op jit(solution)/shard_map/dot_general | solution.py:103
  64.1 57.5 %all-reduce.2 = bf16[256,4096]{1,0:T(8,128)(2,1)} all-reduce(f32[256,4096]{1,0:T(8,128)} %fusion.20), channel_id=1, replica_groups=mesh['seq'=16,'chan'=8] {'chan'}, use_global_device_ids=true, to_apply=%region_0.0 | all-reduce | flops 1048576 | bytes 6291456 | tf_op jit(solution)/shard_map/psum | solution.py:104
  (36 shorter events, 2.1 us)
Async XLA Ops:
  0.0 10.7 %copy-start.3 = (bf16[256,512]{1,0:T(8,128)(2,1)S(1)}, bf16[256,512]{1,0:T(8,128)(2,1)}, u32[]{:S(2)}) copy-start(bf16[256,512]{1,0:T(8,128)(2,1)} %param.13) | copy-start | bytes 786436
  1.3 9.6 %copy-start.4 = (bf16[256,512]{1,0:T(8,128)(2,1)S(1)}, bf16[256,512]{1,0:T(8,128)(2,1)}, u32[]{:S(2)}) copy-start(bf16[256,512]{1,0:T(8,128)(2,1)} %param.14) | copy-start | bytes 786436
  2.4 8.8 %copy-start.5 = (bf16[256,512]{1,0:T(8,128)(2,1)S(1)}, bf16[256,512]{1,0:T(8,128)(2,1)}, u32[]{:S(2)}) copy-start(bf16[256,512]{1,0:T(8,128)(2,1)} %param.15) | copy-start | bytes 786436
  2.4 19.8 %all-to-all-start = ((f32[16,2,32,128]{3,1,2,0:T(2,128)}), f32[16,2,32,128]{3,1,2,0:T(2,128)S(1)}, u32[]{:S(2)}, u32[]{:S(2)}) async-start(f32[16,2,32,128]{3,1,2,0:T(2,128)} %bitcast.1), calls=%async_computation | async-start | bytes 1048576 | tf_op jit(solution)/shard_map/all_to_all | solution.py:82
  22.2 5.5 %copy-start.8 = (f32[66,32]{1,0:T(8,128)S(1)}, f32[66,32]{1,0:T(8,128)}, u32[]{:S(2)}) copy-start(f32[66,32]{1,0:T(8,128)} %constant.26.clone) | copy-start | bytes 25348
  23.9 16.9 %all-to-all-start.1 = ((bf16[16,3,2,32,128]{4,2,3,1,0:T(2,128)(2,1)}), bf16[16,3,2,32,128]{4,2,3,1,0:T(2,128)(2,1)S(1)}, u32[]{:S(2)}, u32[]{:S(2)}) async-start(bf16[16,3,2,32,128]{4,2,3,1,0:T(2,128)(2,1)} %copy.38), calls=%async_computation.1 | async-start | bytes 1572864 | tf_op jit(solution)/shard_map/all_to_all | solution.py:87
  28.7 0.7 copy-start.6
  28.7 0.7 copy-start.7
  28.8 1.0 copy-start.1
  45.3 1.0 copy-start.2
  47.2 0.7 copy-start.9
  47.9 12.9 %copy-start = (bf16[512,4096]{1,0:T(8,128)(2,1)S(1)}, bf16[512,4096]{1,0:T(8,128)(2,1)}, u32[]{:S(2)}) copy-start(bf16[512,4096]{1,0:T(8,128)(2,1)} %param.19) | copy-start | bytes 12582916

commit v10 on v9

--- a/solution.py
+++ b/solution.py
@@ -5,7 +5,7 @@
 from jax import lax
 from jax.sharding import PartitionSpec as P
 
-HIGH = lax.Precision.HIGH
+HIGH = lax.Precision.HIGHEST
 
 
 def dft_tables(seq_len):

time: 122 us -> 124 us (1.016)
  matrix products: 7.19 us -> 9.69 us
  transfers between devices with their start and end apart: 2 -> 2, of which waited for: 2 -> 2; matrix products, arithmetic and copies ran while one was open for 4% -> 5% of each run, Pallas kernels for 0% -> 0%
where the time goes in v10:
time: 124 us; the launch traced here: 123 us
  blocking collectives  69.4 us (56%)
  waiting for transfers between devices  17.5 us (14%)
  starting transfers between devices  12.1 us (10%)
  local copies, waits for them, and re-layouts  10.5 us (8%)
  matrix products  9.69 us (8%)
  other arithmetic  3.68 us (3%)
    psum x1, blocking collectives, on_device(): return lax.psum(terms, 'chan').astype(jnp.bfloat16)  57.5 us
    all_to_all x1, blocking collectives, on_device(): lax.all_to_all(gated.reshape(seq_count, blocks, chans, cols), 'seq', 0, 0...  11.9 us
    all_to_all x1, waiting for transfers between devices, on_device(): full = lax.all_to_all(streams, 'seq', 0, 0, tiled=True)  9.48 us
    all_to_all x1, starting transfers between devices, on_device(): lax.all_to_all(filt, 'seq', 0, 0, tiled=True)  8.29 us
    all_to_all x1, waiting for transfers between devices, on_device(): lax.all_to_all(filt, 'seq', 0, 0, tiled=True)  8 us
    unnamed x31, local copies, waits for them, and re-layouts  4.52 us
    all_to_all x1, starting transfers between devices, on_device(): full = lax.all_to_all(streams, 'seq', 0, 0, tiled=True)  3.79 us
    dot_general x1, matrix products, on_device(): terms = jnp.dot(gated, out_weight, preferred_element_type=jnp.float32)  3.28 us
  transfers between devices with their start and end apart: 2, of which 2 were waited for; matrix products, arithmetic and copies ran while one was open for 5% of the time, Pallas kernels for 0%

profile of v10, /device:TPU:0, one launch (start us, length us, event | category | flops | bytes accessed | tf_op | source)
XLA Modules:
  0.0 123.3 jit_solution(7171042066375817523)
XLA Ops:
  0.0 1.3 %copy.33 = f32[256,512]{0,1:T(8,128)S(1)} copy(f32[256,512]{1,0:T(8,128)} %param.18) | data formatting | bytes 1048576 | tf_op args[5]
  1.3 1.1 reshape.96
  2.4 8.3 %all-to-all-start = ((f32[16,2,32,128]{3,1,2,0:T(2,128)}), f32[16,2,32,128]{3,1,2,0:T(2,128)S(1)}, u32[]{:S(2)}, u32[]{:S(2)}) async-start(f32[16,2,32,128]{3,1,2,0:T(2,128)} %bitcast.1), calls=%async_computation | async-start | bytes 1048576 | tf_op jit(solution)/shard_map/all_to_all | solution.py:82
  11.3 0.8 dynamic_slice.7
  12.1 0.8 dynamic-slice_bitcast_fusion.2
  12.9 1.3 %maximum_bitcast_fusion = bf16[16,3,2,32,128]{4,2,3,0,1:T(2,128)(2,1)S(1)} fusion(bf16[1,2,128,16,32]{2,1,4,3,0:T(2,128)(2,1)S(1)} %stack.14, bf16[1,2,128,16,32]{2,1,4,3,0:T(2,128)(2,1)S(1)} %stack.13, bf16[1,2,128,16,32]{2,1,4,3,0:T(2,128)(2,1)S(1)} %stack.12), kind=kLoop, calls=%fused_computation.20 | loop fusion | flops 786432 | bytes 1572864 | tf_op jit(solution)/shard_map/transpose | solution.py:84
  14.2 8.0 %all-to-all-done = f32[16,2,32,128]{3,1,2,0:T(2,128)S(1)} async-done(((f32[16,2,32,128]{3,1,2,0:T(2,128)}), f32[16,2,32,128]{3,1,2,0:T(2,128)S(1)}, u32[]{:S(2)}, u32[]{:S(2)}) %all-to-all-start) | async-done | bytes 524320 | tf_op jit(solution)/shard_map/all_to_all | solution.py:82
  22.3 1.6 %copy.38 = bf16[16,3,2,32,128]{4,2,3,1,0:T(2,128)(2,1)} copy(bf16[16,3,2,32,128]{4,2,3,0,1:T(2,128)(2,1)S(1)} %maximum_bitcast_fusion) | data formatting | bytes 1572864 | tf_op jit(solution)/shard_map/optimization_barrier | solution.py:85
  23.9 3.8 %all-to-all-start.1 = ((bf16[16,3,2,32,128]{4,2,3,1,0:T(2,128)(2,1)}), bf16[16,3,2,32,128]{4,2,3,1,0:T(2,128)(2,1)S(1)}, u32[]{:S(2)}, u32[]{:S(2)}) async-start(bf16[16,3,2,32,128]{4,2,3,1,0:T(2,128)(2,1)} %copy.38), calls=%async_computation.1 | async-start | bytes 1572864 | tf_op jit(solution)/shard_map/all_to_all | solution.py:87
  27.7 1.3 %fusion.17 = f32[66,4096]{1,0:T(8,128)S(1)} fusion(f32[66,32]{1,0:T(8,128)S(1)} %copy-done.8, f32[4,8,32,128]{3,2,1,0:T(8,128)S(1)} %bitcast.88), kind=kOutput, calls=%fused_computation.33 | convolution fusion | flops 103809024 | bytes 1614080 | tf_op jit(solution)/shard_map/dot_general | solution.py:39
  29.4 0.4 copy-done.6
  29.9 0.2 multiply_add_fusion.3
  30.1 0.2 copy-done.1
  30.3 1.0 fusion.2
  31.3 9.5 %all-to-all-done.1 = bf16[16,3,2,32,128]{4,2,3,1,0:T(2,128)(2,1)S(1)} async-done(((bf16[16,3,2,32,128]{4,2,3,1,0:T(2,128)(2,1)}), bf16[16,3,2,32,128]{4,2,3,1,0:T(2,128)(2,1)S(1)}, u32[]{:S(2)}, u32[]{:S(2)}) %all-to-all-start.1) | async-done | bytes 786464 | tf_op jit(solution)/shard_map/all_to_all | solution.py:87
  40.8 0.2 copy_convert_fusion
  41.1 0.5 pad_slice_fusion
  41.6 0.5 pad_slice_fusion.1
  42.1 1.1 fusion.1
  43.3 1.3 %fusion.14 = f32[66,4096]{1,0:T(8,128)S(1)} fusion(f32[66,32]{1,0:T(8,128)S(1)} %copy-done.8, f32[4,8,32,128]{3,2,1,0:T(8,128)S(1)} %bitcast.77), kind=kOutput, calls=%fused_computation.30 | convolution fusion | flops 103809024 | bytes 1614080 | tf_op jit(solution)/shard_map/dot_general | solution.py:39
  45.0 0.2 multiply_add_fusion.2
  45.2 1.0 fusion.6
  46.4 0.8 copy-done.2
  47.1 1.0 fusion.10
  48.2 0.2 multiply_subtract_fusion
  48.5 0.7 copy.47
  49.3 0.7 convolution_bitcast_fusion
  50.1 0.2 multiply_convert_fusion
  50.3 11.9 %all_to_all.15 = bf16[16,2,32,128]{3,2,1,0:T(8,128)(2,1)S(1)} all-to-all(bf16[16,2,32,128]{3,2,1,0:T(8,128)(2,1)S(1)} %multiply_convert_fusion), channel_id=1, replica_groups=mesh['seq'=16,'chan'=8] {'seq'}, dimensions={0} | all-to-all | bytes 524288 | tf_op jit(solution)/shard_map/all_to_all | solution.py:101
  62.2 0.2 copy.40
  62.5 3.3 %fusion.20 = f32[256,4096]{1,0:T(8,128)} fusion(bf16[512,4096]{1,0:T(8,128)(2,1)S(1)} %copy-done, bf16[64,8,2,128]{3,2,1,0:T(2,128)(2,1)S(1)} %bitcast.90), kind=kOutput, calls=%fused_computation.38 | convolution fusion | flops 1073741824 | bytes 8650752 | tf_op jit(solution)/shard_map/dot_general | solution.py:103
  65.7 57.5 %all-reduce.2 = bf16[256,4096]{1,0:T(8,128)(2,1)} all-reduce(f32[256,4096]{1,0:T(8,128)} %fusion.20), channel_id=1, replica_groups=mesh['seq'=16,'chan'=8] {'chan'}, use_global_device_ids=true, to_apply=%region_0.0 | all-reduce | flops 1048576 | bytes 6291456 | tf_op jit(solution)/shard_map/psum | solution.py:104
  (36 shorter events, 2.1 us)
Async XLA Ops:
  0.0 10.7 %copy-start.3 = (bf16[256,512]{1,0:T(8,128)(2,1)S(1)}, bf16[256,512]{1,0:T(8,128)(2,1)}, u32[]{:S(2)}) copy-start(bf16[256,512]{1,0:T(8,128)(2,1)} %param.13) | copy-start | bytes 786436
  1.3 9.6 %copy-start.4 = (bf16[256,512]{1,0:T(8,128)(2,1)S(1)}, bf16[256,512]{1,0:T(8,128)(2,1)}, u32[]{:S(2)}) copy-start(bf16[256,512]{1,0:T(8,128)(2,1)} %param.14) | copy-start | bytes 786436
  2.4 8.8 %copy-start.5 = (bf16[256,512]{1,0:T(8,128)(2,1)S(1)}, bf16[256,512]{1,0:T(8,128)(2,1)}, u32[]{:S(2)}) copy-start(bf16[256,512]{1,0:T(8,128)(2,1)} %param.15) | copy-start | bytes 786436
  2.4 19.8 %all-to-all-start = ((f32[16,2,32,128]{3,1,2,0:T(2,128)}), f32[16,2,32,128]{3,1,2,0:T(2,128)S(1)}, u32[]{:S(2)}, u32[]{:S(2)}) async-start(f32[16,2,32,128]{3,1,2,0:T(2,128)} %bitcast.1), calls=%async_computation | async-start | bytes 1048576 | tf_op jit(solution)/shard_map/all_to_all | solution.py:82
  22.2 5.5 %copy-start.8 = (f32[66,32]{1,0:T(8,128)S(1)}, f32[66,32]{1,0:T(8,128)}, u32[]{:S(2)}) copy-start(f32[66,32]{1,0:T(8,128)} %constant.26.clone) | copy-start | bytes 25348
  23.9 16.9 %all-to-all-start.1 = ((bf16[16,3,2,32,128]{4,2,3,1,0:T(2,128)(2,1)}), bf16[16,3,2,32,128]{4,2,3,1,0:T(2,128)(2,1)S(1)}, u32[]{:S(2)}, u32[]{:S(2)}) async-start(bf16[16,3,2,32,128]{4,2,3,1,0:T(2,128)(2,1)} %copy.38), calls=%async_computation.1 | async-start | bytes 1572864 | tf_op jit(solution)/shard_map/all_to_all | solution.py:87
  29.2 0.7 copy-start.6
  29.2 0.7 copy-start.7
  29.3 1.0 copy-start.1
  46.2 1.0 copy-start.2
  48.5 0.7 copy-start.9
  49.3 13.2 %copy-start = (bf16[512,4096]{1,0:T(8,128)(2,1)S(1)}, bf16[512,4096]{1,0:T(8,128)(2,1)}, u32[]{:S(2)}) copy-start(bf16[512,4096]{1,0:T(8,128)(2,1)} %param.19) | copy-start | bytes 12582916

commit v11 on v10

--- a/solution.py
+++ b/solution.py
@@ -79,14 +79,15 @@
     cols = tables[1]
     blocks = shard_len // cols
     filt = long_filter.reshape(blocks, cols, seq_count, chans).transpose(2, 0, 3, 1)
-    filt = lax.all_to_all(filt, "seq", 0, 0, tiled=True).reshape(seq_count * blocks, chans, cols)
+    filt = lax.all_to_all(filt.reshape(seq_count, blocks * chans, cols), "seq", 0, 0, tiled=True)
+    filt = filt.reshape(seq_count * blocks, chans, cols)
     streams = jnp.stack([query_projected, key_stream, value_stream])
     streams = streams.reshape(3, blocks, cols, seq_count, chans).transpose(3, 0, 1, 4, 2)
     filt, streams = lax.optimization_barrier((filt, streams))
     spec_f = spectrum(filt, tables)
-    full = lax.all_to_all(streams, "seq", 0, 0, tiled=True)
+    full = lax.all_to_all(streams.reshape(seq_count, 3 * blocks * chans, cols), "seq", 0, 0, tiled=True)
     spec_f, full = lax.optimization_barrier((spec_f, full))
-    full = full.transpose(1, 0, 2, 3, 4).reshape(3, seq_count * blocks, chans, cols)
+    full = full.reshape(seq_count, 3, blocks, chans, cols).transpose(1, 0, 2, 3, 4).reshape(3, seq_count * blocks, chans, cols)
     taps = lax.dynamic_slice_in_dim(short_taps, place * chans, chans, axis=2)
     gain = lax.dynamic_slice_in_dim(skip_gain, place * chans, chans, axis=0)
     x = full.astype(jnp.float32)
@@ -98,8 +99,8 @@
     source = shaped[1] * shaped[2]
     convolved = causal_conv(source, spec_f, tables)
     gated = (shaped[0] * (convolved + gain[None, :, None] * source)).astype(jnp.bfloat16)
-    gated = lax.all_to_all(gated.reshape(seq_count, blocks, chans, cols), "seq", 0, 0, tiled=True)
-    gated = gated.transpose(1, 3, 0, 2).reshape(shard_len, local_chans)
+    gated = lax.all_to_all(gated.reshape(seq_count, blocks * chans, cols), "seq", 0, 0, tiled=True)
+    gated = gated.reshape(seq_count, blocks, chans, cols).transpose(1, 3, 0, 2).reshape(shard_len, local_chans)
     terms = jnp.dot(gated, out_weight, preferred_element_type=jnp.float32)
     return lax.psum(terms, "chan").astype(jnp.bfloat16)
 

time: 124 us -> 125 us (level)
  matrix products: 9.69 us -> 11.8 us
    dot_general x1, matrix products: 3.28 us -> 5.44 us  [on_device(): terms = jnp.dot(gated, out_weight, preferred_element_type=jnp.float32)]
    unnamed x31 -> x28, local copies, waits for them, and re-layouts: 4.52 us -> 4.37 us
where the time goes in v11:
time: 125 us
  blocking collectives  69.3 us (55%)
  waiting for transfers between devices  17.4 us (14%)
  starting transfers between devices  12.1 us (10%)
  matrix products  11.8 us (9%)
  local copies, waits for them, and re-layouts  10.1 us (8%)
  other arithmetic  3.64 us (3%)
    psum x1, blocking collectives, on_device(): return lax.psum(terms, 'chan').astype(jnp.bfloat16)  57.5 us
    all_to_all x1, blocking collectives, on_device(): lax.all_to_all(gated.reshape(seq_count, blocks * chans, cols), 'seq', 0,...  11.8 us
    all_to_all x1, waiting for transfers between devices, on_device(): lax.all_to_all(streams.reshape(seq_count, 3 * blocks * chans, cols), 'seq...  9.48 us
    all_to_all x1, starting transfers between devices, on_device(): lax.all_to_all(filt.reshape(seq_count, blocks * chans, cols), 'seq', 0, 0...  8.29 us
    all_to_all x1, waiting for transfers between devices, on_device(): lax.all_to_all(filt.reshape(seq_count, blocks * chans, cols), 'seq', 0, 0...  7.91 us
    dot_general x1, matrix products, on_device(): terms = jnp.dot(gated, out_weight, preferred_element_type=jnp.float32)  5.44 us
    unnamed x28, local copies, waits for them, and re-layouts  4.37 us
    all_to_all x1, starting transfers between devices, on_device(): lax.all_to_all(streams.reshape(seq_count, 3 * blocks * chans, cols), 'seq...  3.79 us
  transfers between devices with their start and end apart: 2, of which 2 were waited for; matrix products, arithmetic and copies ran while one was open for 5% of the time, Pallas kernels for 0%

profile of v11, /device:TPU:0, one launch (start us, length us, event | category | flops | bytes accessed | tf_op | source)
XLA Modules:
  0.0 124.8 jit_solution(9081951267968519285)
XLA Ops:
  0.0 1.2 copy.20
  1.3 0.3 reshape.110
  1.5 0.9 copy.21
  2.4 8.3 %all-to-all-start = ((f32[16,64,128]{2,1,0:T(8,128)}), f32[16,64,128]{2,1,0:T(8,128)S(1)}, u32[]{:S(2)}, u32[]{:S(2)}) async-start(f32[16,64,128]{2,1,0:T(8,128)} %bitcast.2), calls=%async_computation | async-start | bytes 1048576 | tf_op jit(solution)/shard_map/all_to_all | solution.py:82
  10.7 0.8 dynamic_slice.7
  12.2 0.8 dynamic-slice_bitcast_fusion.2
  13.0 1.3 %maximum_bitcast_fusion = bf16[16,3,2,32,128]{4,2,3,0,1:T(2,128)(2,1)S(1)} fusion(bf16[1,2,128,16,32]{2,1,4,3,0:T(2,128)(2,1)S(1)} %stack.14, bf16[1,2,128,16,32]{2,1,4,3,0:T(2,128)(2,1)S(1)} %stack.13, bf16[1,2,128,16,32]{2,1,4,3,0:T(2,128)(2,1)S(1)} %stack.12), kind=kLoop, calls=%fused_computation.20 | loop fusion | flops 786432 | bytes 1572864 | tf_op jit(solution)/shard_map/transpose | solution.py:85
  14.3 7.9 %all-to-all-done = f32[16,64,128]{2,1,0:T(8,128)S(1)} async-done(((f32[16,64,128]{2,1,0:T(8,128)}), f32[16,64,128]{2,1,0:T(8,128)S(1)}, u32[]{:S(2)}, u32[]{:S(2)}) %all-to-all-start) | async-done | bytes 524320 | tf_op jit(solution)/shard_map/all_to_all | solution.py:82
  22.2 1.1 copy.25
  23.3 3.8 %all-to-all-start.1 = ((bf16[16,192,128]{2,1,0:T(8,128)(2,1)}), bf16[16,192,128]{2,1,0:T(8,128)(2,1)S(1)}, u32[]{:S(2)}, u32[]{:S(2)}) async-start(bf16[16,192,128]{2,1,0:T(8,128)(2,1)} %bitcast.6), calls=%async_computation.1 | async-start | bytes 1572864 | tf_op jit(solution)/shard_map/all_to_all | solution.py:88
  27.1 1.3 %fusion.17 = f32[66,4096]{1,0:T(8,128)S(1)} fusion(f32[66,32]{1,0:T(8,128)S(1)} %copy-done.7, f32[4,8,32,128]{3,2,1,0:T(8,128)S(1)} %bitcast.90), kind=kOutput, calls=%fused_computation.32 | convolution fusion | flops 103809024 | bytes 1614080 | tf_op jit(solution)/shard_map/dot_general | solution.py:39
  28.9 0.4 copy-done.5
  29.3 0.2 multiply_add_fusion.3
  29.5 0.2 copy-done
  29.7 1.0 fusion.2
  30.7 9.5 %all-to-all-done.1 = bf16[16,192,128]{2,1,0:T(8,128)(2,1)S(1)} async-done(((bf16[16,192,128]{2,1,0:T(8,128)(2,1)}), bf16[16,192,128]{2,1,0:T(8,128)(2,1)S(1)}, u32[]{:S(2)}, u32[]{:S(2)}) %all-to-all-start.1) | async-done | bytes 786464 | tf_op jit(solution)/shard_map/all_to_all | solution.py:88
  40.2 0.2 convert_bitcast_fusion
  40.7 0.5 pad_slice_fusion
  41.1 0.5 pad_slice_fusion.1
  41.6 1.1 fusion.1
  42.8 1.3 %fusion.14 = f32[66,4096]{1,0:T(8,128)S(1)} fusion(f32[66,32]{1,0:T(8,128)S(1)} %copy-done.7, f32[4,8,32,128]{3,2,1,0:T(8,128)S(1)} %bitcast.79), kind=kOutput, calls=%fused_computation.29 | convolution fusion | flops 103809024 | bytes 1614080 | tf_op jit(solution)/shard_map/dot_general | solution.py:39
  44.5 0.2 multiply_add_fusion.2
  44.7 1.0 fusion.6
  45.9 0.8 copy-done.1
  46.7 1.0 fusion.10
  48.1 0.7 copy.34
  48.8 0.7 fusion.28
  49.6 0.2 multiply_convert_fusion
  49.8 11.8 %all_to_all.15 = bf16[16,64,128]{2,1,0:T(8,128)(2,1)S(1)} all-to-all(bf16[16,64,128]{2,1,0:T(8,128)(2,1)S(1)} %multiply_convert_fusion), channel_id=1, replica_groups=mesh['seq'=16,'chan'=8] {'seq'}, dimensions={0} | all-to-all | bytes 524288 | tf_op jit(solution)/shard_map/all_to_all | solution.py:102
  61.6 0.2 copy.27
  61.8 5.4 %fusion.20 = f32[256,4096]{1,0:T(8,128)} fusion(bf16[512,4096]{1,0:T(8,128)(2,1)} %param.19, bf16[64,8,2,128]{3,2,1,0:T(2,128)(2,1)S(1)} %bitcast.93), kind=kOutput, calls=%fused_computation.37 | convolution fusion | flops 1073741824 | bytes 8650752 | tf_op jit(solution)/shard_map/dot_general | solution.py:104
  67.2 57.5 %all-reduce.2 = bf16[256,4096]{1,0:T(8,128)(2,1)} all-reduce(f32[256,4096]{1,0:T(8,128)} %fusion.20), channel_id=1, replica_groups=mesh['seq'=16,'chan'=8] {'chan'}, use_global_device_ids=true, to_apply=%region_0.0 | all-reduce | flops 1048576 | bytes 6291456 | tf_op jit(solution)/shard_map/psum | solution.py:105
  (37 shorter events, 2.4 us)
Async XLA Ops:
  1.2 10.3 %copy-start.2 = (bf16[256,512]{1,0:T(8,128)(2,1)S(1)}, bf16[256,512]{1,0:T(8,128)(2,1)}, u32[]{:S(2)}) copy-start(bf16[256,512]{1,0:T(8,128)(2,1)} %param.13) | copy-start | bytes 786436
  1.5 10.2 %copy-start.3 = (bf16[256,512]{1,0:T(8,128)(2,1)S(1)}, bf16[256,512]{1,0:T(8,128)(2,1)}, u32[]{:S(2)}) copy-start(bf16[256,512]{1,0:T(8,128)(2,1)} %param.14) | copy-start | bytes 786436
  2.4 9.6 %copy-start.4 = (bf16[256,512]{1,0:T(8,128)(2,1)S(1)}, bf16[256,512]{1,0:T(8,128)(2,1)}, u32[]{:S(2)}) copy-start(bf16[256,512]{1,0:T(8,128)(2,1)} %param.15) | copy-start | bytes 786436
  2.4 19.8 %all-to-all-start = ((f32[16,64,128]{2,1,0:T(8,128)}), f32[16,64,128]{2,1,0:T(8,128)S(1)}, u32[]{:S(2)}, u32[]{:S(2)}) async-start(f32[16,64,128]{2,1,0:T(8,128)} %bitcast.2), calls=%async_computation | async-start | bytes 1048576 | tf_op jit(solution)/shard_map/all_to_all | solution.py:82
  22.2 4.9 %copy-start.7 = (f32[66,32]{1,0:T(8,128)S(1)}, f32[66,32]{1,0:T(8,128)}, u32[]{:S(2)}) copy-start(f32[66,32]{1,0:T(8,128)} %constant.26.clone) | copy-start | bytes 25348
  23.3 16.9 %all-to-all-start.1 = ((bf16[16,192,128]{2,1,0:T(8,128)(2,1)}), bf16[16,192,128]{2,1,0:T(8,128)(2,1)S(1)}, u32[]{:S(2)}, u32[]{:S(2)}) async-start(bf16[16,192,128]{2,1,0:T(8,128)(2,1)} %bitcast.6), calls=%async_computation.1 | async-start | bytes 1572864 | tf_op jit(solution)/shard_map/all_to_all | solution.py:88
  28.6 0.7 copy-start.5
  28.6 0.7 copy-start.6
  28.7 1.0 copy-start
  45.7 1.0 copy-start.1
  48.1 0.7 copy-start.8

commit v12 on v10

--- a/solution.py
+++ b/solution.py
@@ -82,7 +82,6 @@
     filt = lax.all_to_all(filt, "seq", 0, 0, tiled=True).reshape(seq_count * blocks, chans, cols)
     streams = jnp.stack([query_projected, key_stream, value_stream])
     streams = streams.reshape(3, blocks, cols, seq_count, chans).transpose(3, 0, 1, 4, 2)
-    filt, streams = lax.optimization_barrier((filt, streams))
     spec_f = spectrum(filt, tables)
     full = lax.all_to_all(streams, "seq", 0, 0, tiled=True)
     spec_f, full = lax.optimization_barrier((spec_f, full))

time: 124 us -> 122 us (0.984)
  waiting for transfers between devices: 17.5 us -> 15.9 us
    optimization_barrier x1 -> x0, local copies, waits for them, and re-layouts: 1.64 us -> none  [on_device(): filt, streams = lax.optimization_barrier((filt, streams))]
    all_to_all x1, waiting for transfers between devices: 8 us -> 6.43 us  [on_device(): lax.all_to_all(filt, 'seq', 0, 0, tiled=True)]
    transpose x0 -> x1, local copies, waits for them, and re-layouts: none -> 1.56 us  [on_device(): streams.reshape(3, blocks, cols, seq_count, chans).transpose(3, 0, 1, 4, 2)]
  transfers between devices with their start and end apart: 2 -> 2, of which waited for: 2 -> 2; matrix products, arithmetic and copies ran while one was open for 5% -> 7% of each run, Pallas kernels for 0% -> 0%
where the time goes in v12:
time: 122 us
  blocking collectives  69.4 us (57%)
  waiting for transfers between devices  15.9 us (13%)
  starting transfers between devices  12.1 us (10%)
  local copies, waits for them, and re-layouts  10.4 us (9%)
  matrix products  9.68 us (8%)
  other arithmetic  3.68 us (3%)
    psum x1, blocking collectives, on_device(): return lax.psum(terms, 'chan').astype(jnp.bfloat16)  57.5 us
    all_to_all x1, blocking collectives, on_device(): lax.all_to_all(gated.reshape(seq_count, blocks, chans, cols), 'seq', 0, 0...  11.9 us
    all_to_all x1, waiting for transfers between devices, on_device(): full = lax.all_to_all(streams, 'seq', 0, 0, tiled=True)  9.42 us
    all_to_all x1, starting transfers between devices, on_device(): lax.all_to_all(filt, 'seq', 0, 0, tiled=True)  8.29 us
    all_to_all x1, waiting for transfers between devices, on_device(): lax.all_to_all(filt, 'seq', 0, 0, tiled=True)  6.43 us
    unnamed x31, local copies, waits for them, and re-layouts  4.52 us
    all_to_all x1, starting transfers between devices, on_device(): full = lax.all_to_all(streams, 'seq', 0, 0, tiled=True)  3.8 us
    dot_general x1, matrix products, on_device(): terms = jnp.dot(gated, out_weight, preferred_element_type=jnp.float32)  3.27 us
  transfers between devices with their start and end apart: 2, of which 2 were waited for; matrix products, arithmetic and copies ran while one was open for 7% of the time, Pallas kernels for 0%

profile of v12, /device:TPU:0, one launch (start us, length us, event | category | flops | bytes accessed | tf_op | source)
XLA Modules:
  0.0 121.6 jit_solution(10394605204764126634)
XLA Ops:
  0.0 1.3 %copy.33 = f32[256,512]{0,1:T(8,128)S(1)} copy(f32[256,512]{1,0:T(8,128)} %param.18) | data formatting | bytes 1048576 | tf_op args[5]
  1.3 1.1 reshape.90
  2.4 8.3 %all-to-all-start = ((f32[16,2,32,128]{3,1,2,0:T(2,128)}), f32[16,2,32,128]{3,1,2,0:T(2,128)S(1)}, u32[]{:S(2)}, u32[]{:S(2)}) async-start(f32[16,2,32,128]{3,1,2,0:T(2,128)} %bitcast.1), calls=%async_computation | async-start | bytes 1048576 | tf_op jit(solution)/shard_map/all_to_all | solution.py:82
  11.3 1.3 %maximum_bitcast_fusion = bf16[16,3,2,32,128]{4,2,3,0,1:T(2,128)(2,1)S(1)} fusion(bf16[1,2,128,16,32]{2,1,4,3,0:T(2,128)(2,1)S(1)} %stack.14, bf16[1,2,128,16,32]{2,1,4,3,0:T(2,128)(2,1)S(1)} %stack.13, bf16[1,2,128,16,32]{2,1,4,3,0:T(2,128)(2,1)S(1)} %stack.12), kind=kLoop, calls=%fused_computation.20 | loop fusion | flops 786432 | bytes 1572864 | tf_op jit(solution)/shard_map/transpose | solution.py:84
  12.7 1.6 %copy.38 = bf16[16,3,2,32,128]{4,2,3,1,0:T(2,128)(2,1)} copy(bf16[16,3,2,32,128]{4,2,3,0,1:T(2,128)(2,1)S(1)} %maximum_bitcast_fusion) | data formatting | bytes 1572864 | tf_op jit(solution)/shard_map/transpose | solution.py:84
  14.2 0.8 dynamic_slice.7
  15.0 0.8 dynamic-slice_bitcast_fusion.2
  15.8 6.4 %all-to-all-done = f32[16,2,32,128]{3,1,2,0:T(2,128)S(1)} async-done(((f32[16,2,32,128]{3,1,2,0:T(2,128)}), f32[16,2,32,128]{3,1,2,0:T(2,128)S(1)}, u32[]{:S(2)}, u32[]{:S(2)}) %all-to-all-start) | async-done | bytes 524320 | tf_op jit(solution)/shard_map/all_to_all | solution.py:82
  22.2 3.8 %all-to-all-start.1 = ((bf16[16,3,2,32,128]{4,2,3,1,0:T(2,128)(2,1)}), bf16[16,3,2,32,128]{4,2,3,1,0:T(2,128)(2,1)S(1)}, u32[]{:S(2)}, u32[]{:S(2)}) async-start(bf16[16,3,2,32,128]{4,2,3,1,0:T(2,128)(2,1)} %copy.38), calls=%async_computation.1 | async-start | bytes 1572864 | tf_op jit(solution)/shard_map/all_to_all | solution.py:86
  26.1 1.3 %fusion.17 = f32[66,4096]{1,0:T(8,128)S(1)} fusion(f32[66,32]{1,0:T(8,128)S(1)} %copy-done.8, f32[4,8,32,128]{3,2,1,0:T(8,128)S(1)} %bitcast.88), kind=kOutput, calls=%fused_computation.33 | convolution fusion | flops 103809024 | bytes 1614080 | tf_op jit(solution)/shard_map/dot_general | solution.py:39
  27.8 0.4 copy-done.6
  28.3 0.2 multiply_add_fusion.3
  28.4 0.2 copy-done.1
  28.6 1.0 fusion.2
  29.6 9.4 %all-to-all-done.1 = bf16[16,3,2,32,128]{4,2,3,1,0:T(2,128)(2,1)S(1)} async-done(((bf16[16,3,2,32,128]{4,2,3,1,0:T(2,128)(2,1)}), bf16[16,3,2,32,128]{4,2,3,1,0:T(2,128)(2,1)S(1)}, u32[]{:S(2)}, u32[]{:S(2)}) %all-to-all-start.1) | async-done | bytes 786464 | tf_op jit(solution)/shard_map/all_to_all | solution.py:86
  39.1 0.2 copy_convert_fusion
  39.4 0.5 pad_slice_fusion
  39.9 0.5 pad_slice_fusion.1
  40.3 1.1 fusion.1
  41.6 1.3 %fusion.14 = f32[66,4096]{1,0:T(8,128)S(1)} fusion(f32[66,32]{1,0:T(8,128)S(1)} %copy-done.8, f32[4,8,32,128]{3,2,1,0:T(8,128)S(1)} %bitcast.77), kind=kOutput, calls=%fused_computation.30 | convolution fusion | flops 103809024 | bytes 1614080 | tf_op jit(solution)/shard_map/dot_general | solution.py:39
  43.3 0.2 multiply_add_fusion.2
  43.4 1.0 fusion.6
  44.7 0.8 copy-done.2
  45.4 1.0 fusion.10
  46.5 0.2 multiply_subtract_fusion
  46.8 0.7 copy.47
  47.6 0.7 convolution_bitcast_fusion
  48.4 0.2 multiply_convert_fusion
  48.6 11.9 %all_to_all.15 = bf16[16,2,32,128]{3,2,1,0:T(8,128)(2,1)S(1)} all-to-all(bf16[16,2,32,128]{3,2,1,0:T(8,128)(2,1)S(1)} %multiply_convert_fusion), channel_id=1, replica_groups=mesh['seq'=16,'chan'=8] {'seq'}, dimensions={0} | all-to-all | bytes 524288 | tf_op jit(solution)/shard_map/all_to_all | solution.py:100
  60.5 0.2 copy.40
  60.8 3.3 %fusion.20 = f32[256,4096]{1,0:T(8,128)} fusion(bf16[512,4096]{1,0:T(8,128)(2,1)S(1)} %copy-done, bf16[64,8,2,128]{3,2,1,0:T(2,128)(2,1)S(1)} %bitcast.90), kind=kOutput, calls=%fused_computation.38 | convolution fusion | flops 1073741824 | bytes 8650752 | tf_op jit(solution)/shard_map/dot_general | solution.py:102
  64.0 57.5 %all-reduce.2 = bf16[256,4096]{1,0:T(8,128)(2,1)} all-reduce(f32[256,4096]{1,0:T(8,128)} %fusion.20), channel_id=1, replica_groups=mesh['seq'=16,'chan'=8] {'chan'}, use_global_device_ids=true, to_apply=%region_0.0 | all-reduce | flops 1048576 | bytes 6291456 | tf_op jit(solution)/shard_map/psum | solution.py:103
  (36 shorter events, 2.1 us)
Async XLA Ops:
  0.0 10.7 %copy-start.3 = (bf16[256,512]{1,0:T(8,128)(2,1)S(1)}, bf16[256,512]{1,0:T(8,128)(2,1)}, u32[]{:S(2)}) copy-start(bf16[256,512]{1,0:T(8,128)(2,1)} %param.13) | copy-start | bytes 786436
  1.3 9.6 %copy-start.4 = (bf16[256,512]{1,0:T(8,128)(2,1)S(1)}, bf16[256,512]{1,0:T(8,128)(2,1)}, u32[]{:S(2)}) copy-start(bf16[256,512]{1,0:T(8,128)(2,1)} %param.14) | copy-start | bytes 786436
  2.4 8.8 %copy-start.5 = (bf16[256,512]{1,0:T(8,128)(2,1)S(1)}, bf16[256,512]{1,0:T(8,128)(2,1)}, u32[]{:S(2)}) copy-start(bf16[256,512]{1,0:T(8,128)(2,1)} %param.15) | copy-start | bytes 786436
  2.4 19.8 %all-to-all-start = ((f32[16,2,32,128]{3,1,2,0:T(2,128)}), f32[16,2,32,128]{3,1,2,0:T(2,128)S(1)}, u32[]{:S(2)}, u32[]{:S(2)}) async-start(f32[16,2,32,128]{3,1,2,0:T(2,128)} %bitcast.1), calls=%async_computation | async-start | bytes 1048576 | tf_op jit(solution)/shard_map/all_to_all | solution.py:82
  14.2 11.8 %copy-start.8 = (f32[66,32]{1,0:T(8,128)S(1)}, f32[66,32]{1,0:T(8,128)}, u32[]{:S(2)}) copy-start(f32[66,32]{1,0:T(8,128)} %constant.26.clone) | copy-start | bytes 25348
  22.2 16.9 %all-to-all-start.1 = ((bf16[16,3,2,32,128]{4,2,3,1,0:T(2,128)(2,1)}), bf16[16,3,2,32,128]{4,2,3,1,0:T(2,128)(2,1)S(1)}, u32[]{:S(2)}, u32[]{:S(2)}) async-start(bf16[16,3,2,32,128]{4,2,3,1,0:T(2,128)(2,1)} %copy.38), calls=%async_computation.1 | async-start | bytes 1572864 | tf_op jit(solution)/shard_map/all_to_all | solution.py:86
  27.5 0.7 copy-start.6
  27.5 0.7 copy-start.7
  27.7 1.0 copy-start.1
  44.5 1.0 copy-start.2
  46.8 0.7 copy-start.9
  47.5 13.2 %copy-start = (bf16[512,4096]{1,0:T(8,128)(2,1)S(1)}, bf16[512,4096]{1,0:T(8,128)(2,1)}, u32[]{:S(2)}) copy-start(bf16[512,4096]{1,0:T(8,128)(2,1)} %param.19) | copy-start | bytes 12582916

commit v13 on v12

--- a/solution.py
+++ b/solution.py
@@ -78,8 +78,8 @@
     tables = dft_tables(seq_count * shard_len)
     cols = tables[1]
     blocks = shard_len // cols
-    filt = long_filter.reshape(blocks, cols, seq_count, chans).transpose(2, 0, 3, 1)
-    filt = lax.all_to_all(filt, "seq", 0, 0, tiled=True).reshape(seq_count * blocks, chans, cols)
+    filt = lax.all_to_all(long_filter, "seq", 1, 0, tiled=True)
+    filt = filt.reshape(seq_count * blocks, cols, chans).transpose(0, 2, 1)
     streams = jnp.stack([query_projected, key_stream, value_stream])
     streams = streams.reshape(3, blocks, cols, seq_count, chans).transpose(3, 0, 1, 4, 2)
     spec_f = spectrum(filt, tables)

time: 122 us -> 122 us (level)
  no operation moved by 1% of the time
where the time goes in v13:
time: 122 us; the launch traced here: 121 us
  blocking collectives  69.4 us (57%)
  waiting for transfers between devices  15.8 us (13%)
  starting transfers between devices  12.1 us (10%)
  local copies, waits for them, and re-layouts  10.5 us (9%)
  matrix products  9.43 us (8%)
  other arithmetic  3.68 us (3%)
    psum x1, blocking collectives, on_device(): return lax.psum(terms, 'chan').astype(jnp.bfloat16)  57.5 us
    all_to_all x1, blocking collectives, on_device(): lax.all_to_all(gated.reshape(seq_count, blocks, chans, cols), 'seq', 0, 0...  11.9 us
    all_to_all x1, waiting for transfers between devices, on_device(): full = lax.all_to_all(streams, 'seq', 0, 0, tiled=True)  9.38 us
    all_to_all x1, starting transfers between devices, on_device(): filt = lax.all_to_all(long_filter, 'seq', 1, 0, tiled=True)  8.29 us
    all_to_all x1, waiting for transfers between devices, on_device(): filt = lax.all_to_all(long_filter, 'seq', 1, 0, tiled=True)  6.44 us
    unnamed x31, local copies, waits for them, and re-layouts  5.33 us
    all_to_all x1, starting transfers between devices, on_device(): full = lax.all_to_all(streams, 'seq', 0, 0, tiled=True)  3.8 us
    dot_general x1, matrix products, on_device(): terms = jnp.dot(gated, out_weight, preferred_element_type=jnp.float32)  3.28 us
  transfers between devices with their start and end apart: 2, of which 2 were waited for; matrix products, arithmetic and copies ran while one was open for 7% of the time, Pallas kernels for 0%

profile of v13, /device:TPU:0, one launch (start us, length us, event | category | flops | bytes accessed | tf_op | source)
XLA Modules:
  0.0 121.3 jit_solution(4404560292806051489)
XLA Ops:
  0.0 2.1 %copy.35 = f32[256,512]{0,1:T(8,128)} copy(f32[256,512]{1,0:T(8,128)} %param.18) | data formatting | bytes 1048576 | tf_op args[5]
  2.1 8.3 %all-to-all-start = ((f32[256,16,32]{0,2,1:T(8,128)}), f32[256,16,32]{0,2,1:T(8,128)S(1)}, u32[]{:S(2)}, u32[]{:S(2)}) async-start(f32[256,16,32]{0,2,1:T(8,128)} %bitcast.1), calls=%async_computation | async-start | bytes 1048576 | tf_op jit(solution)/shard_map/all_to_all | solution.py:81
  11.1 1.3 %maximum_bitcast_fusion = bf16[16,3,2,32,128]{4,2,3,0,1:T(2,128)(2,1)S(1)} fusion(bf16[1,2,128,16,32]{2,1,4,3,0:T(2,128)(2,1)S(1)} %stack.14, bf16[1,2,128,16,32]{2,1,4,3,0:T(2,128)(2,1)S(1)} %stack.13, bf16[1,2,128,16,32]{2,1,4,3,0:T(2,128)(2,1)S(1)} %stack.12), kind=kLoop, calls=%fused_computation.20 | loop fusion | flops 786432 | bytes 1572864 | tf_op jit(solution)/shard_map/transpose | solution.py:84
  12.4 1.6 %copy.41 = bf16[16,3,2,32,128]{4,2,3,1,0:T(2,128)(2,1)} copy(bf16[16,3,2,32,128]{4,2,3,0,1:T(2,128)(2,1)S(1)} %maximum_bitcast_fusion) | data formatting | bytes 1572864 | tf_op jit(solution)/shard_map/transpose | solution.py:84
  14.0 0.8 dynamic_slice.7
  14.7 0.8 dynamic-slice_bitcast_fusion.2
  15.5 6.4 %all-to-all-done = f32[256,16,32]{0,2,1:T(8,128)S(1)} async-done(((f32[256,16,32]{0,2,1:T(8,128)}), f32[256,16,32]{0,2,1:T(8,128)S(1)}, u32[]{:S(2)}, u32[]{:S(2)}) %all-to-all-start) | async-done | bytes 524320 | tf_op jit(solution)/shard_map/all_to_all | solution.py:81
  21.9 3.8 %all-to-all-start.1 = ((bf16[16,3,2,32,128]{4,2,3,1,0:T(2,128)(2,1)}), bf16[16,3,2,32,128]{4,2,3,1,0:T(2,128)(2,1)S(1)}, u32[]{:S(2)}, u32[]{:S(2)}) async-start(bf16[16,3,2,32,128]{4,2,3,1,0:T(2,128)(2,1)} %copy.41), calls=%async_computation.1 | async-start | bytes 1572864 | tf_op jit(solution)/shard_map/all_to_all | solution.py:86
  25.7 0.3 copy.36
  26.1 1.1 fusion.17
  27.6 0.4 copy-done.6
  28.0 0.2 multiply_add_fusion.3
  28.2 0.2 copy-done.1
  28.4 1.0 fusion.2
  29.4 9.4 %all-to-all-done.1 = bf16[16,3,2,32,128]{4,2,3,1,0:T(2,128)(2,1)S(1)} async-done(((bf16[16,3,2,32,128]{4,2,3,1,0:T(2,128)(2,1)}), bf16[16,3,2,32,128]{4,2,3,1,0:T(2,128)(2,1)S(1)}, u32[]{:S(2)}, u32[]{:S(2)}) %all-to-all-start.1) | async-done | bytes 786464 | tf_op jit(solution)/shard_map/all_to_all | solution.py:86
  38.8 0.2 copy_convert_fusion
  39.2 0.5 pad_slice_fusion
  39.6 0.5 pad_slice_fusion.1
  40.1 1.1 fusion.1
  41.3 1.3 %fusion.14 = f32[66,4096]{1,0:T(8,128)S(1)} fusion(f32[66,32]{1,0:T(8,128)S(1)} %copy-done.8, f32[4,8,32,128]{3,2,1,0:T(8,128)S(1)} %bitcast.81), kind=kOutput, calls=%fused_computation.30 | convolution fusion | flops 103809024 | bytes 1614080 | tf_op jit(solution)/shard_map/dot_general | solution.py:39
  43.0 0.2 multiply_add_fusion.2
  43.2 1.0 fusion.6
  44.4 0.8 copy-done.2
  45.2 1.0 fusion.10
  46.2 0.2 multiply_subtract_fusion
  46.6 0.7 copy.50
  47.3 0.7 convolution_bitcast_fusion
  48.1 0.2 multiply_convert_fusion
  48.3 11.9 %all_to_all.26 = bf16[16,2,32,128]{3,2,1,0:T(8,128)(2,1)S(1)} all-to-all(bf16[16,2,32,128]{3,2,1,0:T(8,128)(2,1)S(1)} %multiply_convert_fusion), channel_id=1, replica_groups=mesh['seq'=16,'chan'=8] {'seq'}, dimensions={0} | all-to-all | bytes 524288 | tf_op jit(solution)/shard_map/all_to_all | solution.py:100
  60.2 0.2 copy.43
  60.5 3.3 %fusion.20 = f32[256,4096]{1,0:T(8,128)} fusion(bf16[512,4096]{1,0:T(8,128)(2,1)S(1)} %copy-done, bf16[64,8,2,128]{3,2,1,0:T(2,128)(2,1)S(1)} %bitcast.94), kind=kOutput, calls=%fused_computation.38 | convolution fusion | flops 1073741824 | bytes 8650752 | tf_op jit(solution)/shard_map/dot_general | solution.py:102
  63.8 57.5 %all-reduce.2 = bf16[256,4096]{1,0:T(8,128)(2,1)} all-reduce(f32[256,4096]{1,0:T(8,128)} %fusion.20), channel_id=1, replica_groups=mesh['seq'=16,'chan'=8] {'chan'}, use_global_device_ids=true, to_apply=%region_0.0 | all-reduce | flops 1048576 | bytes 6291456 | tf_op jit(solution)/shard_map/psum | solution.py:103
  (36 shorter events, 2.1 us)
Async XLA Ops:
  0.0 10.4 %copy-start.3 = (bf16[256,512]{1,0:T(8,128)(2,1)S(1)}, bf16[256,512]{1,0:T(8,128)(2,1)}, u32[]{:S(2)}) copy-start(bf16[256,512]{1,0:T(8,128)(2,1)} %param.13) | copy-start | bytes 786436
  0.0 10.6 %copy-start.4 = (bf16[256,512]{1,0:T(8,128)(2,1)S(1)}, bf16[256,512]{1,0:T(8,128)(2,1)}, u32[]{:S(2)}) copy-start(bf16[256,512]{1,0:T(8,128)(2,1)} %param.14) | copy-start | bytes 786436
  2.1 8.8 %copy-start.5 = (bf16[256,512]{1,0:T(8,128)(2,1)S(1)}, bf16[256,512]{1,0:T(8,128)(2,1)}, u32[]{:S(2)}) copy-start(bf16[256,512]{1,0:T(8,128)(2,1)} %param.15) | copy-start | bytes 786436
  2.1 19.8 %all-to-all-start = ((f32[256,16,32]{0,2,1:T(8,128)}), f32[256,16,32]{0,2,1:T(8,128)S(1)}, u32[]{:S(2)}, u32[]{:S(2)}) async-start(f32[256,16,32]{0,2,1:T(8,128)} %bitcast.1), calls=%async_computation | async-start | bytes 1048576 | tf_op jit(solution)/shard_map/all_to_all | solution.py:81
  15.5 10.6 %copy-start.8 = (f32[66,32]{1,0:T(8,128)S(1)}, f32[66,32]{1,0:T(8,128)}, u32[]{:S(2)}) copy-start(f32[66,32]{1,0:T(8,128)} %constant.26.clone) | copy-start | bytes 25348
  21.9 16.9 %all-to-all-start.1 = ((bf16[16,3,2,32,128]{4,2,3,1,0:T(2,128)(2,1)}), bf16[16,3,2,32,128]{4,2,3,1,0:T(2,128)(2,1)S(1)}, u32[]{:S(2)}, u32[]{:S(2)}) async-start(bf16[16,3,2,32,128]{4,2,3,1,0:T(2,128)(2,1)} %copy.41), calls=%async_computation.1 | async-start | bytes 1572864 | tf_op jit(solution)/shard_map/all_to_all | solution.py:86
  27.3 0.7 copy-start.6
  27.3 0.7 copy-start.7
  27.4 1.0 copy-start.1
  44.2 1.0 copy-start.2
  46.6 0.7 copy-start.9
  47.3 13.2 %copy-start = (bf16[512,4096]{1,0:T(8,128)(2,1)S(1)}, bf16[512,4096]{1,0:T(8,128)(2,1)}, u32[]{:S(2)}) copy-start(bf16[512,4096]{1,0:T(8,128)(2,1)} %param.19) | copy-start | bytes 12582916
